TPU v7x, 32 devices: a whole 2x2x4 slice. The times are simulated.
32 devices in a mesh: lat: 8 (over z, y), mode: 4 (over x, core).
Axes of the slice: x: 2, y: 2, z: 4, core: 2. Of those that a mesh axis runs over, the one named last changes fastest.
Arguments:
- earlier: bfloat16 [64, 32, 36864], P(None, ('lat', 'mode')), may hold values from -4 to 4
- panels: bfloat16 [2, 16, 32, 36864], P(None, 'mode', None, 'lat'), may hold values from -28 to 28
- further: bfloat16 [16, 32, 36864], P('mode', None, 'lat'), may hold values from -32 to 32
Outputs:
- new_basis: bfloat16 [2, 16, 32, 36864], P(None, None, ('lat', 'mode'))
- coarse: float32 [16, 32, 96], P(None, ('lat', 'mode'))
All inputs are finite; a program needn't handle non-finite values.
Results may differ from a plain program's by a relative error of at most 0.0062.
Values may be sent and summed in bfloat16 or wider, within the bound.
No kernel may reach another device: no remote copies, remote signals or barrier semaphores. Data moves between devices by JAX's collectives and lax.ppermute only.
A program may use at most 64 MiB of HBM per device.

v0:
```python
import jax
import jax.numpy as jnp
from jax import lax
from jax.sharding import PartitionSpec as P


def factor_inverse(gram_matrix):
    lower_factor = jnp.linalg.cholesky(gram_matrix)
    identity = jnp.broadcast_to(
        jnp.eye(gram_matrix.shape[-1], dtype=gram_matrix.dtype), gram_matrix.shape
    )
    return lax.linalg.triangular_solve(lower_factor, identity, left_side=True, lower=True)


def regroup(arriving):
    lat_count = lax.axis_size("lat")
    mode_count = lax.axis_size("mode")
    received = lax.all_to_all(
        arriving[None], ("lat", "mode"), split_axis=2, concat_axis=0, tiled=True
    )
    vector_part = received.shape[1]
    block_count = received.shape[2]
    entry_part = received.shape[3]
    received = received.reshape(lat_count, mode_count, vector_part, block_count, entry_part)
    received = received.transpose(1, 2, 3, 0, 4)
    return received.reshape(mode_count * vector_part, block_count, lat_count * entry_part)


def per_device(earlier, panels, further):
    block_len = earlier.shape[2]
    finished = []
    for panel_index in range(panels.shape[0]):
        vectors = regroup(panels[panel_index])
        pieces = [earlier] + finished
        removed = None
        for basis_part in pieces:
            coeffs = (
                jnp.einsum("nbl,pbl->bnp", basis_part, vectors, preferred_element_type=jnp.float32)
                / block_len
            )
            coeffs = coeffs.astype(jnp.bfloat16)
            term = jnp.einsum(
                "bnp,nbl->pbl", coeffs, basis_part, preferred_element_type=jnp.float32
            )
            removed = term if removed is None else removed + term
        residual = (vectors.astype(jnp.float32) - removed).astype(jnp.bfloat16)
        gram_matrix = (
            jnp.einsum("pbl,qbl->bpq", residual, residual, preferred_element_type=jnp.float32)
            / block_len
        )
        inverse = factor_inverse(gram_matrix)
        residual_wide = lax.optimization_barrier(residual).astype(jnp.float32)
        fresh = jnp.einsum("bpq,qbl->pbl", inverse, residual_wide, precision=lax.Precision.HIGHEST)
        finished.append(fresh.astype(jnp.bfloat16))
    further_blocks = regroup(further)
    products = []
    for basis_part in [earlier] + finished:
        products.append(
            jnp.einsum(
                "nbl,pbl->pbn", basis_part, further_blocks, preferred_element_type=jnp.float32
            )
            / block_len
        )
    coarse = jnp.concatenate(products, axis=2)
    return (jnp.stack(finished, 0), coarse)


def solution(mesh):
    return jax.shard_map(
        per_device,
        mesh=mesh,
        in_specs=(
            P(None, ("lat", "mode"), None),
            P(None, "mode", None, "lat"),
            P("mode", None, "lat"),
        ),
        out_specs=(P(None, None, ("lat", "mode"), None), P(None, ("lat", "mode"), None)),
        check_vma=False,
    )
```

profile of v0, /device:TPU:0, one launch (start us, length us, event | category | flops | bytes accessed | tf_op | source)
XLA Modules:
  0.0 129.2 jit_solution(6858289764617748411)
XLA Ops:
  0.6 1.8 %fusion.92 = (bf16[1,4,32,4608]{3,2,1,0:T(8,128)(2,1)S(1)}, bf16[1,4,32,4608]{3,2,1,0:T(8,128)(2,1)S(1)}) fusion(bf16[2,4,32,4608]{3,2,1,0:T(8,128)(2,1)} %param.7), kind=kLoop, calls=%fused_computation.78 | loop fusion | bytes 4718592 | tf_op jit(solution)/shard_map/slice | solution.py:33
  2.5 1.9 %copy.35 = bf16[1,4,32,4608]{3,1,0,2:T(4,128)(2,1)} copy(bf16[1,4,32,4608]{3,2,1,0:T(8,128)(2,1)S(1)} %get-tuple-element.10) | data formatting | bytes 2359296
  4.4 7.3 %all-to-all-start = ((bf16[1,4,32,4608]{3,1,0,2:T(4,128)(2,1)}), bf16[1,4,32,4608]{3,1,0,2:T(4,128)(2,1)S(1)}, u32[]{:S(2)}, u32[]{:S(2)}) async-start(bf16[1,4,32,4608]{3,1,0,2:T(4,128)(2,1)} %copy.35), calls=%async_computation | async-start | bytes 2359296 | tf_op jit(solution)/shard_map/all_to_all | solution.py:18
  11.7 2.0 %copy.36 = bf16[1,4,32,4608]{3,1,0,2:T(4,128)(2,1)} copy(bf16[1,4,32,4608]{3,2,1,0:T(8,128)(2,1)S(1)} %get-tuple-element.11) | data formatting | bytes 2359296
  13.7 1.9 %copy.45 = bf16[4,32,4608]{2,0,1:T(4,128)(2,1)} copy(bf16[4,32,4608]{2,1,0:T(8,128)(2,1)S(1)} %copy-done) | data formatting | bytes 2359296 | tf_op args[2]
  15.6 25.2 %all-to-all-done = bf16[1,4,32,4608]{3,1,0,2:T(4,128)(2,1)S(1)} async-done(((bf16[1,4,32,4608]{3,1,0,2:T(4,128)(2,1)}), bf16[1,4,32,4608]{3,1,0,2:T(4,128)(2,1)S(1)}, u32[]{:S(2)}, u32[]{:S(2)}) %all-to-all-start) | async-done | bytes 1179680 | tf_op jit(solution)/shard_map/all_to_all | solution.py:18
  40.8 3.8 %all-to-all-start.1 = ((bf16[1,4,32,4608]{3,1,0,2:T(4,128)(2,1)}), bf16[1,4,32,4608]{3,1,0,2:T(4,128)(2,1)}, u32[]{:S(2)}, u32[]{:S(2)}) async-start(bf16[1,4,32,4608]{3,1,0,2:T(4,128)(2,1)} %copy.36), calls=%async_computation.1 | async-start | bytes 2359296 | tf_op jit(solution)/shard_map/all_to_all | solution.py:18
  44.5 2.1 %fusion.93 = (bf16[8,4,4,1,4608]{4,0,2,1,3:T(8,128)(2,1)S(1)}, f32[4,4,1,8,4608]{4,3,1,0,2:T(8,128)}) fusion(bf16[8,4,4,1,4608]{4,2,1,0,3:T(4,128)(2,1)S(1)} %bitcast.200), kind=kLoop, calls=%fused_computation.79 | loop fusion | flops 589824 | bytes 4718592 | tf_op jit(solution)/shard_map/reshape | solution.py:24
  46.7 1.9 %reshape.235 = f32[16,1,36864]{2,0,1:T(8,128)S(1)} reshape(f32[4,4,1,8,4608]{4,3,1,0,2:T(8,128)} %get-tuple-element.13) | data formatting | bytes 4718592 | tf_op jit(solution)/shard_map/convert_element_type | solution.py:46
  48.5 1.4 %copy.37 = bf16[2,8,8,4608]{3,1,2,0:T(8,128)(2,1)} copy(bf16[2,8,8,4608]{3,2,1,0:T(8,128)(2,1)S(1)} %bitcast.202) | data formatting | bytes 2359296
  49.9 7.4 %fusion.4 = bf16[16,1,36864]{2,0,1:T(8,128)(2,1)S(1)} fusion(f32[16,1,36864]{2,0,1:T(8,128)S(1)} %reshape.235, bf16[64,1,36864]{2,0,1:T(8,128)(2,1)} %param.6, bf16[16,36864]{1,0:T(8,128)(2,1)} %bitcast.198), kind=kOutput, calls=%fused_computation.7 | convolution fusion | flops 152176640 | bytes 9437184 | tf_op jit(solution)/shard_map/bnp,nbl->pbl/dot_general | solution.py:42
  57.9 1.5 %custom-call.8 = f32[1,16,16]{2,1,0:T(8,128)S(1)} custom-call(f32[1,16,16]{2,1,0:T(8,128)S(1)} %fusion.77), custom_call_target="Cholesky" | custom-call | tf_op jit(solution)/shard_map/jit(cholesky)/cholesky | solution.py:8
  59.4 14.2 %all-to-all-done.1 = bf16[1,4,32,4608]{3,1,0,2:T(4,128)(2,1)} async-done(((bf16[1,4,32,4608]{3,1,0,2:T(4,128)(2,1)}), bf16[1,4,32,4608]{3,1,0,2:T(4,128)(2,1)}, u32[]{:S(2)}, u32[]{:S(2)}) %all-to-all-start.1) | async-done | bytes 1179680 | tf_op jit(solution)/shard_map/all_to_all | solution.py:18
  73.6 3.9 %all-to-all-start.2 = ((bf16[1,4,32,4608]{3,1,0,2:T(4,128)(2,1)}), bf16[1,4,32,4608]{3,1,0,2:T(4,128)(2,1)}, u32[]{:S(2)}, u32[]{:S(2)}) async-start(bf16[1,4,32,4608]{3,1,0,2:T(4,128)(2,1)} %bitcast.190), calls=%async_computation.2 | async-start | bytes 2359296 | tf_op jit(solution)/shard_map/all_to_all | solution.py:18
  77.6 3.4 %fusion.94 = (bf16[8,4,4,1,4608]{4,0,2,1,3:T(8,128)(2,1)S(1)}, f32[4,4,1,8,4608]{4,3,1,0,2:T(8,128)}) fusion(bf16[8,4,4,1,4608]{4,2,1,0,3:T(4,128)(2,1)} %bitcast.21), kind=kLoop, calls=%fused_computation.80 | loop fusion | flops 589824 | bytes 4718592 | tf_op jit(solution)/shard_map/reshape | solution.py:24
  82.3 1.2 custom-call.9
  83.9 2.9 %reshape.236 = f32[16,1,36864]{2,0,1:T(8,128)} reshape(f32[4,4,1,8,4608]{4,3,1,0,2:T(8,128)} %get-tuple-element.15) | data formatting | bytes 4718592 | tf_op jit(solution)/shard_map/convert_element_type | solution.py:46
  87.0 1.1 convolution_convert_fusion.1
  88.1 8.5 %convolution_bitcast_fusion = f32[36864,16]{0,1:T(8,128)} fusion(bf16[64,1,36864]{2,0,1:T(8,128)(2,1)} %param.6, bf16[16,36864]{1,0:T(8,128)(2,1)S(1)} %bitcast.195), kind=kOutput, calls=%fused_computation.2 | convolution fusion | flops 150996992 | bytes 8257536 | tf_op jit(solution)/shard_map/bnp,nbl->pbl/dot_general | solution.py:42
  96.5 4.1 %fusion.3 = bf16[16,1,36864]{2,0,1:T(8,128)(2,1)S(1)} fusion(f32[16,1,36864]{2,0,1:T(8,128)} %reshape.236, f32[36864,16]{0,1:T(8,128)} %convolution_bitcast_fusion, bf16[36864,16]{0,1:T(8,128)(2,1)S(1)} %convolution_convert_fusion.1, bf16[16,36864]{1,0:T(8,128)(2,1)S(1)} %bitcast.196), kind=kOutput, calls=%fused_computation.6 | convolution fusion | flops 39518720 | bytes 8257536 | tf_op jit(solution)/shard_map/bnp,nbl->pbl/dot_general | solution.py:42
  100.6 1.2 fusion.29
  101.8 4.6 %all-to-all-done.2 = bf16[1,4,32,4608]{3,1,0,2:T(4,128)(2,1)} async-done(((bf16[1,4,32,4608]{3,1,0,2:T(4,128)(2,1)}), bf16[1,4,32,4608]{3,1,0,2:T(4,128)(2,1)}, u32[]{:S(2)}, u32[]{:S(2)}) %all-to-all-start.2) | async-done | bytes 1179680 | tf_op jit(solution)/shard_map/all_to_all | solution.py:18
  106.5 1.9 %copy.30 = bf16[8,4,4,1,4608]{4,0,2,1,3:T(8,128)(2,1)S(1)} copy(bf16[8,4,4,1,4608]{4,2,1,0,3:T(4,128)(2,1)} %bitcast.43) | data formatting | bytes 2359296 | tf_op jit(solution)/shard_map/reshape | solution.py:24
  109.3 3.7 %fusion.56 = f32[16,1,64]{2,0,1:T(8,128)S(1)} fusion(bf16[16,36864]{1,0:T(8,128)(2,1)S(1)} %bitcast.193, bf16[64,1,36864]{2,0,1:T(8,128)(2,1)} %param.6), kind=kOutput, calls=%fused_computation.45 | convolution fusion | flops 75498496 | bytes 5902336 | tf_op jit(solution)/shard_map/nbl,pbl->pbn/dot_general | solution.py:59
  113.0 1.4 %copy.28 = f32[1,16,16]{2,1,0:T(8,128)} copy(f32[1,16,16]{1,2,0:T(8,128)} %bitcast.203) | data formatting | bytes 2048 | tf_op jit(solution)/shard_map/div | solution.py:48
  114.4 1.3 %fusion.76 = f32[1,16,16]{2,1,0:T(8,128)} fusion(f32[1,16,16]{2,1,0:T(8,128)} %copy.28, f32[16,16]{0,1:T(8,128)} %fusion.29), kind=kLoop, calls=%fused_computation.55 | loop fusion | flops 512 | bytes 3072 | tf_op jit(solution)/shard_map/jit(cholesky)/div | solution.py:8
  115.7 2.8 %custom-call.10 = f32[1,16,16]{2,1,0:T(8,128)} custom-call(f32[1,16,16]{2,1,0:T(8,128)} %fusion.76), custom_call_target="Cholesky" | custom-call | tf_op jit(solution)/shard_map/jit(cholesky)/cholesky | solution.py:8
  119.8 1.9 %fusion.75 = f32[1,1,16,16]{3,2,1,0:T(8,128)} fusion(f32[1,16,16]{2,1,0:T(8,128)} %custom-call.10, pred[]{:T(512)} %compare_reduce_fusion), kind=kLoop, calls=%fused_computation.52 | loop fusion | flops 1024 | bytes 2049 | tf_op jit(solution)/shard_map/triangular_solve/reshape.62 | solution.py:12
  121.8 2.5 %custom-call.11 = f32[1,1,16,16]{2,3,1,0:T(8,128)} custom-call(f32[1,1,16,16]{3,2,1,0:T(8,128)} %fusion.75), custom_call_target="InvertDiagBlocksLowerTriangular" | custom-call | tf_op jit(solution)/shard_map/triangular_solve/custom-call.0 | solution.py:12
  124.3 0.9 fusion.78
  125.2 1.1 convolution_convert_fusion
  126.8 1.6 %pad_maximum_fusion = bf16[2,16,1,36864]{3,1,2,0:T(8,128)(2,1)} fusion(bf16[1,16,1,36864]{3,1,2,0:T(8,128)(2,1)S(1)} %bitcast.197, bf16[1,16,1,36864]{3,1,2,0:T(8,128)(2,1)S(1)} %bitcast.191), kind=kLoop, calls=%fused_computation.18 | loop fusion | flops 1179648 | bytes 4718592 | tf_op jit(solution)/shard_map/stack | solution.py:65
  (16 shorter events, 6.1 us)
Async XLA Ops:
  4.4 36.4 %all-to-all-start = ((bf16[1,4,32,4608]{3,1,0,2:T(4,128)(2,1)}), bf16[1,4,32,4608]{3,1,0,2:T(4,128)(2,1)S(1)}, u32[]{:S(2)}, u32[]{:S(2)}) async-start(bf16[1,4,32,4608]{3,1,0,2:T(4,128)(2,1)} %copy.35), calls=%async_computation | async-start | bytes 2359296 | tf_op jit(solution)/shard_map/all_to_all | solution.py:18
  11.7 2.0 %copy-start = (bf16[4,32,4608]{2,1,0:T(8,128)(2,1)S(1)}, bf16[4,32,4608]{2,1,0:T(8,128)(2,1)}, u32[]{:S(2)}) copy-start(bf16[4,32,4608]{2,1,0:T(8,128)(2,1)} %param.8) | copy-start | bytes 3538948
  40.8 32.8 %all-to-all-start.1 = ((bf16[1,4,32,4608]{3,1,0,2:T(4,128)(2,1)}), bf16[1,4,32,4608]{3,1,0,2:T(4,128)(2,1)}, u32[]{:S(2)}, u32[]{:S(2)}) async-start(bf16[1,4,32,4608]{3,1,0,2:T(4,128)(2,1)} %copy.36), calls=%async_computation.1 | async-start | bytes 2359296 | tf_op jit(solution)/shard_map/all_to_all | solution.py:18
  73.6 32.8 %all-to-all-start.2 = ((bf16[1,4,32,4608]{3,1,0,2:T(4,128)(2,1)}), bf16[1,4,32,4608]{3,1,0,2:T(4,128)(2,1)}, u32[]{:S(2)}, u32[]{:S(2)}) async-start(bf16[1,4,32,4608]{3,1,0,2:T(4,128)(2,1)} %bitcast.190), calls=%async_computation.2 | async-start | bytes 2359296 | tf_op jit(solution)/shard_map/all_to_all | solution.py:18
where the time goes:
time: 130 us; the launch traced here: 129 us
  waiting for transfers between devices  44 us (34%)
  matrix products  29.8 us (23%)
  other arithmetic  21.8 us (17%)
  local copies, waits for them, and re-layouts  17.8 us (14%)
  starting transfers between devices  15 us (12%)
    all_to_all x3, waiting for transfers between devices, regroup(): lax.all_to_all(arriving[None], ('lat', 'mode'), split_axis=2, concat_axis...  44 us
    dot_general x3, matrix products, per_device(): jnp.einsum('bnp,nbl->pbl', coeffs, basis_part, preferred_element_type=jnp...  19.9 us
    all_to_all x3, starting transfers between devices, regroup(): lax.all_to_all(arriving[None], ('lat', 'mode'), split_axis=2, concat_axis...  15 us
    unnamed x8, local copies, waits for them, and re-layouts  7.88 us
    another operation x4, other arithmetic, factor_inverse(): lax.linalg.triangular_solve(lower_factor, identity, left_side=True, lower...  6.36 us
    another operation x6, other arithmetic, factor_inverse(): lower_factor = jnp.linalg.cholesky(gram_matrix)  6.24 us
    reshape x2, other arithmetic, regroup(): received.reshape(lat_count, mode_count, vector_part, block_count, entry_p...  5.53 us
    dot_general x3, matrix products, per_device(): jnp.einsum('nbl,pbl->pbn', basis_part, further_blocks, preferred_element_...  4.84 us
  transfers between devices with their start and end apart: 3, of which 3 were waited for; matrix products, arithmetic and copies ran while one was open for 33% of the time, Pallas kernels for 0%

commit v1 on v0

v1 whole, which is shorter than its diff:
```python
import jax
import jax.numpy as jnp
from jax import lax
from jax.sharding import PartitionSpec as P


def factor_inverse(gram_matrix):
    lower_factor = jnp.linalg.cholesky(gram_matrix)
    identity = jnp.broadcast_to(
        jnp.eye(gram_matrix.shape[-1], dtype=gram_matrix.dtype), gram_matrix.shape
    )
    return lax.linalg.triangular_solve(lower_factor, identity, left_side=True, lower=True)


def send(arriving):
    return lax.all_to_all(
        arriving[None], ("lat", "mode"), split_axis=2, concat_axis=0, tiled=True
    )


def arrange(received):
    lat_count = lax.axis_size("lat")
    mode_count = lax.axis_size("mode")
    vector_part = received.shape[1]
    block_count = received.shape[2]
    entry_part = received.shape[3]
    received = received.reshape(lat_count, mode_count, vector_part, block_count, entry_part)
    received = received.transpose(1, 2, 3, 0, 4)
    return received.reshape(mode_count * vector_part, block_count, lat_count * entry_part)


def project(earlier, finished, vectors, block_len):
    pieces = [earlier] + finished
    removed = None
    for basis_part in pieces:
        coeffs = (
            jnp.einsum("nbl,pbl->bnp", basis_part, vectors, preferred_element_type=jnp.float32)
            / block_len
        )
        coeffs = coeffs.astype(jnp.bfloat16)
        term = jnp.einsum("bnp,nbl->pbl", coeffs, basis_part, preferred_element_type=jnp.float32)
        removed = term if removed is None else removed + term
    residual = (vectors.astype(jnp.float32) - removed).astype(jnp.bfloat16)
    gram_matrix = (
        jnp.einsum("pbl,qbl->bpq", residual, residual, preferred_element_type=jnp.float32)
        / block_len
    )
    inverse = factor_inverse(gram_matrix)
    residual_wide = lax.optimization_barrier(residual).astype(jnp.float32)
    fresh = jnp.einsum("bpq,qbl->pbl", inverse, residual_wide, precision=lax.Precision.HIGHEST)
    return fresh.astype(jnp.bfloat16)


def per_device(earlier, panels, further):
    block_len = earlier.shape[2]
    panel_count = panels.shape[0]
    arrived = [send(panels[0])]
    for panel_index in range(1, panel_count):
        outgoing, arrived[-1] = lax.optimization_barrier((panels[panel_index], arrived[-1]))
        arrived.append(send(outgoing))
    outgoing, arrived[-1] = lax.optimization_barrier((further, arrived[-1]))
    further_arrived = send(outgoing)
    finished = []
    for panel_index in range(panel_count):
        vectors = arrange(arrived[panel_index])
        finished.append(project(earlier, finished, vectors, block_len))
    finished, further_arrived = lax.optimization_barrier((finished, further_arrived))
    further_blocks = arrange(further_arrived)
    products = []
    for basis_part in [earlier] + finished:
        products.append(
            jnp.einsum(
                "nbl,pbl->pbn", basis_part, further_blocks, preferred_element_type=jnp.float32
            )
            / block_len
        )
    coarse = jnp.concatenate(products, axis=2)
    return (jnp.stack(finished, 0), coarse)


def solution(mesh):
    return jax.shard_map(
        per_device,
        mesh=mesh,
        in_specs=(
            P(None, ("lat", "mode"), None),
            P(None, "mode", None, "lat"),
            P("mode", None, "lat"),
        ),
        out_specs=(P(None, None, ("lat", "mode"), None), P(None, ("lat", "mode"), None)),
        check_vma=False,
    )
```

time: 130 us -> 126 us (0.969)
  other arithmetic: 21.8 us -> 15.6 us
  waiting for transfers between devices: 44 us -> 47.7 us
    all_to_all x3, waiting for transfers between devices: 44 us -> 47.7 us  [send(): lax.all_to_all(arriving[None], ('lat', 'mode'), split_axis=2, concat_axis...]
    another operation x4, other arithmetic: 6.36 us -> 3.75 us  [factor_inverse(): lax.linalg.triangular_solve(lower_factor, identity, left_side=True, lower...]
    another operation x6, other arithmetic: 6.24 us -> 4.31 us  [factor_inverse(): lower_factor = jnp.linalg.cholesky(gram_matrix)]
    optimization_barrier x0 -> x1, local copies, waits for them, and re-layouts: none -> 1.91 us  [per_device(): outgoing, arrived[-1] = lax.optimization_barrier((further, arrived[-1]))]
    div x2, other arithmetic: 1.32 us -> 0.01 us  [factor_inverse(): lower_factor = jnp.linalg.cholesky(gram_matrix)]
    unnamed x8 -> x9, local copies, waits for them, and re-layouts: 7.88 us -> 7.31 us
  transfers between devices with their start and end apart: 3 -> 3, of which waited for: 3 -> 3; matrix products, arithmetic and copies ran while one was open for 33% -> 31% of each run, Pallas kernels for 0% -> 0%
where the time goes in v1:
time: 126 us; the launch traced here: 125 us
  waiting for transfers between devices  47.7 us (38%)
  matrix products  28.6 us (23%)
  local copies, waits for them, and re-layouts  17.4 us (14%)
  other arithmetic  15.6 us (12%)
  starting transfers between devices  15 us (12%)
    all_to_all x3, waiting for transfers between devices, send(): lax.all_to_all(arriving[None], ('lat', 'mode'), split_axis=2, concat_axis...  47.7 us
    dot_general x3, matrix products, project(): jnp.einsum('bnp,nbl->pbl', coeffs, basis_part, preferred_element_type=jnp...  20 us
    all_to_all x3, starting transfers between devices, send(): lax.all_to_all(arriving[None], ('lat', 'mode'), split_axis=2, concat_axis...  15 us
    unnamed x9, local copies, waits for them, and re-layouts  7.31 us
    reshape x2, other arithmetic, arrange(): received.reshape(lat_count, mode_count, vector_part, block_count, entry_p...  5.17 us
    dot_general x3, matrix products, per_device(): jnp.einsum('nbl,pbl->pbn', basis_part, further_blocks, preferred_element_...  4.83 us
    another operation x6, other arithmetic, factor_inverse(): lower_factor = jnp.linalg.cholesky(gram_matrix)  4.31 us
    another operation x4, other arithmetic, factor_inverse(): lax.linalg.triangular_solve(lower_factor, identity, left_side=True, lower...  3.75 us
  transfers between devices with their start and end apart: 3, of which 3 were waited for; matrix products, arithmetic and copies ran while one was open for 31% of the time, Pallas kernels for 0%

profile of v1, /device:TPU:0, one launch (start us, length us, event | category | flops | bytes accessed | tf_op | source)
XLA Modules:
  0.0 125.0 jit_solution(13439909117281681233)
XLA Ops:
  0.6 1.8 %fusion.93 = (bf16[1,4,32,4608]{3,2,1,0:T(8,128)(2,1)S(1)}, bf16[1,4,32,4608]{3,2,1,0:T(8,128)(2,1)S(1)}) fusion(bf16[2,4,32,4608]{3,2,1,0:T(8,128)(2,1)} %param.7), kind=kLoop, calls=%fused_computation.80 | loop fusion | bytes 4718592 | tf_op jit(solution)/shard_map/slice | solution.py:57
  2.5 1.9 %copy.50 = bf16[1,4,32,4608]{3,1,0,2:T(4,128)(2,1)} copy(bf16[1,4,32,4608]{3,2,1,0:T(8,128)(2,1)S(1)} %get-tuple-element.24) | data formatting | bytes 2359296
  4.4 7.3 %all-to-all-start = ((bf16[1,4,32,4608]{3,1,0,2:T(4,128)(2,1)}), bf16[1,4,32,4608]{3,1,0,2:T(4,128)(2,1)S(1)}, u32[]{:S(2)}, u32[]{:S(2)}) async-start(bf16[1,4,32,4608]{3,1,0,2:T(4,128)(2,1)} %copy.50), calls=%async_computation | async-start | bytes 2359296 | tf_op jit(solution)/shard_map/all_to_all | solution.py:16
  11.7 2.0 %copy.60 = bf16[1,4,32,4608]{3,1,2,0:T(4,128)(2,1)} copy(bf16[1,4,32,4608]{3,2,1,0:T(8,128)(2,1)S(1)} %get-tuple-element.25) | data formatting | bytes 2359296
  13.7 27.1 %all-to-all-done = bf16[1,4,32,4608]{3,1,0,2:T(4,128)(2,1)S(1)} async-done(((bf16[1,4,32,4608]{3,1,0,2:T(4,128)(2,1)}), bf16[1,4,32,4608]{3,1,0,2:T(4,128)(2,1)S(1)}, u32[]{:S(2)}, u32[]{:S(2)}) %all-to-all-start) | async-done | bytes 1179680 | tf_op jit(solution)/shard_map/all_to_all | solution.py:16
  40.8 3.8 %all-to-all-start.1 = ((bf16[1,4,32,4608]{3,1,0,2:T(4,128)(2,1)}), bf16[1,4,32,4608]{3,1,0,2:T(4,128)(2,1)}, u32[]{:S(2)}, u32[]{:S(2)}) async-start(bf16[1,4,32,4608]{3,1,0,2:T(4,128)(2,1)} %bitcast.20), calls=%async_computation.1 | async-start | bytes 2359296 | tf_op jit(solution)/shard_map/all_to_all | solution.py:16
  44.5 2.1 %fusion.95 = (bf16[8,4,4,1,4608]{4,0,2,1,3:T(8,128)(2,1)S(1)}, f32[4,4,1,8,4608]{4,3,1,0,2:T(8,128)}) fusion(bf16[8,4,4,1,4608]{4,2,1,0,3:T(4,128)(2,1)S(1)} %bitcast.203), kind=kLoop, calls=%fused_computation.82 | loop fusion | flops 589824 | bytes 4718592 | tf_op jit(solution)/shard_map/reshape | solution.py:27
  46.7 1.9 %reshape.235 = f32[16,1,36864]{2,0,1:T(8,128)S(1)} reshape(f32[4,4,1,8,4608]{4,3,1,0,2:T(8,128)} %get-tuple-element.29) | data formatting | bytes 4718592 | tf_op jit(solution)/shard_map/convert_element_type | solution.py:43
  48.5 1.4 %copy.51 = bf16[2,8,8,4608]{3,1,2,0:T(8,128)(2,1)} copy(bf16[2,8,8,4608]{3,2,1,0:T(8,128)(2,1)S(1)} %bitcast.204) | data formatting | bytes 2359296
  49.9 7.4 %fusion.4 = bf16[16,1,36864]{2,0,1:T(8,128)(2,1)S(1)} fusion(f32[16,1,36864]{2,0,1:T(8,128)S(1)} %reshape.235, bf16[64,1,36864]{2,0,1:T(8,128)(2,1)} %param.6, bf16[16,36864]{1,0:T(8,128)(2,1)} %bitcast.201), kind=kOutput, calls=%fused_computation.7 | convolution fusion | flops 152176640 | bytes 9437184 | tf_op jit(solution)/shard_map/bnp,nbl->pbl/dot_general | solution.py:41
  58.0 1.5 %custom-call.8 = f32[1,16,16]{2,1,0:T(8,128)S(1)} custom-call(f32[1,16,16]{2,1,0:T(8,128)S(1)} %fusion.78), custom_call_target="Cholesky" | custom-call | tf_op jit(solution)/shard_map/jit(cholesky)/cholesky | solution.py:8
  60.1 0.6 fusion.75
  60.8 1.2 custom-call.9
  62.2 1.1 convolution_convert_fusion.1
  63.3 10.3 %all-to-all-done.1 = bf16[1,4,32,4608]{3,1,0,2:T(4,128)(2,1)} async-done(((bf16[1,4,32,4608]{3,1,0,2:T(4,128)(2,1)}), bf16[1,4,32,4608]{3,1,0,2:T(4,128)(2,1)}, u32[]{:S(2)}, u32[]{:S(2)}) %all-to-all-start.1) | async-done | bytes 1179680 | tf_op jit(solution)/shard_map/all_to_all | solution.py:16
  73.6 3.0 %fusion.94 = (bf16[8,4,4,1,4608]{4,0,2,1,3:T(8,128)(2,1)}, f32[4,4,1,8,4608]{4,3,1,0,2:T(8,128)S(1)}) fusion(bf16[8,4,4,1,4608]{4,2,1,0,3:T(4,128)(2,1)} %bitcast.24), kind=kLoop, calls=%fused_computation.81 | loop fusion | flops 589824 | bytes 4718592 | tf_op jit(solution)/shard_map/reshape | solution.py:27
  76.7 1.6 %reshape.236 = f32[16,1,36864]{2,0,1:T(8,128)} reshape(f32[4,4,1,8,4608]{4,3,1,0,2:T(8,128)S(1)} %get-tuple-element.27) | data formatting | bytes 4718592 | tf_op jit(solution)/shard_map/convert_element_type | solution.py:43
  78.3 1.7 %copy.52 = bf16[2,8,8,4608]{3,1,2,0:T(8,128)(2,1)S(1)} copy(bf16[2,8,8,4608]{3,2,1,0:T(8,128)(2,1)} %bitcast.205) | data formatting | bytes 2359296
  80.0 1.9 %copy.61 = bf16[4,32,4608]{2,0,1:T(4,128)(2,1)} copy(bf16[4,32,4608]{2,1,0:T(8,128)(2,1)S(1)} %copy-done) | data formatting | bytes 2359296 | tf_op jit(solution)/shard_map/optimization_barrier | solution.py:61
  81.9 3.9 %all-to-all-start.2 = ((bf16[1,4,32,4608]{3,1,0,2:T(4,128)(2,1)}), bf16[1,4,32,4608]{3,1,0,2:T(4,128)(2,1)}, u32[]{:S(2)}, u32[]{:S(2)}) async-start(bf16[1,4,32,4608]{3,1,0,2:T(4,128)(2,1)} %bitcast.192), calls=%async_computation.2 | async-start | bytes 2359296 | tf_op jit(solution)/shard_map/all_to_all | solution.py:16
  85.9 8.5 %convolution_bitcast_fusion = f32[36864,16]{0,1:T(8,128)} fusion(bf16[64,1,36864]{2,0,1:T(8,128)(2,1)} %param.6, bf16[16,36864]{1,0:T(8,128)(2,1)S(1)} %bitcast.198), kind=kOutput, calls=%fused_computation.2 | convolution fusion | flops 150996992 | bytes 8257536 | tf_op jit(solution)/shard_map/bnp,nbl->pbl/dot_general | solution.py:41
  94.3 4.1 %fusion.3 = bf16[16,1,36864]{2,0,1:T(8,128)(2,1)S(1)} fusion(f32[16,1,36864]{2,0,1:T(8,128)} %reshape.236, f32[36864,16]{0,1:T(8,128)} %convolution_bitcast_fusion, bf16[36864,16]{0,1:T(8,128)(2,1)S(1)} %convolution_convert_fusion.1, bf16[16,36864]{1,0:T(8,128)(2,1)S(1)} %bitcast.199), kind=kOutput, calls=%fused_computation.6 | convolution fusion | flops 39518720 | bytes 8257536 | tf_op jit(solution)/shard_map/bnp,nbl->pbl/dot_general | solution.py:41
  99.1 1.5 %custom-call.10 = f32[1,16,16]{2,1,0:T(8,128)S(1)} custom-call(f32[1,16,16]{2,1,0:T(8,128)S(1)} %fusion.77), custom_call_target="Cholesky" | custom-call | tf_op jit(solution)/shard_map/jit(cholesky)/cholesky | solution.py:8
  101.3 0.6 fusion.76
  102.0 1.2 custom-call.11
  103.4 1.1 fusion.5
  104.5 10.3 %all-to-all-done.2 = bf16[1,4,32,4608]{3,1,0,2:T(4,128)(2,1)} async-done(((bf16[1,4,32,4608]{3,1,0,2:T(4,128)(2,1)}), bf16[1,4,32,4608]{3,1,0,2:T(4,128)(2,1)}, u32[]{:S(2)}, u32[]{:S(2)}) %all-to-all-start.2) | async-done | bytes 1179680 | tf_op jit(solution)/shard_map/all_to_all | solution.py:16
  114.8 1.9 %copy.38 = bf16[8,4,4,1,4608]{4,0,2,1,3:T(8,128)(2,1)S(1)} copy(bf16[8,4,4,1,4608]{4,2,1,0,3:T(4,128)(2,1)} %bitcast.48) | data formatting | bytes 2359296 | tf_op jit(solution)/shard_map/reshape | solution.py:27
  117.0 3.7 %fusion.57 = f32[16,1,64]{2,0,1:T(8,128)S(1)} fusion(bf16[16,36864]{1,0:T(8,128)(2,1)S(1)} %bitcast.195, bf16[64,1,36864]{2,0,1:T(8,128)(2,1)} %param.6), kind=kOutput, calls=%fused_computation.47 | convolution fusion | flops 75498496 | bytes 5902336 | tf_op jit(solution)/shard_map/nbl,pbl->pbn/dot_general | solution.py:72
  121.3 0.7 copy.42
  122.6 1.6 %pad_maximum_fusion = bf16[2,16,1,36864]{3,1,2,0:T(8,128)(2,1)} fusion(bf16[1,16,1,36864]{3,1,2,0:T(8,128)(2,1)S(1)} %bitcast.200, bf16[1,16,1,36864]{3,1,2,0:T(8,128)(2,1)S(1)} %bitcast.194), kind=kLoop, calls=%fused_computation.19 | loop fusion | flops 1179648 | bytes 4718592 | tf_op jit(solution)/shard_map/stack | solution.py:78
  124.3 0.7 pad_maximum_fusion.1
  (20 shorter events, 4.7 us)
Async XLA Ops:
  4.4 36.4 %all-to-all-start = ((bf16[1,4,32,4608]{3,1,0,2:T(4,128)(2,1)}), bf16[1,4,32,4608]{3,1,0,2:T(4,128)(2,1)S(1)}, u32[]{:S(2)}, u32[]{:S(2)}) async-start(bf16[1,4,32,4608]{3,1,0,2:T(4,128)(2,1)} %copy.50), calls=%async_computation | async-start | bytes 2359296 | tf_op jit(solution)/shard_map/all_to_all | solution.py:16
  40.8 32.8 %all-to-all-start.1 = ((bf16[1,4,32,4608]{3,1,0,2:T(4,128)(2,1)}), bf16[1,4,32,4608]{3,1,0,2:T(4,128)(2,1)}, u32[]{:S(2)}, u32[]{:S(2)}) async-start(bf16[1,4,32,4608]{3,1,0,2:T(4,128)(2,1)} %bitcast.20), calls=%async_computation.1 | async-start | bytes 2359296 | tf_op jit(solution)/shard_map/all_to_all | solution.py:16
  78.3 1.7 %copy-start = (bf16[4,32,4608]{2,1,0:T(8,128)(2,1)S(1)}, bf16[4,32,4608]{2,1,0:T(8,128)(2,1)}, u32[]{:S(2)}) copy-start(bf16[4,32,4608]{2,1,0:T(8,128)(2,1)} %param.8) | copy-start | bytes 3538948
  81.9 32.8 %all-to-all-start.2 = ((bf16[1,4,32,4608]{3,1,0,2:T(4,128)(2,1)}), bf16[1,4,32,4608]{3,1,0,2:T(4,128)(2,1)}, u32[]{:S(2)}, u32[]{:S(2)}) async-start(bf16[1,4,32,4608]{3,1,0,2:T(4,128)(2,1)} %bitcast.192), calls=%async_computation.2 | async-start | bytes 2359296 | tf_op jit(solution)/shard_map/all_to_all | solution.py:16
  122.6 1.6 %copy-start.1 = (f32[16,1,16]{2,0,1:T(8,128)S(1)}, f32[16,1,16]{2,0,1:T(8,128)}, u32[]{:S(2)}) copy-start(f32[16,1,16]{2,0,1:T(8,128)} %copy.42) | copy-start | bytes 3076

commit v2 on v1

--- a/solution.py
+++ b/solution.py
@@ -12,21 +12,21 @@
     return lax.linalg.triangular_solve(lower_factor, identity, left_side=True, lower=True)
 
 
-def send(arriving):
-    return lax.all_to_all(
-        arriving[None], ("lat", "mode"), split_axis=2, concat_axis=0, tiled=True
-    )
+def send(block_major):
+    return lax.all_to_all(block_major, ("lat", "mode"), split_axis=0, concat_axis=0, tiled=True)
+
+
+def split_by_source(received):
+    lat_count = lax.axis_size("lat")
+    mode_count = lax.axis_size("mode")
+    return received.reshape(lat_count, mode_count, received.shape[1], received.shape[2])
 
 
 def arrange(received):
-    lat_count = lax.axis_size("lat")
-    mode_count = lax.axis_size("mode")
-    vector_part = received.shape[1]
-    block_count = received.shape[2]
-    entry_part = received.shape[3]
-    received = received.reshape(lat_count, mode_count, vector_part, block_count, entry_part)
-    received = received.transpose(1, 2, 3, 0, 4)
-    return received.reshape(mode_count * vector_part, block_count, lat_count * entry_part)
+    by_source = split_by_source(received)
+    lat_count, mode_count, vector_part, entry_part = by_source.shape
+    whole = by_source.transpose(1, 2, 0, 3)
+    return whole.reshape(mode_count * vector_part, 1, lat_count * entry_part)
 
 
 def project(earlier, finished, vectors, block_len):
@@ -54,17 +54,18 @@
 def per_device(earlier, panels, further):
     block_len = earlier.shape[2]
     panel_count = panels.shape[0]
-    arrived = [send(panels[0])]
-    for panel_index in range(1, panel_count):
-        outgoing, arrived[-1] = lax.optimization_barrier((panels[panel_index], arrived[-1]))
-        arrived.append(send(outgoing))
-    outgoing, arrived[-1] = lax.optimization_barrier((further, arrived[-1]))
-    further_arrived = send(outgoing)
+    outgoing = [panels[k].transpose(1, 0, 2) for k in range(panel_count)]
+    outgoing.append(further.transpose(1, 0, 2))
+    arrived = [send(outgoing[0])]
+    for index in range(1, len(outgoing)):
+        ready, arrived[-1] = lax.optimization_barrier((outgoing[index], arrived[-1]))
+        arrived.append(send(ready))
     finished = []
     for panel_index in range(panel_count):
         vectors = arrange(arrived[panel_index])
         finished.append(project(earlier, finished, vectors, block_len))
-    finished, further_arrived = lax.optimization_barrier((finished, further_arrived))
+    finished, further_arrived = lax.optimization_barrier((finished, arrived[-1]))
+    new_basis = jnp.stack(finished, 0)
     further_blocks = arrange(further_arrived)
     products = []
     for basis_part in [earlier] + finished:
@@ -75,7 +76,7 @@
             / block_len
         )
     coarse = jnp.concatenate(products, axis=2)
-    return (jnp.stack(finished, 0), coarse)
+    return (new_basis, coarse)
 
 
 def solution(mesh):

time: 126 us -> 124 us (0.984)
  waiting for transfers between devices: 47.7 us -> 44 us
  matrix products: 28.6 us -> 29.9 us
    all_to_all x3, waiting for transfers between devices: 47.7 us -> 44 us  [send(): lax.all_to_all(block_major, ('lat', 'mode'), split_axis=0, concat_axis=0,...]
    optimization_barrier x1 -> x0, local copies, waits for them, and re-layouts: 1.91 us -> none  [per_device(): outgoing, arrived[-1] = lax.optimization_barrier((further, arrived[-1]))]
    unnamed x9 -> x14, local copies, waits for them, and re-layouts: 7.31 us -> 9.19 us
    dot_general x2, matrix products: 2.16 us -> 3.43 us  [project(): jnp.einsum('bpq,qbl->pbl', inverse, residual_wide, precision=lax.Precisio...]
  transfers between devices with their start and end apart: 3 -> 3, of which waited for: 3 -> 3; matrix products, arithmetic and copies ran while one was open for 31% -> 35% of each run, Pallas kernels for 0% -> 0%
where the time goes in v2:
time: 124 us; the launch traced here: 123 us
  waiting for transfers between devices  44 us (35%)
  matrix products  29.9 us (24%)
  local copies, waits for them, and re-layouts  17.4 us (14%)
  other arithmetic  15.9 us (13%)
  starting transfers between devices  15 us (12%)
    all_to_all x3, waiting for transfers between devices, send(): lax.all_to_all(block_major, ('lat', 'mode'), split_axis=0, concat_axis=0,...  44 us
    dot_general x3, matrix products, project(): jnp.einsum('bnp,nbl->pbl', coeffs, basis_part, preferred_element_type=jnp...  20 us
    all_to_all x3, starting transfers between devices, send(): lax.all_to_all(block_major, ('lat', 'mode'), split_axis=0, concat_axis=0,...  15 us
    unnamed x14, local copies, waits for them, and re-layouts  9.19 us
    reshape x2, other arithmetic, split_by_source(): received.reshape(lat_count, mode_count, received.shape[1], received.shape...  5.56 us
    dot_general x3, matrix products, per_device(): jnp.einsum('nbl,pbl->pbn', basis_part, further_blocks, preferred_element_...  4.86 us
    another operation x6, other arithmetic, factor_inverse(): lower_factor = jnp.linalg.cholesky(gram_matrix)  4.31 us
    another operation x4, other arithmetic, factor_inverse(): lax.linalg.triangular_solve(lower_factor, identity, left_side=True, lower...  3.75 us
  transfers between devices with their start and end apart: 3, of which 3 were waited for; matrix products, arithmetic and copies ran while one was open for 35% of the time, Pallas kernels for 0%

profile of v2, /device:TPU:0, one launch (start us, length us, event | category | flops | bytes accessed | tf_op | source)
XLA Modules:
  0.0 123.0 jit_solution(2538599774475353192)
XLA Ops:
  0.6 1.8 %fusion.93 = (bf16[1,4,32,4608]{3,2,1,0:T(8,128)(2,1)S(1)}, bf16[1,4,32,4608]{3,2,1,0:T(8,128)(2,1)S(1)}) fusion(bf16[2,4,32,4608]{3,2,1,0:T(8,128)(2,1)} %param.7), kind=kLoop, calls=%fused_computation.81 | loop fusion | bytes 4718592 | tf_op jit(solution)/shard_map/slice | solution.py:57
  2.4 1.9 %copy.61 = bf16[1,4,32,4608]{3,1,2,0:T(4,128)(2,1)} copy(bf16[1,4,32,4608]{3,2,1,0:T(8,128)(2,1)S(1)} %get-tuple-element.24) | data formatting | bytes 2359296
  4.4 7.3 %all-to-all-start = ((bf16[32,4,4608]{2,1,0:T(4,128)(2,1)}), bf16[32,4,4608]{2,1,0:T(4,128)(2,1)S(1)}, u32[]{:S(2)}, u32[]{:S(2)}) async-start(bf16[32,4,4608]{2,1,0:T(4,128)(2,1)} %bitcast.174), calls=%async_computation | async-start | bytes 2359296 | tf_op jit(solution)/shard_map/all_to_all | solution.py:16
  11.7 2.0 %copy.62 = bf16[1,4,32,4608]{3,1,2,0:T(4,128)(2,1)} copy(bf16[1,4,32,4608]{3,2,1,0:T(8,128)(2,1)S(1)} %get-tuple-element.25) | data formatting | bytes 2359296
  13.7 1.9 %copy.63 = bf16[4,32,4608]{2,0,1:T(4,128)(2,1)} copy(bf16[4,32,4608]{2,1,0:T(8,128)(2,1)S(1)} %copy-done.2) | data formatting | bytes 2359296 | tf_op args[2]
  15.6 25.2 %all-to-all-done = bf16[32,4,4608]{2,1,0:T(4,128)(2,1)S(1)} async-done(((bf16[32,4,4608]{2,1,0:T(4,128)(2,1)}), bf16[32,4,4608]{2,1,0:T(4,128)(2,1)S(1)}, u32[]{:S(2)}, u32[]{:S(2)}) %all-to-all-start) | async-done | bytes 1179680 | tf_op jit(solution)/shard_map/all_to_all | solution.py:16
  40.7 3.8 %all-to-all-start.1 = ((bf16[32,4,4608]{2,1,0:T(4,128)(2,1)}), bf16[32,4,4608]{2,1,0:T(4,128)(2,1)}, u32[]{:S(2)}, u32[]{:S(2)}) async-start(bf16[32,4,4608]{2,1,0:T(4,128)(2,1)} %bitcast.175), calls=%async_computation.1 | async-start | bytes 2359296 | tf_op jit(solution)/shard_map/all_to_all | solution.py:16
  44.5 2.5 %fusion.95 = (bf16[8,4,4,4608]{3,0,2,1:T(8,128)(2,1)}, f32[4,4,8,4608]{3,2,1,0:T(8,128)}) fusion(bf16[8,4,4,4608]{3,2,1,0:T(4,128)(2,1)S(1)} %bitcast.188), kind=kLoop, calls=%fused_computation.83 | loop fusion | flops 589824 | bytes 4718592 | tf_op jit(solution)/shard_map/reshape | solution.py:22
  47.0 1.9 %reshape.235 = f32[16,1,36864]{2,0,1:T(8,128)S(1)} reshape(f32[4,4,8,4608]{3,2,1,0:T(8,128)} %get-tuple-element.29) | data formatting | bytes 4718592 | tf_op jit(solution)/shard_map/convert_element_type | solution.py:43
  49.0 1.4 %copy.51 = bf16[2,8,8,4608]{3,1,2,0:T(8,128)(2,1)} copy(bf16[2,8,8,4608]{3,2,1,0:T(8,128)(2,1)S(1)} %bitcast.189) | data formatting | bytes 2359296
  50.4 7.4 %fusion.4 = bf16[16,1,36864]{2,0,1:T(8,128)(2,1)S(1)} fusion(f32[16,1,36864]{2,0,1:T(8,128)S(1)} %reshape.235, bf16[64,1,36864]{2,0,1:T(8,128)(2,1)} %param.6, bf16[16,36864]{1,0:T(8,128)(2,1)} %bitcast.185), kind=kOutput, calls=%fused_computation.7 | convolution fusion | flops 152176640 | bytes 9437184 | tf_op jit(solution)/shard_map/bnp,nbl->pbl/dot_general | solution.py:41
  58.4 1.5 %custom-call.8 = f32[1,16,16]{2,1,0:T(8,128)S(1)} custom-call(f32[1,16,16]{2,1,0:T(8,128)S(1)} %fusion.78), custom_call_target="Cholesky" | custom-call | tf_op jit(solution)/shard_map/jit(cholesky)/cholesky | solution.py:8
  60.6 0.6 fusion.75
  61.3 1.2 custom-call.9
  62.7 2.4 %convolution_convert_fusion.1 = bf16[36864,16]{0,1:T(8,128)(2,1)S(1)} fusion(f32[16,16]{1,0:T(8,128)S(1)} %fusion.82, bf16[16,1,36864]{2,0,1:T(8,128)(2,1)} %copy-done), kind=kOutput, calls=%fused_computation.9 | convolution fusion | flops 113836032 | bytes 2360320 | tf_op jit(solution)/shard_map/bpq,qbl->pbl/dot_general | solution.py:50
  65.0 8.5 %all-to-all-done.1 = bf16[32,4,4608]{2,1,0:T(4,128)(2,1)} async-done(((bf16[32,4,4608]{2,1,0:T(4,128)(2,1)}), bf16[32,4,4608]{2,1,0:T(4,128)(2,1)}, u32[]{:S(2)}, u32[]{:S(2)}) %all-to-all-start.1) | async-done | bytes 1179680 | tf_op jit(solution)/shard_map/all_to_all | solution.py:16
  73.6 3.1 %fusion.94 = (bf16[8,4,4,4608]{3,0,2,1:T(8,128)(2,1)}, f32[4,4,8,4608]{3,2,1,0:T(8,128)S(1)}) fusion(bf16[8,4,4,4608]{3,2,1,0:T(4,128)(2,1)} %bitcast.21), kind=kLoop, calls=%fused_computation.82 | loop fusion | flops 589824 | bytes 4718592 | tf_op jit(solution)/shard_map/reshape | solution.py:22
  76.6 1.6 %reshape.236 = f32[16,1,36864]{2,0,1:T(8,128)} reshape(f32[4,4,8,4608]{3,2,1,0:T(8,128)S(1)} %get-tuple-element.27) | data formatting | bytes 4718592 | tf_op jit(solution)/shard_map/convert_element_type | solution.py:43
  78.3 1.6 %copy.52 = bf16[2,8,8,4608]{3,1,2,0:T(8,128)(2,1)S(1)} copy(bf16[2,8,8,4608]{3,2,1,0:T(8,128)(2,1)} %bitcast.190) | data formatting | bytes 2359296
  79.9 4.0 %all-to-all-start.2 = ((bf16[32,4,4608]{2,1,0:T(4,128)(2,1)}), bf16[32,4,4608]{2,1,0:T(4,128)(2,1)}, u32[]{:S(2)}, u32[]{:S(2)}) async-start(bf16[32,4,4608]{2,1,0:T(4,128)(2,1)} %bitcast.186), calls=%async_computation.2 | async-start | bytes 2359296 | tf_op jit(solution)/shard_map/all_to_all | solution.py:16
  83.8 8.5 %convolution_bitcast_fusion = f32[36864,16]{0,1:T(8,128)} fusion(bf16[64,1,36864]{2,0,1:T(8,128)(2,1)} %param.6, bf16[16,36864]{1,0:T(8,128)(2,1)S(1)} %bitcast.182), kind=kOutput, calls=%fused_computation.2 | convolution fusion | flops 150996992 | bytes 8257536 | tf_op jit(solution)/shard_map/bnp,nbl->pbl/dot_general | solution.py:41
  92.3 4.1 %fusion.3 = bf16[16,1,36864]{2,0,1:T(8,128)(2,1)S(1)} fusion(f32[16,1,36864]{2,0,1:T(8,128)} %reshape.236, f32[36864,16]{0,1:T(8,128)} %convolution_bitcast_fusion, bf16[36864,16]{0,1:T(8,128)(2,1)S(1)} %convolution_convert_fusion.1, bf16[16,36864]{1,0:T(8,128)(2,1)S(1)} %bitcast.183), kind=kOutput, calls=%fused_computation.6 | convolution fusion | flops 39518720 | bytes 8257536 | tf_op jit(solution)/shard_map/bnp,nbl->pbl/dot_general | solution.py:41
  97.1 1.5 %custom-call.10 = f32[1,16,16]{2,1,0:T(8,128)S(1)} custom-call(f32[1,16,16]{2,1,0:T(8,128)S(1)} %fusion.77), custom_call_target="Cholesky" | custom-call | tf_op jit(solution)/shard_map/jit(cholesky)/cholesky | solution.py:8
  99.3 0.6 fusion.76
  99.9 1.2 custom-call.11
  101.4 1.1 fusion.5
  102.4 10.3 %all-to-all-done.2 = bf16[32,4,4608]{2,1,0:T(4,128)(2,1)} async-done(((bf16[32,4,4608]{2,1,0:T(4,128)(2,1)}), bf16[32,4,4608]{2,1,0:T(4,128)(2,1)}, u32[]{:S(2)}, u32[]{:S(2)}) %all-to-all-start.2) | async-done | bytes 1179680 | tf_op jit(solution)/shard_map/all_to_all | solution.py:16
  112.7 1.9 %copy.38 = bf16[8,4,4,4608]{3,0,2,1:T(8,128)(2,1)S(1)} copy(bf16[8,4,4,4608]{3,2,1,0:T(4,128)(2,1)} %bitcast.41) | data formatting | bytes 2359296 | tf_op jit(solution)/shard_map/reshape | solution.py:22
  115.0 3.7 %fusion.57 = f32[16,1,64]{2,0,1:T(8,128)S(1)} fusion(bf16[16,36864]{1,0:T(8,128)(2,1)S(1)} %bitcast.179, bf16[64,1,36864]{2,0,1:T(8,128)(2,1)} %param.6), kind=kOutput, calls=%fused_computation.48 | convolution fusion | flops 75498496 | bytes 5902336 | tf_op jit(solution)/shard_map/nbl,pbl->pbn/dot_general | solution.py:73
  119.3 0.7 copy.42
  120.7 1.6 %pad_maximum_fusion = bf16[2,16,1,36864]{3,1,2,0:T(8,128)(2,1)} fusion(bf16[1,16,1,36864]{3,1,2,0:T(8,128)(2,1)S(1)} %bitcast.184, bf16[1,16,1,36864]{3,1,2,0:T(8,128)(2,1)S(1)} %bitcast.178), kind=kLoop, calls=%fused_computation.19 | loop fusion | flops 1179648 | bytes 4718592 | tf_op jit(solution)/shard_map/stack | solution.py:68
  122.3 0.7 pad_maximum_fusion.1
  (24 shorter events, 4.8 us)
Async XLA Ops:
  4.4 36.4 %all-to-all-start = ((bf16[32,4,4608]{2,1,0:T(4,128)(2,1)}), bf16[32,4,4608]{2,1,0:T(4,128)(2,1)S(1)}, u32[]{:S(2)}, u32[]{:S(2)}) async-start(bf16[32,4,4608]{2,1,0:T(4,128)(2,1)} %bitcast.174), calls=%async_computation | async-start | bytes 2359296 | tf_op jit(solution)/shard_map/all_to_all | solution.py:16
  11.7 2.0 %copy-start.2 = (bf16[4,32,4608]{2,1,0:T(8,128)(2,1)S(1)}, bf16[4,32,4608]{2,1,0:T(8,128)(2,1)}, u32[]{:S(2)}) copy-start(bf16[4,32,4608]{2,1,0:T(8,128)(2,1)} %param.8) | copy-start | bytes 3538948
  40.7 32.8 %all-to-all-start.1 = ((bf16[32,4,4608]{2,1,0:T(4,128)(2,1)}), bf16[32,4,4608]{2,1,0:T(4,128)(2,1)}, u32[]{:S(2)}, u32[]{:S(2)}) async-start(bf16[32,4,4608]{2,1,0:T(4,128)(2,1)} %bitcast.175), calls=%async_computation.1 | async-start | bytes 2359296 | tf_op jit(solution)/shard_map/all_to_all | solution.py:16
  47.0 2.0 %copy-start.1 = (bf16[8,4,4,4608]{3,0,2,1:T(8,128)(2,1)S(1)}, bf16[8,4,4,4608]{3,0,2,1:T(8,128)(2,1)}, u32[]{:S(2)}) copy-start(bf16[8,4,4,4608]{3,0,2,1:T(8,128)(2,1)} %get-tuple-element.28) | copy-start | bytes 3538948
  57.8 4.7 %copy-start = (bf16[16,1,36864]{2,0,1:T(8,128)(2,1)}, bf16[16,1,36864]{2,0,1:T(8,128)(2,1)S(1)}, u32[]{:S(2)}) copy-start(bf16[16,1,36864]{2,0,1:T(8,128)(2,1)S(1)} %fusion.4) | copy-start | bytes 3538948
  79.9 32.9 %all-to-all-start.2 = ((bf16[32,4,4608]{2,1,0:T(4,128)(2,1)}), bf16[32,4,4608]{2,1,0:T(4,128)(2,1)}, u32[]{:S(2)}, u32[]{:S(2)}) async-start(bf16[32,4,4608]{2,1,0:T(4,128)(2,1)} %bitcast.186), calls=%async_computation.2 | async-start | bytes 2359296 | tf_op jit(solution)/shard_map/all_to_all | solution.py:16
  120.6 1.6 %copy-start.3 = (f32[16,1,16]{2,0,1:T(8,128)S(1)}, f32[16,1,16]{2,0,1:T(8,128)}, u32[]{:S(2)}) copy-start(f32[16,1,16]{2,0,1:T(8,128)} %copy.42) | copy-start | bytes 3076

commit v3 on v2

--- a/solution.py
+++ b/solution.py
@@ -1,7 +1,50 @@
+import functools
+
 import jax
 import jax.numpy as jnp
 from jax import lax
+from jax.experimental import pallas as pl
+from jax.experimental.pallas import tpu as pltpu
 from jax.sharding import PartitionSpec as P
+
+NT = (((1,), (1,)), ((), ()))
+
+
+def project_kernel(*refs, piece_count, block_len):
+    basis_refs = refs[:piece_count]
+    vectors_ref, residual_ref, gram_ref = refs[piece_count:]
+    vectors = vectors_ref[...]
+    removed = None
+    for basis_ref in basis_refs:
+        basis = basis_ref[...]
+        coeffs_t = lax.dot_general(vectors, basis, NT, preferred_element_type=jnp.float32)
+        coeffs_t = (coeffs_t / block_len).astype(jnp.bfloat16)
+        term = jnp.dot(coeffs_t, basis, preferred_element_type=jnp.float32)
+        removed = term if removed is None else removed + term
+    residual = (vectors.astype(jnp.float32) - removed).astype(jnp.bfloat16)
+    residual_ref[...] = residual
+    gram_ref[...] = lax.dot_general(residual, residual, NT, preferred_element_type=jnp.float32) / block_len
+
+
+def project_call(pieces, vectors):
+    count, block_len = vectors.shape
+    rows = sum(p.shape[0] for p in pieces)
+    spec = pl.BlockSpec(memory_space=pltpu.MemorySpace.VMEM)
+    return pl.pallas_call(
+        functools.partial(project_kernel, piece_count=len(pieces), block_len=block_len),
+        out_shape=(
+            jax.ShapeDtypeStruct((count, block_len), jnp.bfloat16),
+            jax.ShapeDtypeStruct((count, count), jnp.float32),
+        ),
+        in_specs=[spec] * (len(pieces) + 1),
+        out_specs=(spec, spec),
+        compiler_params=pltpu.CompilerParams(vmem_limit_bytes=48 * 1024 * 1024),
+        cost_estimate=pl.CostEstimate(
+            flops=4 * rows * count * block_len + 2 * count * count * block_len,
+            transcendentals=0,
+            bytes_accessed=2 * block_len * (rows + 2 * count) + 4 * count * count,
+        ),
+    )(*pieces, vectors)
 
 
 def factor_inverse(gram_matrix):
@@ -30,25 +73,12 @@
 
 
 def project(earlier, finished, vectors, block_len):
-    pieces = [earlier] + finished
-    removed = None
-    for basis_part in pieces:
-        coeffs = (
-            jnp.einsum("nbl,pbl->bnp", basis_part, vectors, preferred_element_type=jnp.float32)
-            / block_len
-        )
-        coeffs = coeffs.astype(jnp.bfloat16)
-        term = jnp.einsum("bnp,nbl->pbl", coeffs, basis_part, preferred_element_type=jnp.float32)
-        removed = term if removed is None else removed + term
-    residual = (vectors.astype(jnp.float32) - removed).astype(jnp.bfloat16)
-    gram_matrix = (
-        jnp.einsum("pbl,qbl->bpq", residual, residual, preferred_element_type=jnp.float32)
-        / block_len
-    )
+    count = vectors.shape[0]
+    pieces = [piece.reshape(piece.shape[0], block_len) for piece in [earlier] + finished]
+    residual, gram_matrix = project_call(pieces, vectors.reshape(count, block_len))
     inverse = factor_inverse(gram_matrix)
-    residual_wide = lax.optimization_barrier(residual).astype(jnp.float32)
-    fresh = jnp.einsum("bpq,qbl->pbl", inverse, residual_wide, precision=lax.Precision.HIGHEST)
-    return fresh.astype(jnp.bfloat16)
+    fresh = jnp.dot(inverse, residual.astype(jnp.float32), precision=lax.Precision.HIGHEST)
+    return fresh.astype(jnp.bfloat16).reshape(count, 1, block_len)
 
 
 def per_device(earlier, panels, further):

time: 124 us -> 116 us (0.935)
  matrix products: 29.9 us -> 7.48 us
  waiting for transfers between devices: 44 us -> 57.5 us
  Pallas kernels: 0 us -> 12.9 us
  other arithmetic: 15.9 us -> 10.4 us
  local copies, waits for them, and re-layouts: 17.4 us -> 12 us
    dot_general x7 -> x2, matrix products: 24.6 us -> 2.16 us  [project(): jnp.dot(inverse, residual.astype(jnp.float32), precision=lax.Precision.HI...]
    all_to_all x3, waiting for transfers between devices: 44 us -> 57.5 us  [send(): lax.all_to_all(block_major, ('lat', 'mode'), split_axis=0, concat_axis=0,...]
    pallas_call x0 -> x2, Pallas kernels: none -> 12.9 us  [project_call(): pl.pallas_call(functools.partial(project_kernel, piece_count=len(pieces),...]
    reshape x2 -> x0, other arithmetic: 5.56 us -> none  [split_by_source(): received.reshape(lat_count, mode_count, received.shape[1], received.shape...]
    convert_element_type x2 -> x0, local copies, waits for them, and re-layouts: 3.57 us -> none  [project(): residual = (vectors.astype(jnp.float32) - removed).astype(jnp.bfloat16)]
    unnamed x14 -> x8, local copies, waits for them, and re-layouts: 9.19 us -> 6.81 us
    reshape x1 -> x3, local copies, waits for them, and re-layouts: 1.92 us -> 3.22 us  [split_by_source(): received.reshape(lat_count, mode_count, received.shape[1], received.shape...]
  transfers between devices with their start and end apart: 3 -> 3, of which waited for: 3 -> 3; matrix products, arithmetic and copies ran while one was open for 35% -> 14% of each run, Pallas kernels for 0% -> 11%
where the time goes in v3:
time: 116 us
  waiting for transfers between devices  57.5 us (50%)
  starting transfers between devices  14.9 us (13%)
  Pallas kernels  12.9 us (11%)
  local copies, waits for them, and re-layouts  12 us (10%)
  other arithmetic  10.4 us (9%)
  matrix products  7.48 us (6%)
    all_to_all x3, waiting for transfers between devices, send(): lax.all_to_all(block_major, ('lat', 'mode'), split_axis=0, concat_axis=0,...  57.5 us
    all_to_all x3, starting transfers between devices, send(): lax.all_to_all(block_major, ('lat', 'mode'), split_axis=0, concat_axis=0,...  14.9 us
    pallas_call x2, Pallas kernels, project_call(): pl.pallas_call(functools.partial(project_kernel, piece_count=len(pieces),...  12.9 us
    unnamed x8, local copies, waits for them, and re-layouts  6.81 us
    dot_general x3, matrix products, per_device(): jnp.einsum('nbl,pbl->pbn', basis_part, further_blocks, preferred_element_...  4.92 us
    another operation x6, other arithmetic, factor_inverse(): lower_factor = jnp.linalg.cholesky(gram_matrix)  4.31 us
    another operation x4, other arithmetic, factor_inverse(): lax.linalg.triangular_solve(lower_factor, identity, left_side=True, lower...  3.75 us
    reshape x3, local copies, waits for them, and re-layouts, split_by_source(): received.reshape(lat_count, mode_count, received.shape[1], received.shape...  3.22 us
  transfers between devices with their start and end apart: 3, of which 3 were waited for; matrix products, arithmetic and copies ran while one was open for 14% of the time, Pallas kernels for 11%

profile of v3, /device:TPU:0, one launch (start us, length us, event | category | flops | bytes accessed | tf_op | source)
XLA Modules:
  0.0 115.9 jit_solution(9288815799733217027)
XLA Ops:
  0.6 1.8 %fusion.29 = (bf16[1,4,32,4608]{3,2,1,0:T(8,128)(2,1)S(1)}, bf16[1,4,32,4608]{3,2,1,0:T(8,128)(2,1)S(1)}) fusion(bf16[2,4,32,4608]{3,2,1,0:T(8,128)(2,1)} %param.7), kind=kLoop, calls=%fused_computation.39 | loop fusion | bytes 4718592 | tf_op jit(solution)/shard_map/slice | solution.py:87
  2.5 1.9 %copy.33 = bf16[1,4,32,4608]{3,1,2,0:T(4,128)(2,1)} copy(bf16[1,4,32,4608]{3,2,1,0:T(8,128)(2,1)S(1)} %get-tuple-element.32) | data formatting | bytes 2359296
  4.4 7.3 %all-to-all-start = ((bf16[32,4,4608]{2,1,0:T(4,128)(2,1)}), bf16[32,4,4608]{2,1,0:T(4,128)(2,1)S(1)}, u32[]{:S(2)}, u32[]{:S(2)}) async-start(bf16[32,4,4608]{2,1,0:T(4,128)(2,1)} %bitcast.79), calls=%async_computation | async-start | bytes 2359296 | tf_op jit(solution)/shard_map/all_to_all | solution.py:59
  11.7 1.9 %copy.34 = bf16[1,4,32,4608]{3,1,2,0:T(4,128)(2,1)} copy(bf16[1,4,32,4608]{3,2,1,0:T(8,128)(2,1)S(1)} %get-tuple-element.33) | data formatting | bytes 2359296
  13.6 27.2 %all-to-all-done = bf16[32,4,4608]{2,1,0:T(4,128)(2,1)S(1)} async-done(((bf16[32,4,4608]{2,1,0:T(4,128)(2,1)}), bf16[32,4,4608]{2,1,0:T(4,128)(2,1)S(1)}, u32[]{:S(2)}, u32[]{:S(2)}) %all-to-all-start) | async-done | bytes 1179680 | tf_op jit(solution)/shard_map/all_to_all | solution.py:59
  40.8 3.7 %all-to-all-start.1 = ((bf16[32,4,4608]{2,1,0:T(4,128)(2,1)}), bf16[32,4,4608]{2,1,0:T(4,128)(2,1)S(1)}, u32[]{:S(2)}, u32[]{:S(2)}) async-start(bf16[32,4,4608]{2,1,0:T(4,128)(2,1)} %bitcast.80), calls=%async_computation.1 | async-start | bytes 2359296 | tf_op jit(solution)/shard_map/all_to_all | solution.py:59
  44.4 1.9 %copy.35 = bf16[4,32,4608]{2,0,1:T(4,128)(2,1)} copy(bf16[4,32,4608]{2,1,0:T(8,128)(2,1)S(1)} %copy-done) | data formatting | bytes 2359296 | tf_op args[2]
  46.4 0.7 copy.18
  47.0 0.3 copy.27
  47.4 26.1 %all-to-all-done.1 = bf16[32,4,4608]{2,1,0:T(4,128)(2,1)S(1)} async-done(((bf16[32,4,4608]{2,1,0:T(4,128)(2,1)}), bf16[32,4,4608]{2,1,0:T(4,128)(2,1)S(1)}, u32[]{:S(2)}, u32[]{:S(2)}) %all-to-all-start.1) | async-done | bytes 1179680 | tf_op jit(solution)/shard_map/all_to_all | solution.py:59
  73.5 3.9 %all-to-all-start.2 = ((bf16[32,4,4608]{2,1,0:T(4,128)(2,1)}), bf16[32,4,4608]{2,1,0:T(4,128)(2,1)}, u32[]{:S(2)}, u32[]{:S(2)}) async-start(bf16[32,4,4608]{2,1,0:T(4,128)(2,1)} %bitcast.81), calls=%async_computation.2 | async-start | bytes 2359296 | tf_op jit(solution)/shard_map/all_to_all | solution.py:59
  77.5 6.8 %shard_map.50 = (bf16[16,36864]{1,0:T(8,128)(2,1)S(1)}, f32[16,16]{1,0:T(8,128)S(1)}) custom-call(bf16[64,36864]{1,0:T(8,128)(2,1)} %bitcast.86, bf16[16,36864]{1,0:T(8,128)(2,1)S(1)} %bitcast.85), custom_call_target="tpu_custom_call" | custom-call | flops 169869312 | bytes 7078912 | tf_op jit(solution)/shard_map/pallas_call | solution.py:33
  84.4 1.5 %cholesky.44 = f32[16,16]{1,0:T(8,128)S(1)} custom-call(f32[16,16]{1,0:T(8,128)S(1)} %fusion.27), custom_call_target="Cholesky" | custom-call | tf_op jit(solution)/shard_map/jit(cholesky)/cholesky | solution.py:51
  85.9 0.6 compare_reduce_fusion.1
  86.5 0.6 fusion.22
  87.2 1.2 %custom-call.6 = f32[1,16,16]{1,2,0:T(8,128)S(1)} custom-call(f32[1,16,16]{2,1,0:T(8,128)S(1)} %fusion.22), custom_call_target="InvertDiagBlocksLowerTriangular" | custom-call | tf_op jit(solution)/shard_map/triangular_solve/custom-call.0 | solution.py:55
  88.6 1.1 convolution_convert_fusion.1.refs_1_
  89.7 0.7 copy.21
  90.4 0.3 copy.28
  90.7 6.1 %shard_map.51 = (bf16[16,36864]{1,0:T(8,128)(2,1)S(1)}, f32[16,16]{1,0:T(8,128)S(1)}) custom-call(bf16[64,36864]{1,0:T(8,128)(2,1)} %bitcast.87, bf16[16,36864]{1,0:T(8,128)(2,1)S(1)} %convolution_convert_fusion.1.refs_1_, bf16[16,36864]{1,0:T(8,128)(2,1)S(1)} %bitcast.84), custom_call_target="tpu_custom_call" | custom-call | flops 207618048 | bytes 8258560 | tf_op jit(solution)/shard_map/pallas_call | solution.py:33
  96.9 1.5 %cholesky.55 = f32[16,16]{1,0:T(8,128)S(1)} custom-call(f32[16,16]{1,0:T(8,128)S(1)} %fusion.25), custom_call_target="Cholesky" | custom-call | tf_op jit(solution)/shard_map/jit(cholesky)/cholesky | solution.py:51
  98.4 0.6 compare_reduce_fusion
  99.0 0.6 fusion.23
  99.7 1.2 %custom-call.7 = f32[1,16,16]{1,2,0:T(8,128)S(1)} custom-call(f32[1,16,16]{2,1,0:T(8,128)S(1)} %fusion.23), custom_call_target="InvertDiagBlocksLowerTriangular" | custom-call | tf_op jit(solution)/shard_map/triangular_solve/custom-call.0 | solution.py:55
  101.1 1.1 fusion
  102.2 4.2 %all-to-all-done.2 = bf16[32,4,4608]{2,1,0:T(4,128)(2,1)} async-done(((bf16[32,4,4608]{2,1,0:T(4,128)(2,1)}), bf16[32,4,4608]{2,1,0:T(4,128)(2,1)}, u32[]{:S(2)}, u32[]{:S(2)}) %all-to-all-start.2) | async-done | bytes 1179680 | tf_op jit(solution)/shard_map/all_to_all | solution.py:59
  106.4 1.9 %copy.23 = bf16[8,4,4,4608]{3,0,2,1:T(8,128)(2,1)S(1)} copy(bf16[8,4,4,4608]{3,2,1,0:T(4,128)(2,1)} %bitcast.20) | data formatting | bytes 2359296 | tf_op jit(solution)/shard_map/reshape | solution.py:65
  108.6 3.7 %fusion.5 = f32[16,1,64]{2,0,1:T(8,128)S(1)} fusion(bf16[16,36864]{1,0:T(8,128)(2,1)S(1)} %bitcast.88, bf16[64,1,36864]{2,0,1:T(8,128)(2,1)} %param.6), kind=kOutput, calls=%fused_computation.12 | convolution fusion | flops 75498496 | bytes 5902336 | tf_op jit(solution)/shard_map/nbl,pbl->pbn/dot_general | solution.py:103
  112.3 0.6 fusion.15
  112.9 0.6 fusion.9
  113.6 1.6 %pad_maximum_fusion = bf16[2,16,1,36864]{3,1,2,0:T(8,128)(2,1)} fusion(bf16[1,16,1,36864]{3,1,2,0:T(8,128)(2,1)S(1)} %bitcast.91, bf16[1,16,1,36864]{3,1,2,0:T(8,128)(2,1)S(1)} %bitcast.83), kind=kLoop, calls=%fused_computation.3 | loop fusion | flops 1179648 | bytes 4718592 | tf_op jit(solution)/shard_map/stack | solution.py:98
  115.2 0.7 pad_maximum_fusion.1
  (11 shorter events, 1.0 us)
Async XLA Ops:
  4.4 36.4 %all-to-all-start = ((bf16[32,4,4608]{2,1,0:T(4,128)(2,1)}), bf16[32,4,4608]{2,1,0:T(4,128)(2,1)S(1)}, u32[]{:S(2)}, u32[]{:S(2)}) async-start(bf16[32,4,4608]{2,1,0:T(4,128)(2,1)} %bitcast.79), calls=%async_computation | async-start | bytes 2359296 | tf_op jit(solution)/shard_map/all_to_all | solution.py:59
  40.8 3.7 %copy-start = (bf16[4,32,4608]{2,1,0:T(8,128)(2,1)S(1)}, bf16[4,32,4608]{2,1,0:T(8,128)(2,1)}, u32[]{:S(2)}) copy-start(bf16[4,32,4608]{2,1,0:T(8,128)(2,1)} %param.8) | copy-start | bytes 3538948
  40.8 32.7 %all-to-all-start.1 = ((bf16[32,4,4608]{2,1,0:T(4,128)(2,1)}), bf16[32,4,4608]{2,1,0:T(4,128)(2,1)S(1)}, u32[]{:S(2)}, u32[]{:S(2)}) async-start(bf16[32,4,4608]{2,1,0:T(4,128)(2,1)} %bitcast.80), calls=%async_computation.1 | async-start | bytes 2359296 | tf_op jit(solution)/shard_map/all_to_all | solution.py:59
  73.5 32.8 %all-to-all-start.2 = ((bf16[32,4,4608]{2,1,0:T(4,128)(2,1)}), bf16[32,4,4608]{2,1,0:T(4,128)(2,1)}, u32[]{:S(2)}, u32[]{:S(2)}) async-start(bf16[32,4,4608]{2,1,0:T(4,128)(2,1)} %bitcast.81), calls=%async_computation.2 | async-start | bytes 2359296 | tf_op jit(solution)/shard_map/all_to_all | solution.py:59

commit v4 on v3

--- a/solution.py
+++ b/solution.py
@@ -45,6 +45,45 @@
             bytes_accessed=2 * block_len * (rows + 2 * count) + 4 * count * count,
         ),
     )(*pieces, vectors)
+
+
+def coarse_kernel(*refs, piece_count):
+    further_ref = refs[0]
+    basis_refs = refs[1:1 + piece_count]
+    out_refs = refs[1 + piece_count:]
+    for mode_index in range(further_ref.shape[1]):
+        vectors = further_ref[0, mode_index]
+        for basis_ref, out_ref in zip(basis_refs, out_refs):
+            out_ref[0, mode_index] = lax.dot_general(
+                vectors, basis_ref[...], NT, preferred_element_type=jnp.float32
+            )
+
+
+def coarse_call(further_parts, pieces):
+    lat_count, mode_count, vector_part, entry_part = further_parts.shape
+    rows = sum(p.shape[0] for p in pieces)
+    further_spec = pl.BlockSpec((1, mode_count, vector_part, entry_part), lambda l: (l, 0, 0, 0))
+    piece_specs = [pl.BlockSpec((p.shape[0], entry_part), lambda l: (0, l)) for p in pieces]
+    out_specs = [
+        pl.BlockSpec((1, mode_count, vector_part, p.shape[0]), lambda l: (l, 0, 0, 0)) for p in pieces
+    ]
+    out_shape = [
+        jax.ShapeDtypeStruct((lat_count, mode_count, vector_part, p.shape[0]), jnp.float32)
+        for p in pieces
+    ]
+    block_len = lat_count * entry_part
+    return pl.pallas_call(
+        functools.partial(coarse_kernel, piece_count=len(pieces)),
+        grid=(lat_count,),
+        out_shape=out_shape,
+        in_specs=[further_spec] + piece_specs,
+        out_specs=out_specs,
+        cost_estimate=pl.CostEstimate(
+            flops=2 * rows * mode_count * vector_part * block_len,
+            transcendentals=0,
+            bytes_accessed=2 * block_len * (rows + mode_count * vector_part),
+        ),
+    )(further_parts, *pieces)
 
 
 def factor_inverse(gram_matrix):
@@ -96,16 +135,12 @@
         finished.append(project(earlier, finished, vectors, block_len))
     finished, further_arrived = lax.optimization_barrier((finished, arrived[-1]))
     new_basis = jnp.stack(finished, 0)
-    further_blocks = arrange(further_arrived)
-    products = []
-    for basis_part in [earlier] + finished:
-        products.append(
-            jnp.einsum(
-                "nbl,pbl->pbn", basis_part, further_blocks, preferred_element_type=jnp.float32
-            )
-            / block_len
-        )
-    coarse = jnp.concatenate(products, axis=2)
+    further_parts = split_by_source(further_arrived)
+    pieces = [piece.reshape(piece.shape[0], block_len) for piece in [earlier] + finished]
+    partials = coarse_call(further_parts, pieces)
+    count = further_parts.shape[1] * further_parts.shape[2]
+    coarse = jnp.concatenate([partial.sum(0) for partial in partials], axis=-1)
+    coarse = (coarse / block_len).reshape(count, 1, -1)
     return (new_basis, coarse)
 
 

time: 116 us -> 124 us (1.069)
  Pallas kernels: 12.9 us -> 24.6 us
  matrix products: 7.48 us -> 3.58 us
  other arithmetic: 10.4 us -> 13 us
  local copies, waits for them, and re-layouts: 12 us -> 9.76 us
    pallas_call x0 -> x1, Pallas kernels: none -> 11.8 us  [coarse_call(): pl.pallas_call(functools.partial(coarse_kernel, piece_count=len(pieces)),...]
    dot_general x3 -> x0, matrix products: 4.92 us -> none  [per_device(): jnp.einsum('nbl,pbl->pbn', basis_part, further_blocks, preferred_element_...]
    reduce_sum x0 -> x3, other arithmetic: none -> 2.6 us  [per_device(): coarse = jnp.concatenate([partial.sum(0) for partial in partials], axis=-1)]
    reshape x3 -> x2, local copies, waits for them, and re-layouts: 3.22 us -> 1.3 us  [split_by_source(): received.reshape(lat_count, mode_count, received.shape[1], received.shape...]
    unnamed x8 -> x13, local copies, waits for them, and re-layouts: 6.81 us -> 6.48 us
  transfers between devices with their start and end apart: 3 -> 3, of which waited for: 3 -> 3; matrix products, arithmetic and copies ran while one was open for 14% -> 14% of each run, Pallas kernels for 11% -> 10%
where the time goes in v4:
time: 124 us; the launch traced here: 123 us
  waiting for transfers between devices  56.5 us (46%)
  Pallas kernels  24.6 us (20%)
  starting transfers between devices  14.9 us (12%)
  other arithmetic  13 us (10%)
  local copies, waits for them, and re-layouts  9.76 us (8%)
  matrix products  3.58 us (3%)
    all_to_all x3, waiting for transfers between devices, send(): lax.all_to_all(block_major, ('lat', 'mode'), split_axis=0, concat_axis=0,...  56.5 us
    all_to_all x3, starting transfers between devices, send(): lax.all_to_all(block_major, ('lat', 'mode'), split_axis=0, concat_axis=0,...  14.9 us
    pallas_call x2, Pallas kernels, project_call(): pl.pallas_call(functools.partial(project_kernel, piece_count=len(pieces),...  12.9 us
    pallas_call x1, Pallas kernels, coarse_call(): pl.pallas_call(functools.partial(coarse_kernel, piece_count=len(pieces)),...  11.8 us
    unnamed x13, local copies, waits for them, and re-layouts  6.48 us
    another operation x6, other arithmetic, factor_inverse(): lower_factor = jnp.linalg.cholesky(gram_matrix)  4.31 us
    another operation x4, other arithmetic, factor_inverse(): lax.linalg.triangular_solve(lower_factor, identity, left_side=True, lower...  3.75 us
    dot_general x2, matrix products, project(): jnp.dot(inverse, residual.astype(jnp.float32), precision=lax.Precision.HI...  3.17 us
  transfers between devices with their start and end apart: 3, of which 3 were waited for; matrix products, arithmetic and copies ran while one was open for 14% of the time, Pallas kernels for 10%

profile of v4, /device:TPU:0, one launch (start us, length us, event | category | flops | bytes accessed | tf_op | source)
XLA Modules:
  0.0 123.1 jit_solution(5526081983084599985)
XLA Ops:
  0.6 1.8 %fusion.11 = (bf16[1,4,32,4608]{3,2,1,0:T(8,128)(2,1)S(1)}, bf16[1,4,32,4608]{3,2,1,0:T(8,128)(2,1)S(1)}) fusion(bf16[2,4,32,4608]{3,2,1,0:T(8,128)(2,1)} %param.7), kind=kLoop, calls=%fused_computation.28 | loop fusion | bytes 4718592 | tf_op jit(solution)/shard_map/slice | solution.py:126
  2.5 1.9 %copy.24 = bf16[1,4,32,4608]{3,1,2,0:T(4,128)(2,1)} copy(bf16[1,4,32,4608]{3,2,1,0:T(8,128)(2,1)S(1)} %get-tuple-element.32) | data formatting | bytes 2359296
  4.4 7.3 %all-to-all-start = ((bf16[32,4,4608]{2,1,0:T(4,128)(2,1)}), bf16[32,4,4608]{2,1,0:T(4,128)(2,1)S(1)}, u32[]{:S(2)}, u32[]{:S(2)}) async-start(bf16[32,4,4608]{2,1,0:T(4,128)(2,1)} %bitcast.54), calls=%async_computation | async-start | bytes 2359296 | tf_op jit(solution)/shard_map/all_to_all | solution.py:98
  11.7 1.9 %copy.25 = bf16[1,4,32,4608]{3,1,2,0:T(4,128)(2,1)} copy(bf16[1,4,32,4608]{3,2,1,0:T(8,128)(2,1)S(1)} %get-tuple-element.33) | data formatting | bytes 2359296
  13.6 27.2 %all-to-all-done = bf16[32,4,4608]{2,1,0:T(4,128)(2,1)S(1)} async-done(((bf16[32,4,4608]{2,1,0:T(4,128)(2,1)}), bf16[32,4,4608]{2,1,0:T(4,128)(2,1)S(1)}, u32[]{:S(2)}, u32[]{:S(2)}) %all-to-all-start) | async-done | bytes 1179680 | tf_op jit(solution)/shard_map/all_to_all | solution.py:98
  40.8 3.7 %all-to-all-start.1 = ((bf16[32,4,4608]{2,1,0:T(4,128)(2,1)}), bf16[32,4,4608]{2,1,0:T(4,128)(2,1)S(1)}, u32[]{:S(2)}, u32[]{:S(2)}) async-start(bf16[32,4,4608]{2,1,0:T(4,128)(2,1)} %bitcast.55), calls=%async_computation.1 | async-start | bytes 2359296 | tf_op jit(solution)/shard_map/all_to_all | solution.py:98
  44.4 1.9 %copy.26 = bf16[4,32,4608]{2,0,1:T(4,128)(2,1)} copy(bf16[4,32,4608]{2,1,0:T(8,128)(2,1)S(1)} %copy-done.3) | data formatting | bytes 2359296 | tf_op args[2]
  46.4 0.7 copy.12
  47.0 0.3 copy.19
  47.4 26.1 %all-to-all-done.1 = bf16[32,4,4608]{2,1,0:T(4,128)(2,1)S(1)} async-done(((bf16[32,4,4608]{2,1,0:T(4,128)(2,1)}), bf16[32,4,4608]{2,1,0:T(4,128)(2,1)S(1)}, u32[]{:S(2)}, u32[]{:S(2)}) %all-to-all-start.1) | async-done | bytes 1179680 | tf_op jit(solution)/shard_map/all_to_all | solution.py:98
  73.5 3.9 %all-to-all-start.2 = ((bf16[32,4,4608]{2,1,0:T(4,128)(2,1)}), bf16[32,4,4608]{2,1,0:T(4,128)(2,1)}, u32[]{:S(2)}, u32[]{:S(2)}) async-start(bf16[32,4,4608]{2,1,0:T(4,128)(2,1)} %bitcast.56), calls=%async_computation.2 | async-start | bytes 2359296 | tf_op jit(solution)/shard_map/all_to_all | solution.py:98
  77.5 6.8 %shard_map.50 = (bf16[16,36864]{1,0:T(8,128)(2,1)S(1)}, f32[16,16]{1,0:T(8,128)S(1)}) custom-call(bf16[64,36864]{1,0:T(8,128)(2,1)} %bitcast.60, bf16[16,36864]{1,0:T(8,128)(2,1)S(1)} %bitcast.59), custom_call_target="tpu_custom_call" | custom-call | flops 169869312 | bytes 7078912 | tf_op jit(solution)/shard_map/pallas_call | solution.py:33
  84.4 1.5 %cholesky.44 = f32[16,16]{1,0:T(8,128)S(1)} custom-call(f32[16,16]{1,0:T(8,128)S(1)} %fusion.10), custom_call_target="Cholesky" | custom-call | tf_op jit(solution)/shard_map/jit(cholesky)/cholesky | solution.py:90
  85.9 0.6 compare_reduce_fusion.1
  86.5 0.6 fusion.5
  87.2 1.2 custom-call.6
  88.6 1.1 convolution_convert_fusion.1.refs_1_
  89.7 0.7 copy.15
  90.4 0.3 copy.20
  90.7 6.1 %shard_map.51 = (bf16[16,36864]{1,0:T(8,128)(2,1)S(1)}, f32[16,16]{1,0:T(8,128)S(1)}) custom-call(bf16[64,36864]{1,0:T(8,128)(2,1)} %bitcast.61, bf16[16,36864]{1,0:T(8,128)(2,1)S(1)} %convolution_convert_fusion.1.refs_1_, bf16[16,36864]{1,0:T(8,128)(2,1)S(1)} %bitcast.58), custom_call_target="tpu_custom_call" | custom-call | flops 207618048 | bytes 8258560 | tf_op jit(solution)/shard_map/pallas_call | solution.py:33
  96.9 1.5 %cholesky.55 = f32[16,16]{1,0:T(8,128)S(1)} custom-call(f32[16,16]{1,0:T(8,128)S(1)} %fusion.8), custom_call_target="Cholesky" | custom-call | tf_op jit(solution)/shard_map/jit(cholesky)/cholesky | solution.py:90
  98.4 0.6 compare_reduce_fusion
  99.0 0.6 fusion.6
  99.7 1.2 custom-call.7
  101.1 2.1 %fusion = bf16[16,1,36864]{2,0,1:T(8,128)(2,1)} fusion(f32[16,16]{1,0:T(8,128)S(1)} %fusion.1, bf16[16,36864]{1,0:T(8,128)(2,1)S(1)} %get-tuple-element.24), kind=kOutput, calls=%fused_computation.2 | convolution fusion | flops 113836032 | bytes 2360320 | tf_op jit(solution)/shard_map/dot_general | solution.py:119
  103.2 3.2 %all-to-all-done.2 = bf16[32,4,4608]{2,1,0:T(4,128)(2,1)} async-done(((bf16[32,4,4608]{2,1,0:T(4,128)(2,1)}), bf16[32,4,4608]{2,1,0:T(4,128)(2,1)}, u32[]{:S(2)}, u32[]{:S(2)}) %all-to-all-start.2) | async-done | bytes 1179680 | tf_op jit(solution)/shard_map/all_to_all | solution.py:98
  106.4 11.8 %shard_map.52 = (f32[8,4,4,64]{3,2,1,0:T(4,128)}, f32[8,4,4,16]{3,2,1,0:T(4,128)}, f32[8,4,4,16]{3,2,1,0:T(4,128)}) custom-call(bf16[8,4,4,4608]{3,2,1,0:T(4,128)(2,1)} %bitcast.20.refs_0_, bf16[64,36864]{1,0:T(8,128)(2,1)} %bitcast.62, bf16[16,36864]{1,0:T(8,128)(2,1)} %copy-done, bf16[16,36864]{1,0:T(8,128)(2,1)} %bitcast.63), custom_call_target="tpu_custom_call" | custom-call | flops 113246208 | bytes 8257536 | tf_op jit(solution)/shard_map/pallas_call | solution.py:75
  118.1 0.9 reduce_sum.27
  119.0 0.9 reduce_sum.28
  119.9 0.9 reduce_sum.29
  120.7 1.6 %pad_maximum_fusion = bf16[2,16,1,36864]{3,1,2,0:T(8,128)(2,1)} fusion(bf16[1,16,1,36864]{3,1,2,0:T(8,128)(2,1)S(1)} %bitcast.64, bf16[1,16,1,36864]{3,1,2,0:T(8,128)(2,1)S(1)} %bitcast.57), kind=kLoop, calls=%fused_computation.3 | loop fusion | flops 1179648 | bytes 4718592 | tf_op jit(solution)/shard_map/stack | solution.py:137
  122.4 0.7 maximum_multiply_fusion
  (16 shorter events, 0.6 us)
Async XLA Ops:
  4.4 36.4 %all-to-all-start = ((bf16[32,4,4608]{2,1,0:T(4,128)(2,1)}), bf16[32,4,4608]{2,1,0:T(4,128)(2,1)S(1)}, u32[]{:S(2)}, u32[]{:S(2)}) async-start(bf16[32,4,4608]{2,1,0:T(4,128)(2,1)} %bitcast.54), calls=%async_computation | async-start | bytes 2359296 | tf_op jit(solution)/shard_map/all_to_all | solution.py:98
  40.8 3.7 %copy-start.3 = (bf16[4,32,4608]{2,1,0:T(8,128)(2,1)S(1)}, bf16[4,32,4608]{2,1,0:T(8,128)(2,1)}, u32[]{:S(2)}) copy-start(bf16[4,32,4608]{2,1,0:T(8,128)(2,1)} %param.8) | copy-start | bytes 3538948
  40.8 32.7 %all-to-all-start.1 = ((bf16[32,4,4608]{2,1,0:T(4,128)(2,1)}), bf16[32,4,4608]{2,1,0:T(4,128)(2,1)S(1)}, u32[]{:S(2)}, u32[]{:S(2)}) async-start(bf16[32,4,4608]{2,1,0:T(4,128)(2,1)} %bitcast.55), calls=%async_computation.1 | async-start | bytes 2359296 | tf_op jit(solution)/shard_map/all_to_all | solution.py:98
  73.5 32.8 %all-to-all-start.2 = ((bf16[32,4,4608]{2,1,0:T(4,128)(2,1)}), bf16[32,4,4608]{2,1,0:T(4,128)(2,1)}, u32[]{:S(2)}, u32[]{:S(2)}) async-start(bf16[32,4,4608]{2,1,0:T(4,128)(2,1)} %bitcast.56), calls=%async_computation.2 | async-start | bytes 2359296 | tf_op jit(solution)/shard_map/all_to_all | solution.py:98
  89.7 1.0 copy-start
  106.4 14.4 %copy-start.1 = (bf16[16,36864]{1,0:T(8,128)(2,1)S(1)}, bf16[16,36864]{1,0:T(8,128)(2,1)}, u32[]{:S(2)}) copy-start(bf16[16,36864]{1,0:T(8,128)(2,1)} %copy-done) | copy-start | bytes 3538948
  106.4 14.4 %copy-start.2 = (bf16[16,1,36864]{2,0,1:T(8,128)(2,1)S(1)}, bf16[16,1,36864]{2,0,1:T(8,128)(2,1)}, u32[]{:S(2)}) copy-start(bf16[16,1,36864]{2,0,1:T(8,128)(2,1)} %fusion) | copy-start | bytes 3538948

commit v5 on v3

--- a/solution.py
+++ b/solution.py
@@ -88,14 +88,14 @@
     outgoing.append(further.transpose(1, 0, 2))
     arrived = [send(outgoing[0])]
     for index in range(1, len(outgoing)):
-        ready, arrived[-1] = lax.optimization_barrier((outgoing[index], arrived[-1]))
+        ready, arrived[0] = lax.optimization_barrier((outgoing[index], arrived[0]))
         arrived.append(send(ready))
     finished = []
     for panel_index in range(panel_count):
         vectors = arrange(arrived[panel_index])
         finished.append(project(earlier, finished, vectors, block_len))
+    new_basis = jnp.stack(finished, 0)
     finished, further_arrived = lax.optimization_barrier((finished, arrived[-1]))
-    new_basis = jnp.stack(finished, 0)
     further_blocks = arrange(further_arrived)
     products = []
     for basis_part in [earlier] + finished:

time: 116 us -> 116 us (level)
  no operation moved by 1% of the time
where the time goes in v5:
time: 116 us
  waiting for transfers between devices  57.5 us (50%)
  starting transfers between devices  14.9 us (13%)
  Pallas kernels  12.9 us (11%)
  local copies, waits for them, and re-layouts  12 us (10%)
  other arithmetic  10.3 us (9%)
  matrix products  7.48 us (6%)
    all_to_all x3, waiting for transfers between devices, send(): lax.all_to_all(block_major, ('lat', 'mode'), split_axis=0, concat_axis=0,...  57.5 us
    all_to_all x3, starting transfers between devices, send(): lax.all_to_all(block_major, ('lat', 'mode'), split_axis=0, concat_axis=0,...  14.9 us
    pallas_call x2, Pallas kernels, project_call(): pl.pallas_call(functools.partial(project_kernel, piece_count=len(pieces),...  12.9 us
    unnamed x8, local copies, waits for them, and re-layouts  6.81 us
    dot_general x3, matrix products, per_device(): jnp.einsum('nbl,pbl->pbn', basis_part, further_blocks, preferred_element_...  4.92 us
    another operation x6, other arithmetic, factor_inverse(): lower_factor = jnp.linalg.cholesky(gram_matrix)  4.26 us
    another operation x4, other arithmetic, factor_inverse(): lax.linalg.triangular_solve(lower_factor, identity, left_side=True, lower...  3.75 us
    reshape x3, local copies, waits for them, and re-layouts, split_by_source(): received.reshape(lat_count, mode_count, received.shape[1], received.shape...  3.22 us
  transfers between devices with their start and end apart: 3, of which 3 were waited for; matrix products, arithmetic and copies ran while one was open for 14% of the time, Pallas kernels for 11%

profile of v5, /device:TPU:0, one launch (start us, length us, event | category | flops | bytes accessed | tf_op | source)
XLA Modules:
  0.0 115.9 jit_solution(12785197830078878279)
XLA Ops:
  0.6 1.8 %fusion.28 = (bf16[1,4,32,4608]{3,2,1,0:T(8,128)(2,1)S(1)}, bf16[1,4,32,4608]{3,2,1,0:T(8,128)(2,1)S(1)}) fusion(bf16[2,4,32,4608]{3,2,1,0:T(8,128)(2,1)} %param.7), kind=kLoop, calls=%fused_computation.38 | loop fusion | bytes 4718592 | tf_op jit(solution)/shard_map/slice | solution.py:87
  2.5 1.9 %copy.33 = bf16[1,4,32,4608]{3,1,2,0:T(4,128)(2,1)} copy(bf16[1,4,32,4608]{3,2,1,0:T(8,128)(2,1)S(1)} %get-tuple-element.32) | data formatting | bytes 2359296
  4.4 7.3 %all-to-all-start = ((bf16[32,4,4608]{2,1,0:T(4,128)(2,1)}), bf16[32,4,4608]{2,1,0:T(4,128)(2,1)S(1)}, u32[]{:S(2)}, u32[]{:S(2)}) async-start(bf16[32,4,4608]{2,1,0:T(4,128)(2,1)} %bitcast.78), calls=%async_computation | async-start | bytes 2359296 | tf_op jit(solution)/shard_map/all_to_all | solution.py:59
  11.7 1.9 %copy.34 = bf16[1,4,32,4608]{3,1,2,0:T(4,128)(2,1)} copy(bf16[1,4,32,4608]{3,2,1,0:T(8,128)(2,1)S(1)} %get-tuple-element.33) | data formatting | bytes 2359296
  13.6 27.2 %all-to-all-done = bf16[32,4,4608]{2,1,0:T(4,128)(2,1)S(1)} async-done(((bf16[32,4,4608]{2,1,0:T(4,128)(2,1)}), bf16[32,4,4608]{2,1,0:T(4,128)(2,1)S(1)}, u32[]{:S(2)}, u32[]{:S(2)}) %all-to-all-start) | async-done | bytes 1179680 | tf_op jit(solution)/shard_map/all_to_all | solution.py:59
  40.8 3.7 %all-to-all-start.1 = ((bf16[32,4,4608]{2,1,0:T(4,128)(2,1)}), bf16[32,4,4608]{2,1,0:T(4,128)(2,1)S(1)}, u32[]{:S(2)}, u32[]{:S(2)}) async-start(bf16[32,4,4608]{2,1,0:T(4,128)(2,1)} %bitcast.79), calls=%async_computation.1 | async-start | bytes 2359296 | tf_op jit(solution)/shard_map/all_to_all | solution.py:59
  44.4 1.9 %copy.35 = bf16[4,32,4608]{2,0,1:T(4,128)(2,1)} copy(bf16[4,32,4608]{2,1,0:T(8,128)(2,1)S(1)} %copy-done) | data formatting | bytes 2359296 | tf_op args[2]
  46.4 0.7 copy.19
  47.0 0.3 copy.27
  47.4 6.8 %shard_map.50 = (bf16[16,36864]{1,0:T(8,128)(2,1)S(1)}, f32[16,16]{1,0:T(8,128)S(1)}) custom-call(bf16[64,36864]{1,0:T(8,128)(2,1)} %bitcast.85, bf16[16,36864]{1,0:T(8,128)(2,1)S(1)} %bitcast.84), custom_call_target="tpu_custom_call" | custom-call | flops 169869312 | bytes 7078912 | tf_op jit(solution)/shard_map/pallas_call | solution.py:33
  54.3 19.3 %all-to-all-done.1 = bf16[32,4,4608]{2,1,0:T(4,128)(2,1)S(1)} async-done(((bf16[32,4,4608]{2,1,0:T(4,128)(2,1)}), bf16[32,4,4608]{2,1,0:T(4,128)(2,1)S(1)}, u32[]{:S(2)}, u32[]{:S(2)}) %all-to-all-start.1) | async-done | bytes 1179680 | tf_op jit(solution)/shard_map/all_to_all | solution.py:59
  73.5 3.9 %all-to-all-start.2 = ((bf16[32,4,4608]{2,1,0:T(4,128)(2,1)}), bf16[32,4,4608]{2,1,0:T(4,128)(2,1)}, u32[]{:S(2)}, u32[]{:S(2)}) async-start(bf16[32,4,4608]{2,1,0:T(4,128)(2,1)} %bitcast.80), calls=%async_computation.2 | async-start | bytes 2359296 | tf_op jit(solution)/shard_map/all_to_all | solution.py:59
  77.5 1.4 %cholesky.44 = f32[16,16]{1,0:T(8,128)S(1)} custom-call(f32[16,16]{1,0:T(8,128)S(1)} %fusion.26), custom_call_target="Cholesky" | custom-call | tf_op jit(solution)/shard_map/jit(cholesky)/cholesky | solution.py:51
  79.0 0.6 compare_reduce_fusion.1
  79.6 0.6 fusion.21
  80.3 1.2 %custom-call.6 = f32[1,16,16]{1,2,0:T(8,128)S(1)} custom-call(f32[1,16,16]{2,1,0:T(8,128)S(1)} %fusion.21), custom_call_target="InvertDiagBlocksLowerTriangular" | custom-call | tf_op jit(solution)/shard_map/triangular_solve/custom-call.0 | solution.py:55
  81.7 1.1 convolution_convert_fusion.1.refs_1_
  82.8 0.7 copy.21
  83.8 6.1 %shard_map.51 = (bf16[16,36864]{1,0:T(8,128)(2,1)S(1)}, f32[16,16]{1,0:T(8,128)S(1)}) custom-call(bf16[64,36864]{1,0:T(8,128)(2,1)} %bitcast.86, bf16[16,36864]{1,0:T(8,128)(2,1)S(1)} %convolution_convert_fusion.1.refs_1_, bf16[16,36864]{1,0:T(8,128)(2,1)S(1)} %bitcast.83), custom_call_target="tpu_custom_call" | custom-call | flops 207618048 | bytes 8258560 | tf_op jit(solution)/shard_map/pallas_call | solution.py:33
  89.9 1.5 %cholesky.55 = f32[16,16]{1,0:T(8,128)S(1)} custom-call(f32[16,16]{1,0:T(8,128)S(1)} %fusion.24), custom_call_target="Cholesky" | custom-call | tf_op jit(solution)/shard_map/jit(cholesky)/cholesky | solution.py:51
  91.4 0.6 compare_reduce_fusion
  92.1 0.6 fusion.22
  92.7 1.2 %custom-call.7 = f32[1,16,16]{1,2,0:T(8,128)S(1)} custom-call(f32[1,16,16]{2,1,0:T(8,128)S(1)} %fusion.22), custom_call_target="InvertDiagBlocksLowerTriangular" | custom-call | tf_op jit(solution)/shard_map/triangular_solve/custom-call.0 | solution.py:55
  94.2 1.1 convolution_convert_fusion
  95.3 11.1 %all-to-all-done.2 = bf16[32,4,4608]{2,1,0:T(4,128)(2,1)} async-done(((bf16[32,4,4608]{2,1,0:T(4,128)(2,1)}), bf16[32,4,4608]{2,1,0:T(4,128)(2,1)}, u32[]{:S(2)}, u32[]{:S(2)}) %all-to-all-start.2) | async-done | bytes 1179680 | tf_op jit(solution)/shard_map/all_to_all | solution.py:59
  106.4 1.9 %copy.23 = bf16[8,4,4,4608]{3,0,2,1:T(8,128)(2,1)S(1)} copy(bf16[8,4,4,4608]{3,2,1,0:T(4,128)(2,1)} %bitcast.20) | data formatting | bytes 2359296 | tf_op jit(solution)/shard_map/reshape | solution.py:65
  108.3 0.3 copy.29
  108.6 3.7 %fusion.4 = f32[16,1,64]{2,0,1:T(8,128)S(1)} fusion(bf16[16,36864]{1,0:T(8,128)(2,1)S(1)} %bitcast.87, bf16[64,1,36864]{2,0,1:T(8,128)(2,1)} %param.6), kind=kOutput, calls=%fused_computation.11 | convolution fusion | flops 75498496 | bytes 5902336 | tf_op jit(solution)/shard_map/nbl,pbl->pbn/dot_general | solution.py:103
  112.3 0.6 fusion.14
  112.9 0.6 fusion.8
  113.6 1.6 %pad_maximum_fusion = bf16[2,16,1,36864]{3,1,2,0:T(8,128)(2,1)} fusion(bf16[1,16,1,36864]{3,1,2,0:T(8,128)(2,1)S(1)} %bitcast.91, bf16[1,16,1,36864]{3,1,2,0:T(8,128)(2,1)S(1)} %bitcast.82), kind=kLoop, calls=%fused_computation.2 | loop fusion | flops 1179648 | bytes 4718592 | tf_op jit(solution)/shard_map/stack | solution.py:97
  115.2 0.7 pad_maximum_fusion.1
  (11 shorter events, 1.0 us)
Async XLA Ops:
  4.4 36.4 %all-to-all-start = ((bf16[32,4,4608]{2,1,0:T(4,128)(2,1)}), bf16[32,4,4608]{2,1,0:T(4,128)(2,1)S(1)}, u32[]{:S(2)}, u32[]{:S(2)}) async-start(bf16[32,4,4608]{2,1,0:T(4,128)(2,1)} %bitcast.78), calls=%async_computation | async-start | bytes 2359296 | tf_op jit(solution)/shard_map/all_to_all | solution.py:59
  40.8 3.7 %copy-start = (bf16[4,32,4608]{2,1,0:T(8,128)(2,1)S(1)}, bf16[4,32,4608]{2,1,0:T(8,128)(2,1)}, u32[]{:S(2)}) copy-start(bf16[4,32,4608]{2,1,0:T(8,128)(2,1)} %param.8) | copy-start | bytes 3538948
  40.8 32.7 %all-to-all-start.1 = ((bf16[32,4,4608]{2,1,0:T(4,128)(2,1)}), bf16[32,4,4608]{2,1,0:T(4,128)(2,1)S(1)}, u32[]{:S(2)}, u32[]{:S(2)}) async-start(bf16[32,4,4608]{2,1,0:T(4,128)(2,1)} %bitcast.79), calls=%async_computation.1 | async-start | bytes 2359296 | tf_op jit(solution)/shard_map/all_to_all | solution.py:59
  73.5 32.8 %all-to-all-start.2 = ((bf16[32,4,4608]{2,1,0:T(4,128)(2,1)}), bf16[32,4,4608]{2,1,0:T(4,128)(2,1)}, u32[]{:S(2)}, u32[]{:S(2)}) async-start(bf16[32,4,4608]{2,1,0:T(4,128)(2,1)} %bitcast.80), calls=%async_computation.2 | async-start | bytes 2359296 | tf_op jit(solution)/shard_map/all_to_all | solution.py:59

commit v6 on v5

--- a/solution.py
+++ b/solution.py
@@ -95,7 +95,7 @@
         vectors = arrange(arrived[panel_index])
         finished.append(project(earlier, finished, vectors, block_len))
     new_basis = jnp.stack(finished, 0)
-    finished, further_arrived = lax.optimization_barrier((finished, arrived[-1]))
+    new_basis, finished, further_arrived = lax.optimization_barrier((new_basis, finished, arrived[-1]))
     further_blocks = arrange(further_arrived)
     products = []
     for basis_part in [earlier] + finished:

time: 116 us -> 115 us (level)
  waiting for transfers between devices: 57.5 us -> 55.8 us
    all_to_all x3, waiting for transfers between devices: 57.5 us -> 55.8 us  [send(): lax.all_to_all(block_major, ('lat', 'mode'), split_axis=0, concat_axis=0,...]
  transfers between devices with their start and end apart: 3 -> 3, of which waited for: 3 -> 3; matrix products, arithmetic and copies ran while one was open for 14% -> 16% of each run, Pallas kernels for 11% -> 11%
where the time goes in v6:
time: 115 us; the launch traced here: 114 us
  waiting for transfers between devices  55.8 us (49%)
  starting transfers between devices  14.9 us (13%)
  Pallas kernels  12.9 us (11%)
  local copies, waits for them, and re-layouts  12 us (10%)
  other arithmetic  10.4 us (9%)
  matrix products  7.48 us (7%)
    all_to_all x3, waiting for transfers between devices, send(): lax.all_to_all(block_major, ('lat', 'mode'), split_axis=0, concat_axis=0,...  55.8 us
    all_to_all x3, starting transfers between devices, send(): lax.all_to_all(block_major, ('lat', 'mode'), split_axis=0, concat_axis=0,...  14.9 us
    pallas_call x2, Pallas kernels, project_call(): pl.pallas_call(functools.partial(project_kernel, piece_count=len(pieces),...  12.9 us
    unnamed x8, local copies, waits for them, and re-layouts  6.85 us
    dot_general x3, matrix products, per_device(): jnp.einsum('nbl,pbl->pbn', basis_part, further_blocks, preferred_element_...  4.92 us
    another operation x6, other arithmetic, factor_inverse(): lower_factor = jnp.linalg.cholesky(gram_matrix)  4.31 us
    another operation x4, other arithmetic, factor_inverse(): lax.linalg.triangular_solve(lower_factor, identity, left_side=True, lower...  3.75 us
    reshape x3, local copies, waits for them, and re-layouts, split_by_source(): received.reshape(lat_count, mode_count, received.shape[1], received.shape...  3.22 us
  transfers between devices with their start and end apart: 3, of which 3 were waited for; matrix products, arithmetic and copies ran while one was open for 16% of the time, Pallas kernels for 11%

profile of v6, /device:TPU:0, one launch (start us, length us, event | category | flops | bytes accessed | tf_op | source)
XLA Modules:
  0.0 114.3 jit_solution(943629056300046958)
XLA Ops:
  0.6 1.8 %fusion.28 = (bf16[1,4,32,4608]{3,2,1,0:T(8,128)(2,1)S(1)}, bf16[1,4,32,4608]{3,2,1,0:T(8,128)(2,1)S(1)}) fusion(bf16[2,4,32,4608]{3,2,1,0:T(8,128)(2,1)} %param.7), kind=kLoop, calls=%fused_computation.38 | loop fusion | bytes 4718592 | tf_op jit(solution)/shard_map/slice | solution.py:87
  2.5 1.9 %copy.33 = bf16[1,4,32,4608]{3,1,2,0:T(4,128)(2,1)} copy(bf16[1,4,32,4608]{3,2,1,0:T(8,128)(2,1)S(1)} %get-tuple-element.34) | data formatting | bytes 2359296
  4.4 7.3 %all-to-all-start = ((bf16[32,4,4608]{2,1,0:T(4,128)(2,1)}), bf16[32,4,4608]{2,1,0:T(4,128)(2,1)S(1)}, u32[]{:S(2)}, u32[]{:S(2)}) async-start(bf16[32,4,4608]{2,1,0:T(4,128)(2,1)} %bitcast.78), calls=%async_computation | async-start | bytes 2359296 | tf_op jit(solution)/shard_map/all_to_all | solution.py:59
  11.7 2.0 %copy.34 = bf16[1,4,32,4608]{3,1,2,0:T(4,128)(2,1)} copy(bf16[1,4,32,4608]{3,2,1,0:T(8,128)(2,1)S(1)} %get-tuple-element.35) | data formatting | bytes 2359296
  13.7 27.1 %all-to-all-done = bf16[32,4,4608]{2,1,0:T(4,128)(2,1)S(1)} async-done(((bf16[32,4,4608]{2,1,0:T(4,128)(2,1)}), bf16[32,4,4608]{2,1,0:T(4,128)(2,1)S(1)}, u32[]{:S(2)}, u32[]{:S(2)}) %all-to-all-start) | async-done | bytes 1179680 | tf_op jit(solution)/shard_map/all_to_all | solution.py:59
  40.8 3.7 %all-to-all-start.1 = ((bf16[32,4,4608]{2,1,0:T(4,128)(2,1)}), bf16[32,4,4608]{2,1,0:T(4,128)(2,1)S(1)}, u32[]{:S(2)}, u32[]{:S(2)}) async-start(bf16[32,4,4608]{2,1,0:T(4,128)(2,1)} %bitcast.79), calls=%async_computation.1 | async-start | bytes 2359296 | tf_op jit(solution)/shard_map/all_to_all | solution.py:59
  44.4 1.9 %copy.35 = bf16[4,32,4608]{2,0,1:T(4,128)(2,1)} copy(bf16[4,32,4608]{2,1,0:T(8,128)(2,1)S(1)} %copy-done) | data formatting | bytes 2359296 | tf_op args[2]
  46.4 0.7 copy.19
  47.0 0.3 copy.27
  47.4 6.8 %shard_map.50 = (bf16[16,36864]{1,0:T(8,128)(2,1)S(1)}, f32[16,16]{1,0:T(8,128)S(1)}) custom-call(bf16[64,36864]{1,0:T(8,128)(2,1)} %bitcast.85, bf16[16,36864]{1,0:T(8,128)(2,1)S(1)} %bitcast.84), custom_call_target="tpu_custom_call" | custom-call | flops 169869312 | bytes 7078912 | tf_op jit(solution)/shard_map/pallas_call | solution.py:33
  54.3 1.5 %cholesky.44 = f32[16,16]{1,0:T(8,128)S(1)} custom-call(f32[16,16]{1,0:T(8,128)S(1)} %fusion.26), custom_call_target="Cholesky" | custom-call | tf_op jit(solution)/shard_map/jit(cholesky)/cholesky | solution.py:51
  55.8 0.6 compare_reduce_fusion.1
  56.4 0.6 fusion.21
  57.1 1.2 %custom-call.6 = f32[1,16,16]{1,2,0:T(8,128)S(1)} custom-call(f32[1,16,16]{2,1,0:T(8,128)S(1)} %fusion.21), custom_call_target="InvertDiagBlocksLowerTriangular" | custom-call | tf_op jit(solution)/shard_map/triangular_solve/custom-call.0 | solution.py:55
  58.5 1.1 convolution_convert_fusion.1.refs_1_
  59.6 13.9 %all-to-all-done.1 = bf16[32,4,4608]{2,1,0:T(4,128)(2,1)S(1)} async-done(((bf16[32,4,4608]{2,1,0:T(4,128)(2,1)}), bf16[32,4,4608]{2,1,0:T(4,128)(2,1)S(1)}, u32[]{:S(2)}, u32[]{:S(2)}) %all-to-all-start.1) | async-done | bytes 1179680 | tf_op jit(solution)/shard_map/all_to_all | solution.py:59
  73.5 3.9 %all-to-all-start.2 = ((bf16[32,4,4608]{2,1,0:T(4,128)(2,1)}), bf16[32,4,4608]{2,1,0:T(4,128)(2,1)}, u32[]{:S(2)}, u32[]{:S(2)}) async-start(bf16[32,4,4608]{2,1,0:T(4,128)(2,1)} %bitcast.80), calls=%async_computation.2 | async-start | bytes 2359296 | tf_op jit(solution)/shard_map/all_to_all | solution.py:59
  77.5 0.7 copy.21
  78.1 0.3 copy.28
  78.5 6.1 %shard_map.51 = (bf16[16,36864]{1,0:T(8,128)(2,1)S(1)}, f32[16,16]{1,0:T(8,128)S(1)}) custom-call(bf16[64,36864]{1,0:T(8,128)(2,1)} %bitcast.86, bf16[16,36864]{1,0:T(8,128)(2,1)S(1)} %convolution_convert_fusion.1.refs_1_, bf16[16,36864]{1,0:T(8,128)(2,1)S(1)} %bitcast.83), custom_call_target="tpu_custom_call" | custom-call | flops 207618048 | bytes 8258560 | tf_op jit(solution)/shard_map/pallas_call | solution.py:33
  84.6 1.5 %cholesky.55 = f32[16,16]{1,0:T(8,128)S(1)} custom-call(f32[16,16]{1,0:T(8,128)S(1)} %fusion.24), custom_call_target="Cholesky" | custom-call | tf_op jit(solution)/shard_map/jit(cholesky)/cholesky | solution.py:51
  86.1 0.6 compare_reduce_fusion
  86.8 0.6 fusion.22
  87.4 1.2 %custom-call.7 = f32[1,16,16]{1,2,0:T(8,128)S(1)} custom-call(f32[1,16,16]{2,1,0:T(8,128)S(1)} %fusion.22), custom_call_target="InvertDiagBlocksLowerTriangular" | custom-call | tf_op jit(solution)/shard_map/triangular_solve/custom-call.0 | solution.py:55
  88.9 1.1 convolution_convert_fusion
  89.9 1.6 %pad_maximum_fusion = bf16[2,16,1,36864]{3,1,2,0:T(8,128)(2,1)} fusion(bf16[1,16,1,36864]{3,1,2,0:T(8,128)(2,1)S(1)} %bitcast.90, bf16[1,16,1,36864]{3,1,2,0:T(8,128)(2,1)S(1)} %bitcast.81), kind=kLoop, calls=%fused_computation.2 | loop fusion | flops 1179648 | bytes 4718592 | tf_op jit(solution)/shard_map/stack | solution.py:97
  91.6 14.8 %all-to-all-done.2 = bf16[32,4,4608]{2,1,0:T(4,128)(2,1)} async-done(((bf16[32,4,4608]{2,1,0:T(4,128)(2,1)}), bf16[32,4,4608]{2,1,0:T(4,128)(2,1)}, u32[]{:S(2)}, u32[]{:S(2)}) %all-to-all-start.2) | async-done | bytes 1179680 | tf_op jit(solution)/shard_map/all_to_all | solution.py:59
  106.4 1.9 %copy.23 = bf16[8,4,4,4608]{3,0,2,1:T(8,128)(2,1)S(1)} copy(bf16[8,4,4,4608]{3,2,1,0:T(4,128)(2,1)} %bitcast.20) | data formatting | bytes 2359296 | tf_op jit(solution)/shard_map/reshape | solution.py:65
  108.6 3.7 %fusion.4 = f32[16,1,64]{2,0,1:T(8,128)S(1)} fusion(bf16[16,36864]{1,0:T(8,128)(2,1)S(1)} %bitcast.87, bf16[64,1,36864]{2,0,1:T(8,128)(2,1)} %param.6), kind=kOutput, calls=%fused_computation.11 | convolution fusion | flops 75498496 | bytes 5902336 | tf_op jit(solution)/shard_map/nbl,pbl->pbn/dot_general | solution.py:103
  112.3 0.6 fusion.14
  112.9 0.6 fusion.8
  113.6 0.7 pad_maximum_fusion.1
  (11 shorter events, 1.0 us)
Async XLA Ops:
  4.4 36.4 %all-to-all-start = ((bf16[32,4,4608]{2,1,0:T(4,128)(2,1)}), bf16[32,4,4608]{2,1,0:T(4,128)(2,1)S(1)}, u32[]{:S(2)}, u32[]{:S(2)}) async-start(bf16[32,4,4608]{2,1,0:T(4,128)(2,1)} %bitcast.78), calls=%async_computation | async-start | bytes 2359296 | tf_op jit(solution)/shard_map/all_to_all | solution.py:59
  40.8 3.7 %copy-start = (bf16[4,32,4608]{2,1,0:T(8,128)(2,1)S(1)}, bf16[4,32,4608]{2,1,0:T(8,128)(2,1)}, u32[]{:S(2)}) copy-start(bf16[4,32,4608]{2,1,0:T(8,128)(2,1)} %param.8) | copy-start | bytes 3538948
  40.8 32.7 %all-to-all-start.1 = ((bf16[32,4,4608]{2,1,0:T(4,128)(2,1)}), bf16[32,4,4608]{2,1,0:T(4,128)(2,1)S(1)}, u32[]{:S(2)}, u32[]{:S(2)}) async-start(bf16[32,4,4608]{2,1,0:T(4,128)(2,1)} %bitcast.79), calls=%async_computation.1 | async-start | bytes 2359296 | tf_op jit(solution)/shard_map/all_to_all | solution.py:59
  73.5 32.8 %all-to-all-start.2 = ((bf16[32,4,4608]{2,1,0:T(4,128)(2,1)}), bf16[32,4,4608]{2,1,0:T(4,128)(2,1)}, u32[]{:S(2)}, u32[]{:S(2)}) async-start(bf16[32,4,4608]{2,1,0:T(4,128)(2,1)} %bitcast.80), calls=%async_computation.2 | async-start | bytes 2359296 | tf_op jit(solution)/shard_map/all_to_all | solution.py:59

commit v7 on v6

--- a/solution.py
+++ b/solution.py
@@ -95,17 +95,15 @@
         vectors = arrange(arrived[panel_index])
         finished.append(project(earlier, finished, vectors, block_len))
     new_basis = jnp.stack(finished, 0)
-    new_basis, finished, further_arrived = lax.optimization_barrier((new_basis, finished, arrived[-1]))
+    full_basis = jnp.concatenate([earlier] + finished, axis=0)
+    new_basis, full_basis, further_arrived = lax.optimization_barrier(
+        (new_basis, full_basis, arrived[-1])
+    )
     further_blocks = arrange(further_arrived)
-    products = []
-    for basis_part in [earlier] + finished:
-        products.append(
-            jnp.einsum(
-                "nbl,pbl->pbn", basis_part, further_blocks, preferred_element_type=jnp.float32
-            )
-            / block_len
-        )
-    coarse = jnp.concatenate(products, axis=2)
+    coarse = (
+        jnp.einsum("nbl,pbl->pbn", full_basis, further_blocks, preferred_element_type=jnp.float32)
+        / block_len
+    )
     return (new_basis, coarse)
 
 

time: 115 us -> 115 us (level)
  waiting for transfers between devices: 55.8 us -> 50.1 us
  other arithmetic: 10.4 us -> 15.4 us
    all_to_all x3, waiting for transfers between devices: 55.8 us -> 50.1 us  [send(): lax.all_to_all(block_major, ('lat', 'mode'), split_axis=0, concat_axis=0,...]
    concatenate x1, other arithmetic: 0.7 us -> 5.76 us  [per_device(): full_basis = jnp.concatenate([earlier] + finished, axis=0)]
    dot_general x3 -> x1, matrix products: 4.92 us -> 5.55 us  [per_device(): jnp.einsum('nbl,pbl->pbn', full_basis, further_blocks, preferred_element_...]
  transfers between devices with their start and end apart: 3 -> 3, of which waited for: 3 -> 3; matrix products, arithmetic and copies ran while one was open for 16% -> 21% of each run, Pallas kernels for 11% -> 11%
where the time goes in v7:
time: 115 us; the launch traced here: 114 us
  waiting for transfers between devices  50.1 us (44%)
  other arithmetic  15.4 us (13%)
  starting transfers between devices  14.9 us (13%)
  Pallas kernels  12.9 us (11%)
  local copies, waits for them, and re-layouts  12 us (10%)
  matrix products  8.11 us (7%)
    all_to_all x3, waiting for transfers between devices, send(): lax.all_to_all(block_major, ('lat', 'mode'), split_axis=0, concat_axis=0,...  50.1 us
    all_to_all x3, starting transfers between devices, send(): lax.all_to_all(block_major, ('lat', 'mode'), split_axis=0, concat_axis=0,...  14.9 us
    pallas_call x2, Pallas kernels, project_call(): pl.pallas_call(functools.partial(project_kernel, piece_count=len(pieces),...  12.9 us
    unnamed x8, local copies, waits for them, and re-layouts  6.81 us
    concatenate x1, other arithmetic, per_device(): full_basis = jnp.concatenate([earlier] + finished, axis=0)  5.76 us
    dot_general x1, matrix products, per_device(): jnp.einsum('nbl,pbl->pbn', full_basis, further_blocks, preferred_element_...  5.55 us
    another operation x6, other arithmetic, factor_inverse(): lower_factor = jnp.linalg.cholesky(gram_matrix)  4.31 us
    another operation x4, other arithmetic, factor_inverse(): lax.linalg.triangular_solve(lower_factor, identity, left_side=True, lower...  3.75 us
  transfers between devices with their start and end apart: 3, of which 3 were waited for; matrix products, arithmetic and copies ran while one was open for 21% of the time, Pallas kernels for 11%

profile of v7, /device:TPU:0, one launch (start us, length us, event | category | flops | bytes accessed | tf_op | source)
XLA Modules:
  0.0 114.2 jit_solution(2921694785063230251)
XLA Ops:
  0.6 1.8 %fusion.15 = (bf16[1,4,32,4608]{3,2,1,0:T(8,128)(2,1)S(1)}, bf16[1,4,32,4608]{3,2,1,0:T(8,128)(2,1)S(1)}) fusion(bf16[2,4,32,4608]{3,2,1,0:T(8,128)(2,1)} %param.7), kind=kLoop, calls=%fused_computation.30 | loop fusion | bytes 4718592 | tf_op jit(solution)/shard_map/slice | solution.py:87
  2.5 1.9 %copy.33 = bf16[1,4,32,4608]{3,1,2,0:T(4,128)(2,1)} copy(bf16[1,4,32,4608]{3,2,1,0:T(8,128)(2,1)S(1)} %get-tuple-element.32) | data formatting | bytes 2359296
  4.4 7.3 %all-to-all-start = ((bf16[32,4,4608]{2,1,0:T(4,128)(2,1)}), bf16[32,4,4608]{2,1,0:T(4,128)(2,1)S(1)}, u32[]{:S(2)}, u32[]{:S(2)}) async-start(bf16[32,4,4608]{2,1,0:T(4,128)(2,1)} %bitcast.61), calls=%async_computation | async-start | bytes 2359296 | tf_op jit(solution)/shard_map/all_to_all | solution.py:59
  11.7 1.9 %copy.34 = bf16[1,4,32,4608]{3,1,2,0:T(4,128)(2,1)} copy(bf16[1,4,32,4608]{3,2,1,0:T(8,128)(2,1)S(1)} %get-tuple-element.33) | data formatting | bytes 2359296
  13.6 27.2 %all-to-all-done = bf16[32,4,4608]{2,1,0:T(4,128)(2,1)S(1)} async-done(((bf16[32,4,4608]{2,1,0:T(4,128)(2,1)}), bf16[32,4,4608]{2,1,0:T(4,128)(2,1)S(1)}, u32[]{:S(2)}, u32[]{:S(2)}) %all-to-all-start) | async-done | bytes 1179680 | tf_op jit(solution)/shard_map/all_to_all | solution.py:59
  40.8 3.7 %all-to-all-start.1 = ((bf16[32,4,4608]{2,1,0:T(4,128)(2,1)}), bf16[32,4,4608]{2,1,0:T(4,128)(2,1)S(1)}, u32[]{:S(2)}, u32[]{:S(2)}) async-start(bf16[32,4,4608]{2,1,0:T(4,128)(2,1)} %bitcast.62), calls=%async_computation.1 | async-start | bytes 2359296 | tf_op jit(solution)/shard_map/all_to_all | solution.py:59
  44.4 1.9 %copy.35 = bf16[4,32,4608]{2,0,1:T(4,128)(2,1)} copy(bf16[4,32,4608]{2,1,0:T(8,128)(2,1)S(1)} %copy-done) | data formatting | bytes 2359296 | tf_op args[2]
  46.4 0.7 copy.19
  47.0 0.3 copy.27
  47.4 6.8 %shard_map.50 = (bf16[16,36864]{1,0:T(8,128)(2,1)S(1)}, f32[16,16]{1,0:T(8,128)S(1)}) custom-call(bf16[64,36864]{1,0:T(8,128)(2,1)} %bitcast.68, bf16[16,36864]{1,0:T(8,128)(2,1)S(1)} %bitcast.67), custom_call_target="tpu_custom_call" | custom-call | flops 169869312 | bytes 7078912 | tf_op jit(solution)/shard_map/pallas_call | solution.py:33
  54.3 1.5 %cholesky.44 = f32[16,16]{1,0:T(8,128)S(1)} custom-call(f32[16,16]{1,0:T(8,128)S(1)} %fusion.14), custom_call_target="Cholesky" | custom-call | tf_op jit(solution)/shard_map/jit(cholesky)/cholesky | solution.py:51
  55.8 0.6 compare_reduce_fusion.1
  56.4 0.6 fusion.9
  57.1 1.2 %custom-call.6 = f32[1,16,16]{1,2,0:T(8,128)S(1)} custom-call(f32[1,16,16]{2,1,0:T(8,128)S(1)} %fusion.9), custom_call_target="InvertDiagBlocksLowerTriangular" | custom-call | tf_op jit(solution)/shard_map/triangular_solve/custom-call.0 | solution.py:55
  58.3 0.2 fusion.7
  58.5 1.1 convolution_convert_fusion.1.refs_1_
  59.6 13.9 %all-to-all-done.1 = bf16[32,4,4608]{2,1,0:T(4,128)(2,1)S(1)} async-done(((bf16[32,4,4608]{2,1,0:T(4,128)(2,1)}), bf16[32,4,4608]{2,1,0:T(4,128)(2,1)S(1)}, u32[]{:S(2)}, u32[]{:S(2)}) %all-to-all-start.1) | async-done | bytes 1179680 | tf_op jit(solution)/shard_map/all_to_all | solution.py:59
  73.5 3.9 %all-to-all-start.2 = ((bf16[32,4,4608]{2,1,0:T(4,128)(2,1)}), bf16[32,4,4608]{2,1,0:T(4,128)(2,1)}, u32[]{:S(2)}, u32[]{:S(2)}) async-start(bf16[32,4,4608]{2,1,0:T(4,128)(2,1)} %bitcast.63), calls=%async_computation.2 | async-start | bytes 2359296 | tf_op jit(solution)/shard_map/all_to_all | solution.py:59
  77.5 0.7 copy.21
  78.1 0.3 copy.28
  78.5 6.1 %shard_map.51 = (bf16[16,36864]{1,0:T(8,128)(2,1)S(1)}, f32[16,16]{1,0:T(8,128)S(1)}) custom-call(bf16[64,36864]{1,0:T(8,128)(2,1)} %bitcast.69, bf16[16,36864]{1,0:T(8,128)(2,1)S(1)} %convolution_convert_fusion.1.refs_1_, bf16[16,36864]{1,0:T(8,128)(2,1)S(1)} %bitcast.66), custom_call_target="tpu_custom_call" | custom-call | flops 207618048 | bytes 8258560 | tf_op jit(solution)/shard_map/pallas_call | solution.py:33
  84.6 1.5 %cholesky.55 = f32[16,16]{1,0:T(8,128)S(1)} custom-call(f32[16,16]{1,0:T(8,128)S(1)} %fusion.12), custom_call_target="Cholesky" | custom-call | tf_op jit(solution)/shard_map/jit(cholesky)/cholesky | solution.py:51
  86.1 0.6 compare_reduce_fusion
  86.8 0.6 fusion.10
  87.4 1.2 %custom-call.7 = f32[1,16,16]{1,2,0:T(8,128)S(1)} custom-call(f32[1,16,16]{2,1,0:T(8,128)S(1)} %fusion.10), custom_call_target="InvertDiagBlocksLowerTriangular" | custom-call | tf_op jit(solution)/shard_map/triangular_solve/custom-call.0 | solution.py:55
  88.9 1.1 convolution_convert_fusion
  89.9 5.8 %pad_maximum_fusion = bf16[96,1,36864]{2,0,1:T(8,128)(2,1)} fusion(bf16[16,1,36864]{2,0,1:T(8,128)(2,1)S(1)} %bitcast.70, bf16[16,1,36864]{2,0,1:T(8,128)(2,1)S(1)} %bitcast.64, bf16[64,1,36864]{2,0,1:T(8,128)(2,1)} %param.6), kind=kLoop, calls=%fused_computation.2 | loop fusion | flops 21233664 | bytes 14155776 | tf_op jit(solution)/shard_map/concatenate | solution.py:98
  95.7 1.6 %pad_maximum_fusion.1 = bf16[2,16,1,36864]{3,1,2,0:T(8,128)(2,1)} fusion(bf16[1,16,1,36864]{3,1,2,0:T(8,128)(2,1)S(1)} %bitcast.71, bf16[1,16,1,36864]{3,1,2,0:T(8,128)(2,1)S(1)} %bitcast.65), kind=kLoop, calls=%fused_computation.5 | loop fusion | flops 1179648 | bytes 4718592 | tf_op jit(solution)/shard_map/stack | solution.py:97
  97.3 9.0 %all-to-all-done.2 = bf16[32,4,4608]{2,1,0:T(4,128)(2,1)} async-done(((bf16[32,4,4608]{2,1,0:T(4,128)(2,1)}), bf16[32,4,4608]{2,1,0:T(4,128)(2,1)}, u32[]{:S(2)}, u32[]{:S(2)}) %all-to-all-start.2) | async-done | bytes 1179680 | tf_op jit(solution)/shard_map/all_to_all | solution.py:59
  106.4 1.9 %copy.23 = bf16[8,4,4,4608]{3,0,2,1:T(8,128)(2,1)S(1)} copy(bf16[8,4,4,4608]{3,2,1,0:T(4,128)(2,1)} %bitcast.20) | data formatting | bytes 2359296 | tf_op jit(solution)/shard_map/reshape | solution.py:65
  108.3 0.3 copy.29
  108.6 5.5 %fusion.2 = f32[16,96]{1,0:T(8,128)} fusion(bf16[16,36864]{1,0:T(8,128)(2,1)S(1)} %bitcast.72, bf16[96,1,36864]{2,0,1:T(8,128)(2,1)} %pad_maximum_fusion), kind=kOutput, calls=%fused_computation.9 | convolution fusion | flops 113247744 | bytes 8263680 | tf_op jit(solution)/shard_map/nbl,pbl->pbn/dot_general | solution.py:104
  (9 shorter events, 0.4 us)
Async XLA Ops:
  4.4 36.4 %all-to-all-start = ((bf16[32,4,4608]{2,1,0:T(4,128)(2,1)}), bf16[32,4,4608]{2,1,0:T(4,128)(2,1)S(1)}, u32[]{:S(2)}, u32[]{:S(2)}) async-start(bf16[32,4,4608]{2,1,0:T(4,128)(2,1)} %bitcast.61), calls=%async_computation | async-start | bytes 2359296 | tf_op jit(solution)/shard_map/all_to_all | solution.py:59
  40.8 3.7 %copy-start = (bf16[4,32,4608]{2,1,0:T(8,128)(2,1)S(1)}, bf16[4,32,4608]{2,1,0:T(8,128)(2,1)}, u32[]{:S(2)}) copy-start(bf16[4,32,4608]{2,1,0:T(8,128)(2,1)} %param.8) | copy-start | bytes 3538948
  40.8 32.7 %all-to-all-start.1 = ((bf16[32,4,4608]{2,1,0:T(4,128)(2,1)}), bf16[32,4,4608]{2,1,0:T(4,128)(2,1)S(1)}, u32[]{:S(2)}, u32[]{:S(2)}) async-start(bf16[32,4,4608]{2,1,0:T(4,128)(2,1)} %bitcast.62), calls=%async_computation.1 | async-start | bytes 2359296 | tf_op jit(solution)/shard_map/all_to_all | solution.py:59
  73.5 32.8 %all-to-all-start.2 = ((bf16[32,4,4608]{2,1,0:T(4,128)(2,1)}), bf16[32,4,4608]{2,1,0:T(4,128)(2,1)}, u32[]{:S(2)}, u32[]{:S(2)}) async-start(bf16[32,4,4608]{2,1,0:T(4,128)(2,1)} %bitcast.63), calls=%async_computation.2 | async-start | bytes 2359296 | tf_op jit(solution)/shard_map/all_to_all | solution.py:59

commit v8 on v6

--- a/solution.py
+++ b/solution.py
@@ -84,18 +84,18 @@
 def per_device(earlier, panels, further):
     block_len = earlier.shape[2]
     panel_count = panels.shape[0]
-    outgoing = [panels[k].transpose(1, 0, 2) for k in range(panel_count)]
-    outgoing.append(further.transpose(1, 0, 2))
-    arrived = [send(outgoing[0])]
-    for index in range(1, len(outgoing)):
-        ready, arrived[0] = lax.optimization_barrier((outgoing[index], arrived[0]))
-        arrived.append(send(ready))
+    vector_part = panels.shape[1]
+    outgoing = panels.transpose(2, 0, 1, 3).reshape(panels.shape[2], -1, panels.shape[3])
+    panels_arrived = send(outgoing)
+    further_arrived = send(further.transpose(1, 0, 2))
     finished = []
     for panel_index in range(panel_count):
-        vectors = arrange(arrived[panel_index])
-        finished.append(project(earlier, finished, vectors, block_len))
+        part = panels_arrived[:, panel_index * vector_part:(panel_index + 1) * vector_part]
+        finished.append(project(earlier, finished, arrange(part), block_len))
     new_basis = jnp.stack(finished, 0)
-    new_basis, finished, further_arrived = lax.optimization_barrier((new_basis, finished, arrived[-1]))
+    new_basis, finished, further_arrived = lax.optimization_barrier(
+        (new_basis, finished, further_arrived)
+    )
     further_blocks = arrange(further_arrived)
     products = []
     for basis_part in [earlier] + finished:

time: 115 us -> 108 us (0.939)
  starting transfers between devices: 14.9 us -> 11.6 us
  waiting for transfers between devices: 55.8 us -> 53.3 us
    reshape x0 -> x1, local copies, waits for them, and re-layouts: none -> 4.36 us  [per_device(): panels.transpose(2, 0, 1, 3).reshape(panels.shape[2], -1, panels.shape[3])]
    unnamed x8 -> x6, local copies, waits for them, and re-layouts: 6.85 us -> 3 us
    all_to_all x3 -> x2, starting transfers between devices: 14.9 us -> 11.6 us  [send(): lax.all_to_all(block_major, ('lat', 'mode'), split_axis=0, concat_axis=0,...]
    all_to_all x3 -> x2, waiting for transfers between devices: 55.8 us -> 53.3 us  [send(): lax.all_to_all(block_major, ('lat', 'mode'), split_axis=0, concat_axis=0,...]
    transpose x0 -> x2, local copies, waits for them, and re-layouts: none -> 1.3 us  [arrange(): whole = by_source.transpose(1, 2, 0, 3)]
    reshape x3 -> x1, local copies, waits for them, and re-layouts: 3.22 us -> 1.92 us  [split_by_source(): received.reshape(lat_count, mode_count, received.shape[1], received.shape...]
  transfers between devices with their start and end apart: 3 -> 2, of which waited for: 3 -> 2; matrix products, arithmetic and copies ran while one was open for 16% -> 16% of each run, Pallas kernels for 11% -> 12%
where the time goes in v8:
time: 108 us
  waiting for transfers between devices  53.3 us (49%)
  Pallas kernels  12.9 us (12%)
  starting transfers between devices  11.6 us (11%)
  local copies, waits for them, and re-layouts  11.5 us (11%)
  other arithmetic  10.4 us (10%)
  matrix products  7.48 us (7%)
    all_to_all x2, waiting for transfers between devices, send(): lax.all_to_all(block_major, ('lat', 'mode'), split_axis=0, concat_axis=0,...  53.3 us
    pallas_call x2, Pallas kernels, project_call(): pl.pallas_call(functools.partial(project_kernel, piece_count=len(pieces),...  12.9 us
    all_to_all x2, starting transfers between devices, send(): lax.all_to_all(block_major, ('lat', 'mode'), split_axis=0, concat_axis=0,...  11.6 us
    dot_general x3, matrix products, per_device(): jnp.einsum('nbl,pbl->pbn', basis_part, further_blocks, preferred_element_...  4.92 us
    reshape x1, local copies, waits for them, and re-layouts, per_device(): panels.transpose(2, 0, 1, 3).reshape(panels.shape[2], -1, panels.shape[3])  4.36 us
    another operation x6, other arithmetic, factor_inverse(): lower_factor = jnp.linalg.cholesky(gram_matrix)  4.31 us
    another operation x4, other arithmetic, factor_inverse(): lax.linalg.triangular_solve(lower_factor, identity, left_side=True, lower...  3.75 us
    unnamed x6, local copies, waits for them, and re-layouts  3 us
  transfers between devices with their start and end apart: 2, of which 2 were waited for; matrix products, arithmetic and copies ran while one was open for 16% of the time, Pallas kernels for 12%

profile of v8, /device:TPU:0, one launch (start us, length us, event | category | flops | bytes accessed | tf_op | source)
XLA Modules:
  0.0 107.9 jit_solution(8885799742883289753)
XLA Ops:
  0.6 4.4 %copy.15 = bf16[32,8,4608]{2,1,0:T(8,128)(2,1)} copy(bf16[32,8,4608]{2,0,1:T(8,128)(2,1)} %bitcast.92) | data formatting | bytes 4718592 | tf_op jit(solution)/shard_map/reshape | solution.py:88
  5.0 7.3 %all-to-all-start = ((bf16[32,8,4608]{2,1,0:T(8,128)(2,1)}), bf16[32,8,4608]{2,1,0:T(8,128)(2,1)S(1)}, u32[]{:S(2)}, u32[]{:S(2)}) async-start(bf16[32,8,4608]{2,1,0:T(8,128)(2,1)} %copy.15), calls=%async_computation | async-start | bytes 4718592 | tf_op jit(solution)/shard_map/all_to_all | solution.py:59
  12.3 2.0 %copy.27 = bf16[4,32,4608]{2,0,1:T(4,128)(2,1)} copy(bf16[4,32,4608]{2,1,0:T(8,128)(2,1)S(1)} %copy-done) | data formatting | bytes 2359296 | tf_op args[2]
  14.3 52.6 %all-to-all-done = bf16[32,8,4608]{2,1,0:T(8,128)(2,1)S(1)} async-done(((bf16[32,8,4608]{2,1,0:T(8,128)(2,1)}), bf16[32,8,4608]{2,1,0:T(8,128)(2,1)S(1)}, u32[]{:S(2)}, u32[]{:S(2)}) %all-to-all-start) | async-done | bytes 2359328 | tf_op jit(solution)/shard_map/all_to_all | solution.py:59
  66.8 4.3 %all-to-all-start.1 = ((bf16[32,4,4608]{2,1,0:T(4,128)(2,1)}), bf16[32,4,4608]{2,1,0:T(4,128)(2,1)}, u32[]{:S(2)}, u32[]{:S(2)}) async-start(bf16[32,4,4608]{2,1,0:T(4,128)(2,1)} %bitcast.75), calls=%async_computation.1 | async-start | bytes 2359296 | tf_op jit(solution)/shard_map/all_to_all | solution.py:59
  71.1 0.8 fusion.28
  71.9 0.7 copy.18
  72.6 0.3 copy.24
  72.9 0.7 copy.16
  73.6 0.3 copy.23
  73.9 6.8 %shard_map.50 = (bf16[16,36864]{1,0:T(8,128)(2,1)S(1)}, f32[16,16]{1,0:T(8,128)S(1)}) custom-call(bf16[64,36864]{1,0:T(8,128)(2,1)} %bitcast.80, bf16[16,36864]{1,0:T(8,128)(2,1)S(1)} %bitcast.79), custom_call_target="tpu_custom_call" | custom-call | flops 169869312 | bytes 7078912 | tf_op jit(solution)/shard_map/pallas_call | solution.py:33
  80.8 1.5 %cholesky.44 = f32[16,16]{1,0:T(8,128)S(1)} custom-call(f32[16,16]{1,0:T(8,128)S(1)} %fusion.26), custom_call_target="Cholesky" | custom-call | tf_op jit(solution)/shard_map/jit(cholesky)/cholesky | solution.py:51
  82.3 0.6 compare_reduce_fusion.1
  83.0 0.6 fusion.21
  83.6 1.2 %custom-call.6 = f32[1,16,16]{1,2,0:T(8,128)S(1)} custom-call(f32[1,16,16]{2,1,0:T(8,128)S(1)} %fusion.21), custom_call_target="InvertDiagBlocksLowerTriangular" | custom-call | tf_op jit(solution)/shard_map/triangular_solve/custom-call.0 | solution.py:55
  84.9 0.2 fusion.19
  85.1 1.1 convolution_convert_fusion.1.refs_1_
  86.2 6.1 %shard_map.51 = (bf16[16,36864]{1,0:T(8,128)(2,1)S(1)}, f32[16,16]{1,0:T(8,128)S(1)}) custom-call(bf16[64,36864]{1,0:T(8,128)(2,1)} %bitcast.81, bf16[16,36864]{1,0:T(8,128)(2,1)S(1)} %convolution_convert_fusion.1.refs_1_, bf16[16,36864]{1,0:T(8,128)(2,1)S(1)} %bitcast.78), custom_call_target="tpu_custom_call" | custom-call | flops 207618048 | bytes 8258560 | tf_op jit(solution)/shard_map/pallas_call | solution.py:33
  92.3 1.5 %cholesky.55 = f32[16,16]{1,0:T(8,128)S(1)} custom-call(f32[16,16]{1,0:T(8,128)S(1)} %fusion.24), custom_call_target="Cholesky" | custom-call | tf_op jit(solution)/shard_map/jit(cholesky)/cholesky | solution.py:51
  93.8 0.6 compare_reduce_fusion
  94.5 0.6 fusion.22
  95.1 1.2 %custom-call.7 = f32[1,16,16]{1,2,0:T(8,128)S(1)} custom-call(f32[1,16,16]{2,1,0:T(8,128)S(1)} %fusion.22), custom_call_target="InvertDiagBlocksLowerTriangular" | custom-call | tf_op jit(solution)/shard_map/triangular_solve/custom-call.0 | solution.py:55
  96.3 0.2 fusion.17
  96.5 1.1 %convolution_convert_fusion = bf16[16,36864]{1,0:T(8,128)(2,1)S(1)} fusion(f32[16,16]{1,0:T(8,128)S(1)} %fusion.17, bf16[16,36864]{1,0:T(8,128)(2,1)S(1)} %get-tuple-element.15), kind=kOutput, calls=%fused_computation | convolution fusion | flops 113836032 | bytes 2360320 | tf_op jit(solution)/shard_map/dot_general | solution.py:80
  97.6 1.6 %pad_maximum_fusion = bf16[2,16,1,36864]{3,1,2,0:T(8,128)(2,1)} fusion(bf16[1,16,1,36864]{3,1,2,0:T(8,128)(2,1)S(1)} %bitcast.85, bf16[1,16,1,36864]{3,1,2,0:T(8,128)(2,1)S(1)} %bitcast.76), kind=kLoop, calls=%fused_computation.2 | loop fusion | flops 1179648 | bytes 4718592 | tf_op jit(solution)/shard_map/stack | solution.py:95
  99.2 0.8 all-to-all-done.1
  100.0 1.9 %copy.21 = bf16[8,4,4,4608]{3,0,2,1:T(8,128)(2,1)S(1)} copy(bf16[8,4,4,4608]{3,2,1,0:T(4,128)(2,1)} %bitcast.18) | data formatting | bytes 2359296 | tf_op jit(solution)/shard_map/reshape | solution.py:65
  102.0 0.3 copy.25
  102.3 3.7 %fusion.4 = f32[16,1,64]{2,0,1:T(8,128)S(1)} fusion(bf16[16,36864]{1,0:T(8,128)(2,1)S(1)} %bitcast.82, bf16[64,1,36864]{2,0,1:T(8,128)(2,1)} %param.6), kind=kOutput, calls=%fused_computation.9 | convolution fusion | flops 75498496 | bytes 5902336 | tf_op jit(solution)/shard_map/nbl,pbl->pbn/dot_general | solution.py:103
  106.0 0.6 fusion.14
  106.6 0.6 fusion.8
  107.2 0.7 pad_maximum_fusion.1
  (8 shorter events, 0.2 us)
Async XLA Ops:
  5.0 7.3 %copy-start = (bf16[4,32,4608]{2,1,0:T(8,128)(2,1)S(1)}, bf16[4,32,4608]{2,1,0:T(8,128)(2,1)}, u32[]{:S(2)}) copy-start(bf16[4,32,4608]{2,1,0:T(8,128)(2,1)} %param.8) | copy-start | bytes 3538948
  5.0 61.8 %all-to-all-start = ((bf16[32,8,4608]{2,1,0:T(8,128)(2,1)}), bf16[32,8,4608]{2,1,0:T(8,128)(2,1)S(1)}, u32[]{:S(2)}, u32[]{:S(2)}) async-start(bf16[32,8,4608]{2,1,0:T(8,128)(2,1)} %copy.15), calls=%async_computation | async-start | bytes 4718592 | tf_op jit(solution)/shard_map/all_to_all | solution.py:59
  66.8 33.2 %all-to-all-start.1 = ((bf16[32,4,4608]{2,1,0:T(4,128)(2,1)}), bf16[32,4,4608]{2,1,0:T(4,128)(2,1)}, u32[]{:S(2)}, u32[]{:S(2)}) async-start(bf16[32,4,4608]{2,1,0:T(4,128)(2,1)} %bitcast.75), calls=%async_computation.1 | async-start | bytes 2359296 | tf_op jit(solution)/shard_map/all_to_all | solution.py:59

commit v9 on v8

--- a/solution.py
+++ b/solution.py
@@ -84,13 +84,12 @@
 def per_device(earlier, panels, further):
     block_len = earlier.shape[2]
     panel_count = panels.shape[0]
-    vector_part = panels.shape[1]
-    outgoing = panels.transpose(2, 0, 1, 3).reshape(panels.shape[2], -1, panels.shape[3])
+    outgoing = panels.transpose(2, 0, 1, 3)
     panels_arrived = send(outgoing)
     further_arrived = send(further.transpose(1, 0, 2))
     finished = []
     for panel_index in range(panel_count):
-        part = panels_arrived[:, panel_index * vector_part:(panel_index + 1) * vector_part]
+        part = panels_arrived[:, panel_index]
         finished.append(project(earlier, finished, arrange(part), block_len))
     new_basis = jnp.stack(finished, 0)
     new_basis, finished, further_arrived = lax.optimization_barrier(

time: 108 us -> 109 us (level)
    unnamed x6 -> x7, local copies, waits for them, and re-layouts: 3 us -> 7.9 us
    reshape x1 -> x0, local copies, waits for them, and re-layouts: 4.36 us -> none  [per_device(): panels.transpose(2, 0, 1, 3).reshape(panels.shape[2], -1, panels.shape[3])]
    another operation x0 -> x2, local copies, waits for them, and re-layouts: none -> 1.3 us  [split_by_source(): received.reshape(lat_count, mode_count, received.shape[1], received.shape...]
    transpose x2 -> x0, local copies, waits for them, and re-layouts: 1.3 us -> none  [arrange(): whole = by_source.transpose(1, 2, 0, 3)]
where the time goes in v9:
time: 109 us; the launch traced here: 108 us
  waiting for transfers between devices  53.3 us (49%)
  Pallas kernels  12.9 us (12%)
  local copies, waits for them, and re-layouts  12.1 us (11%)
  starting transfers between devices  11.6 us (11%)
  other arithmetic  10.4 us (10%)
  matrix products  7.48 us (7%)
    all_to_all x2, waiting for transfers between devices, send(): lax.all_to_all(block_major, ('lat', 'mode'), split_axis=0, concat_axis=0,...  53.3 us
    pallas_call x2, Pallas kernels, project_call(): pl.pallas_call(functools.partial(project_kernel, piece_count=len(pieces),...  12.9 us
    all_to_all x2, starting transfers between devices, send(): lax.all_to_all(block_major, ('lat', 'mode'), split_axis=0, concat_axis=0,...  11.6 us
    unnamed x7, local copies, waits for them, and re-layouts  7.9 us
    dot_general x3, matrix products, per_device(): jnp.einsum('nbl,pbl->pbn', basis_part, further_blocks, preferred_element_...  4.92 us
    another operation x6, other arithmetic, factor_inverse(): lower_factor = jnp.linalg.cholesky(gram_matrix)  4.31 us
    another operation x4, other arithmetic, factor_inverse(): lax.linalg.triangular_solve(lower_factor, identity, left_side=True, lower...  3.75 us
  transfers between devices with their start and end apart: 2, of which 2 were waited for; matrix products, arithmetic and copies ran while one was open for 16% of the time, Pallas kernels for 12%

profile of v9, /device:TPU:0, one launch (start us, length us, event | category | flops | bytes accessed | tf_op | source)
XLA Modules:
  0.0 108.5 jit_solution(6018938525376978739)
XLA Ops:
  0.6 4.9 %copy.29 = bf16[2,4,32,4608]{3,1,0,2:T(4,128)(2,1)} copy(bf16[2,4,32,4608]{3,2,1,0:T(8,128)(2,1)} %param.7) | data formatting | bytes 4718592 | tf_op args[1]
  5.5 7.3 %all-to-all-start = ((bf16[32,2,4,4608]{3,2,1,0:T(4,128)(2,1)}), bf16[32,2,4,4608]{3,2,1,0:T(4,128)(2,1)S(1)}, u32[]{:S(2)}, u32[]{:S(2)}) async-start(bf16[32,2,4,4608]{3,2,1,0:T(4,128)(2,1)} %bitcast.85), calls=%async_computation | async-start | bytes 4718592 | tf_op jit(solution)/shard_map/all_to_all | solution.py:59
  12.8 2.0 %copy.30 = bf16[4,32,4608]{2,0,1:T(4,128)(2,1)} copy(bf16[4,32,4608]{2,1,0:T(8,128)(2,1)S(1)} %copy-done) | data formatting | bytes 2359296 | tf_op args[2]
  14.8 52.6 %all-to-all-done = bf16[32,2,4,4608]{3,2,1,0:T(4,128)(2,1)S(1)} async-done(((bf16[32,2,4,4608]{3,2,1,0:T(4,128)(2,1)}), bf16[32,2,4,4608]{3,2,1,0:T(4,128)(2,1)S(1)}, u32[]{:S(2)}, u32[]{:S(2)}) %all-to-all-start) | async-done | bytes 2359328 | tf_op jit(solution)/shard_map/all_to_all | solution.py:59
  67.4 4.3 %all-to-all-start.1 = ((bf16[32,4,4608]{2,1,0:T(4,128)(2,1)}), bf16[32,4,4608]{2,1,0:T(4,128)(2,1)}, u32[]{:S(2)}, u32[]{:S(2)}) async-start(bf16[32,4,4608]{2,1,0:T(4,128)(2,1)} %bitcast.73), calls=%async_computation.1 | async-start | bytes 2359296 | tf_op jit(solution)/shard_map/all_to_all | solution.py:59
  71.7 0.8 fusion.28
  72.5 0.7 copy.19
  73.1 0.3 copy.25
  73.5 0.7 copy.17
  74.2 0.3 copy.24
  74.5 6.8 %shard_map.50 = (bf16[16,36864]{1,0:T(8,128)(2,1)S(1)}, f32[16,16]{1,0:T(8,128)S(1)}) custom-call(bf16[64,36864]{1,0:T(8,128)(2,1)} %bitcast.78, bf16[16,36864]{1,0:T(8,128)(2,1)S(1)} %bitcast.77), custom_call_target="tpu_custom_call" | custom-call | flops 169869312 | bytes 7078912 | tf_op jit(solution)/shard_map/pallas_call | solution.py:33
  81.4 1.5 %cholesky.44 = f32[16,16]{1,0:T(8,128)S(1)} custom-call(f32[16,16]{1,0:T(8,128)S(1)} %fusion.26), custom_call_target="Cholesky" | custom-call | tf_op jit(solution)/shard_map/jit(cholesky)/cholesky | solution.py:51
  82.9 0.6 compare_reduce_fusion.1
  83.6 0.6 fusion.21
  84.2 1.2 %custom-call.6 = f32[1,16,16]{1,2,0:T(8,128)S(1)} custom-call(f32[1,16,16]{2,1,0:T(8,128)S(1)} %fusion.21), custom_call_target="InvertDiagBlocksLowerTriangular" | custom-call | tf_op jit(solution)/shard_map/triangular_solve/custom-call.0 | solution.py:55
  85.5 0.2 fusion.19
  85.7 1.1 convolution_convert_fusion.1.refs_1_
  86.7 6.1 %shard_map.51 = (bf16[16,36864]{1,0:T(8,128)(2,1)S(1)}, f32[16,16]{1,0:T(8,128)S(1)}) custom-call(bf16[64,36864]{1,0:T(8,128)(2,1)} %bitcast.79, bf16[16,36864]{1,0:T(8,128)(2,1)S(1)} %convolution_convert_fusion.1.refs_1_, bf16[16,36864]{1,0:T(8,128)(2,1)S(1)} %bitcast.76), custom_call_target="tpu_custom_call" | custom-call | flops 207618048 | bytes 8258560 | tf_op jit(solution)/shard_map/pallas_call | solution.py:33
  92.9 1.5 %cholesky.55 = f32[16,16]{1,0:T(8,128)S(1)} custom-call(f32[16,16]{1,0:T(8,128)S(1)} %fusion.24), custom_call_target="Cholesky" | custom-call | tf_op jit(solution)/shard_map/jit(cholesky)/cholesky | solution.py:51
  94.4 0.6 compare_reduce_fusion
  95.0 0.6 fusion.22
  95.7 1.2 %custom-call.7 = f32[1,16,16]{1,2,0:T(8,128)S(1)} custom-call(f32[1,16,16]{2,1,0:T(8,128)S(1)} %fusion.22), custom_call_target="InvertDiagBlocksLowerTriangular" | custom-call | tf_op jit(solution)/shard_map/triangular_solve/custom-call.0 | solution.py:55
  96.9 0.2 fusion.17
  97.1 1.1 convolution_convert_fusion
  98.2 1.6 %pad_maximum_fusion = bf16[2,16,1,36864]{3,1,2,0:T(8,128)(2,1)} fusion(bf16[1,16,1,36864]{3,1,2,0:T(8,128)(2,1)S(1)} %bitcast.83, bf16[1,16,1,36864]{3,1,2,0:T(8,128)(2,1)S(1)} %bitcast.74), kind=kLoop, calls=%fused_computation.2 | loop fusion | flops 1179648 | bytes 4718592 | tf_op jit(solution)/shard_map/stack | solution.py:94
  99.8 0.7 all-to-all-done.1
  100.6 1.9 %copy.22 = bf16[8,4,4,4608]{3,0,2,1:T(8,128)(2,1)S(1)} copy(bf16[8,4,4,4608]{3,2,1,0:T(4,128)(2,1)} %bitcast.17) | data formatting | bytes 2359296 | tf_op jit(solution)/shard_map/reshape | solution.py:65
  102.5 0.3 copy.26
  102.8 3.7 %fusion.4 = f32[16,1,64]{2,0,1:T(8,128)S(1)} fusion(bf16[16,36864]{1,0:T(8,128)(2,1)S(1)} %bitcast.80, bf16[64,1,36864]{2,0,1:T(8,128)(2,1)} %param.6), kind=kOutput, calls=%fused_computation.10 | convolution fusion | flops 75498496 | bytes 5902336 | tf_op jit(solution)/shard_map/nbl,pbl->pbn/dot_general | solution.py:102
  106.5 0.6 fusion.14
  107.1 0.6 fusion.8
  107.8 0.7 pad_maximum_fusion.1
  (8 shorter events, 0.2 us)
Async XLA Ops:
  5.5 7.3 %copy-start = (bf16[4,32,4608]{2,1,0:T(8,128)(2,1)S(1)}, bf16[4,32,4608]{2,1,0:T(8,128)(2,1)}, u32[]{:S(2)}) copy-start(bf16[4,32,4608]{2,1,0:T(8,128)(2,1)} %param.8) | copy-start | bytes 3538948
  5.5 61.8 %all-to-all-start = ((bf16[32,2,4,4608]{3,2,1,0:T(4,128)(2,1)}), bf16[32,2,4,4608]{3,2,1,0:T(4,128)(2,1)S(1)}, u32[]{:S(2)}, u32[]{:S(2)}) async-start(bf16[32,2,4,4608]{3,2,1,0:T(4,128)(2,1)} %bitcast.85), calls=%async_computation | async-start | bytes 4718592 | tf_op jit(solution)/shard_map/all_to_all | solution.py:59
  67.4 33.2 %all-to-all-start.1 = ((bf16[32,4,4608]{2,1,0:T(4,128)(2,1)}), bf16[32,4,4608]{2,1,0:T(4,128)(2,1)}, u32[]{:S(2)}, u32[]{:S(2)}) async-start(bf16[32,4,4608]{2,1,0:T(4,128)(2,1)} %bitcast.73), calls=%async_computation.1 | async-start | bytes 2359296 | tf_op jit(solution)/shard_map/all_to_all | solution.py:59

commit v10 on v8

--- a/solution.py
+++ b/solution.py
@@ -96,15 +96,15 @@
     new_basis, finished, further_arrived = lax.optimization_barrier(
         (new_basis, finished, further_arrived)
     )
-    further_blocks = arrange(further_arrived)
+    lat_count = lax.axis_size("lat")
+    further_parts = further_arrived.reshape(lat_count, -1, further_arrived.shape[-1])
     products = []
     for basis_part in [earlier] + finished:
-        products.append(
-            jnp.einsum(
-                "nbl,pbl->pbn", basis_part, further_blocks, preferred_element_type=jnp.float32
-            )
-            / block_len
-        )
+        rows = basis_part.reshape(basis_part.shape[0], lat_count, -1)
+        product = jnp.einsum(
+            "lpe,jle->lpj", further_parts, rows, preferred_element_type=jnp.float32
+        ).sum(0)
+        products.append(product.reshape(-1, 1, rows.shape[0]) / block_len)
     coarse = jnp.concatenate(products, axis=2)
     return (new_basis, coarse)
 

time: 108 us -> 110 us (1.019)
  local copies, waits for them, and re-layouts: 11.5 us -> 17.5 us
  waiting for transfers between devices: 53.3 us -> 47.4 us
  matrix products: 7.48 us -> 9.3 us
    unnamed x6 -> x8, local copies, waits for them, and re-layouts: 3 us -> 9.3 us
    all_to_all x2, waiting for transfers between devices: 53.3 us -> 47.4 us  [send(): lax.all_to_all(block_major, ('lat', 'mode'), split_axis=0, concat_axis=0,...]
    dot_general x3, matrix products: 4.92 us -> 6.73 us  [per_device(): jnp.einsum('lpe,jle->lpj', further_parts, rows, preferred_element_type=jn...]
  transfers between devices with their start and end apart: 2 -> 2, of which waited for: 2 -> 2; matrix products, arithmetic and copies ran while one was open for 16% -> 21% of each run, Pallas kernels for 12% -> 12%
where the time goes in v10:
time: 110 us
  waiting for transfers between devices  47.4 us (43%)
  local copies, waits for them, and re-layouts  17.5 us (16%)
  Pallas kernels  12.9 us (12%)
  starting transfers between devices  11.6 us (11%)
  other arithmetic  10.4 us (9%)
  matrix products  9.3 us (8%)
    all_to_all x2, waiting for transfers between devices, send(): lax.all_to_all(block_major, ('lat', 'mode'), split_axis=0, concat_axis=0,...  47.4 us
    pallas_call x2, Pallas kernels, project_call(): pl.pallas_call(functools.partial(project_kernel, piece_count=len(pieces),...  12.9 us
    all_to_all x2, starting transfers between devices, send(): lax.all_to_all(block_major, ('lat', 'mode'), split_axis=0, concat_axis=0,...  11.6 us
    unnamed x8, local copies, waits for them, and re-layouts  9.3 us
    dot_general x3, matrix products, per_device(): jnp.einsum('lpe,jle->lpj', further_parts, rows, preferred_element_type=jn...  6.73 us
    reshape x1, local copies, waits for them, and re-layouts, per_device(): panels.transpose(2, 0, 1, 3).reshape(panels.shape[2], -1, panels.shape[3])  4.36 us
    another operation x6, other arithmetic, factor_inverse(): lower_factor = jnp.linalg.cholesky(gram_matrix)  4.31 us
    another operation x4, other arithmetic, factor_inverse(): lax.linalg.triangular_solve(lower_factor, identity, left_side=True, lower...  3.75 us
  transfers between devices with their start and end apart: 2, of which 2 were waited for; matrix products, arithmetic and copies ran while one was open for 21% of the time, Pallas kernels for 12%

profile of v10, /device:TPU:0, one launch (start us, length us, event | category | flops | bytes accessed | tf_op | source)
XLA Modules:
  0.0 109.8 jit_solution(14931262484728617152)
XLA Ops:
  0.6 4.4 %copy.21 = bf16[32,8,4608]{2,1,0:T(8,128)(2,1)} copy(bf16[32,8,4608]{2,0,1:T(8,128)(2,1)} %bitcast.99) | data formatting | bytes 4718592 | tf_op jit(solution)/shard_map/reshape | solution.py:88
  5.0 7.3 %all-to-all-start = ((bf16[32,8,4608]{2,1,0:T(8,128)(2,1)}), bf16[32,8,4608]{2,1,0:T(8,128)(2,1)S(1)}, u32[]{:S(2)}, u32[]{:S(2)}) async-start(bf16[32,8,4608]{2,1,0:T(8,128)(2,1)} %copy.21), calls=%async_computation | async-start | bytes 4718592 | tf_op jit(solution)/shard_map/all_to_all | solution.py:59
  12.3 2.0 %copy.61 = bf16[4,32,4608]{2,0,1:T(4,128)(2,1)} copy(bf16[4,32,4608]{2,1,0:T(8,128)(2,1)S(1)} %copy-done) | data formatting | bytes 2359296 | tf_op args[2]
  14.3 5.9 %copy.33 = bf16[8,8,8,4608]{3,2,1,0:T(8,128)(2,1)} copy(bf16[8,8,8,4608]{3,1,2,0:T(8,128)(2,1)} %bitcast.89) | data formatting | bytes 9437184
  20.2 46.6 %all-to-all-done = bf16[32,8,4608]{2,1,0:T(8,128)(2,1)S(1)} async-done(((bf16[32,8,4608]{2,1,0:T(8,128)(2,1)}), bf16[32,8,4608]{2,1,0:T(8,128)(2,1)S(1)}, u32[]{:S(2)}, u32[]{:S(2)}) %all-to-all-start) | async-done | bytes 2359328 | tf_op jit(solution)/shard_map/all_to_all | solution.py:59
  66.8 4.3 %all-to-all-start.1 = ((bf16[32,4,4608]{2,1,0:T(4,128)(2,1)}), bf16[32,4,4608]{2,1,0:T(4,128)(2,1)}, u32[]{:S(2)}, u32[]{:S(2)}) async-start(bf16[32,4,4608]{2,1,0:T(4,128)(2,1)} %bitcast.84), calls=%async_computation.1 | async-start | bytes 2359296 | tf_op jit(solution)/shard_map/all_to_all | solution.py:59
  71.1 0.8 fusion.43
  71.9 0.7 copy.24
  72.6 0.3 copy.32
  72.9 0.7 copy.22
  73.6 0.3 copy.31
  73.9 6.8 %shard_map.50 = (bf16[16,36864]{1,0:T(8,128)(2,1)S(1)}, f32[16,16]{1,0:T(8,128)S(1)}) custom-call(bf16[64,36864]{1,0:T(8,128)(2,1)} %bitcast.90, bf16[16,36864]{1,0:T(8,128)(2,1)S(1)} %bitcast.88), custom_call_target="tpu_custom_call" | custom-call | flops 169869312 | bytes 7078912 | tf_op jit(solution)/shard_map/pallas_call | solution.py:33
  80.8 1.5 %cholesky.44 = f32[16,16]{1,0:T(8,128)S(1)} custom-call(f32[16,16]{1,0:T(8,128)S(1)} %fusion.42), custom_call_target="Cholesky" | custom-call | tf_op jit(solution)/shard_map/jit(cholesky)/cholesky | solution.py:51
  82.3 0.6 compare_reduce_fusion.1
  83.0 0.6 fusion.37
  83.6 1.2 %custom-call.6 = f32[1,16,16]{1,2,0:T(8,128)S(1)} custom-call(f32[1,16,16]{2,1,0:T(8,128)S(1)} %fusion.37), custom_call_target="InvertDiagBlocksLowerTriangular" | custom-call | tf_op jit(solution)/shard_map/triangular_solve/custom-call.0 | solution.py:55
  85.1 1.1 convolution_convert_fusion.1.refs_1_
  86.2 6.1 %shard_map.51 = (bf16[16,36864]{1,0:T(8,128)(2,1)S(1)}, f32[16,16]{1,0:T(8,128)S(1)}) custom-call(bf16[64,36864]{1,0:T(8,128)(2,1)} %bitcast.91, bf16[16,36864]{1,0:T(8,128)(2,1)S(1)} %convolution_convert_fusion.1.refs_1_, bf16[16,36864]{1,0:T(8,128)(2,1)S(1)} %bitcast.87), custom_call_target="tpu_custom_call" | custom-call | flops 207618048 | bytes 8258560 | tf_op jit(solution)/shard_map/pallas_call | solution.py:33
  92.3 1.5 %cholesky.55 = f32[16,16]{1,0:T(8,128)S(1)} custom-call(f32[16,16]{1,0:T(8,128)S(1)} %fusion.40), custom_call_target="Cholesky" | custom-call | tf_op jit(solution)/shard_map/jit(cholesky)/cholesky | solution.py:51
  93.8 0.6 compare_reduce_fusion
  94.5 0.6 fusion.38
  95.1 1.2 %custom-call.7 = f32[1,16,16]{1,2,0:T(8,128)S(1)} custom-call(f32[1,16,16]{2,1,0:T(8,128)S(1)} %fusion.38), custom_call_target="InvertDiagBlocksLowerTriangular" | custom-call | tf_op jit(solution)/shard_map/triangular_solve/custom-call.0 | solution.py:55
  96.5 1.1 convolution_convert_fusion
  97.6 1.6 %pad_maximum_fusion = bf16[2,16,1,36864]{3,1,2,0:T(8,128)(2,1)} fusion(bf16[1,16,1,36864]{3,1,2,0:T(8,128)(2,1)S(1)} %bitcast.93, bf16[1,16,1,36864]{3,1,2,0:T(8,128)(2,1)S(1)} %bitcast.85), kind=kLoop, calls=%fused_computation.4 | loop fusion | flops 1179648 | bytes 4718592 | tf_op jit(solution)/shard_map/stack | solution.py:95
  99.2 0.8 all-to-all-done.1
  100.0 1.6 %reshape.58 = bf16[8,16,4608]{2,1,0:T(8,128)(2,1)S(1)} reshape(bf16[32,4,4608]{2,1,0:T(4,128)(2,1)} %all-to-all-done.1) | data formatting | bytes 2359296 | tf_op jit(solution)/shard_map/reshape | solution.py:100
  101.7 0.3 copy.34
  102.0 0.3 copy.35
  102.4 0.9 fusion.30
  103.2 0.9 fusion.24
  104.1 5.0 %fusion.18 = f32[16,1,64]{2,0,1:T(8,128)S(1)} fusion(bf16[8,16,4608]{2,1,0:T(8,128)(2,1)S(1)} %reshape.58, bf16[64,8,4608]{2,1,0:T(8,128)(2,1)} %bitcast.92), kind=kOutput, calls=%fused_computation.14 | convolution fusion | flops 75498496 | bytes 5902336 | tf_op jit(solution)/shard_map/lpe,jle->lpj/dot_general | solution.py:104
  109.1 0.7 pad_maximum_fusion.1
  (10 shorter events, 0.6 us)
Async XLA Ops:
  5.0 7.3 %copy-start = (bf16[4,32,4608]{2,1,0:T(8,128)(2,1)S(1)}, bf16[4,32,4608]{2,1,0:T(8,128)(2,1)}, u32[]{:S(2)}) copy-start(bf16[4,32,4608]{2,1,0:T(8,128)(2,1)} %param.8) | copy-start | bytes 3538948
  5.0 61.8 %all-to-all-start = ((bf16[32,8,4608]{2,1,0:T(8,128)(2,1)}), bf16[32,8,4608]{2,1,0:T(8,128)(2,1)S(1)}, u32[]{:S(2)}, u32[]{:S(2)}) async-start(bf16[32,8,4608]{2,1,0:T(8,128)(2,1)} %copy.21), calls=%async_computation | async-start | bytes 4718592 | tf_op jit(solution)/shard_map/all_to_all | solution.py:59
  66.8 33.2 %all-to-all-start.1 = ((bf16[32,4,4608]{2,1,0:T(4,128)(2,1)}), bf16[32,4,4608]{2,1,0:T(4,128)(2,1)}, u32[]{:S(2)}, u32[]{:S(2)}) async-start(bf16[32,4,4608]{2,1,0:T(4,128)(2,1)} %bitcast.84), calls=%async_computation.1 | async-start | bytes 2359296 | tf_op jit(solution)/shard_map/all_to_all | solution.py:59

commit v11 on v8

--- a/solution.py
+++ b/solution.py
@@ -47,6 +47,26 @@
     )(*pieces, vectors)
 
 
+def block_major_kernel(panels_ref, out_ref):
+    rows = panels_ref[...]
+    rows = rows.reshape(-1, rows.shape[2], rows.shape[3])
+    out_ref[...] = jnp.swapaxes(rows, 0, 1)
+
+
+def block_major(panels, group=16):
+    panel_count, vector_part, block_count, entry_part = panels.shape
+    group = min(group, block_count)
+    return pl.pallas_call(
+        block_major_kernel,
+        grid=(block_count // group,),
+        out_shape=jax.ShapeDtypeStruct(
+            (block_count, panel_count * vector_part, entry_part), panels.dtype
+        ),
+        in_specs=[pl.BlockSpec((panel_count, vector_part, group, entry_part), lambda g: (0, 0, g, 0))],
+        out_specs=pl.BlockSpec((group, panel_count * vector_part, entry_part), lambda g: (g, 0, 0)),
+    )(panels)
+
+
 def factor_inverse(gram_matrix):
     lower_factor = jnp.linalg.cholesky(gram_matrix)
     identity = jnp.broadcast_to(
@@ -85,7 +105,7 @@
     block_len = earlier.shape[2]
     panel_count = panels.shape[0]
     vector_part = panels.shape[1]
-    outgoing = panels.transpose(2, 0, 1, 3).reshape(panels.shape[2], -1, panels.shape[3])
+    outgoing = block_major(panels)
     panels_arrived = send(outgoing)
     further_arrived = send(further.transpose(1, 0, 2))
     finished = []

time: 108 us -> 107 us (level)
  local copies, waits for them, and re-layouts: 11.5 us -> 7.14 us
  Pallas kernels: 12.9 us -> 15.9 us
    reshape x1 -> x0, local copies, waits for them, and re-layouts: 4.36 us -> none  [per_device(): panels.transpose(2, 0, 1, 3).reshape(panels.shape[2], -1, panels.shape[3])]
    pallas_call x0 -> x1, Pallas kernels: none -> 2.99 us  [block_major(): pl.pallas_call(block_major_kernel, grid=(block_count // group,), out_shap...]
    reshape x1 -> x3, local copies, waits for them, and re-layouts: 1.92 us -> 3.22 us  [split_by_source(): received.reshape(lat_count, mode_count, received.shape[1], received.shape...]
    transpose x2 -> x0, local copies, waits for them, and re-layouts: 1.3 us -> none  [arrange(): whole = by_source.transpose(1, 2, 0, 3)]
where the time goes in v11:
time: 107 us
  waiting for transfers between devices  53.5 us (50%)
  Pallas kernels  15.9 us (15%)
  starting transfers between devices  11.4 us (11%)
  other arithmetic  10.4 us (10%)
  matrix products  7.48 us (7%)
  local copies, waits for them, and re-layouts  7.14 us (7%)
    all_to_all x2, waiting for transfers between devices, send(): lax.all_to_all(block_major, ('lat', 'mode'), split_axis=0, concat_axis=0,...  53.5 us
    pallas_call x2, Pallas kernels, project_call(): pl.pallas_call(functools.partial(project_kernel, piece_count=len(pieces),...  12.9 us
    all_to_all x2, starting transfers between devices, send(): lax.all_to_all(block_major, ('lat', 'mode'), split_axis=0, concat_axis=0,...  11.4 us
    dot_general x3, matrix products, per_device(): jnp.einsum('nbl,pbl->pbn', basis_part, further_blocks, preferred_element_...  4.92 us
    another operation x6, other arithmetic, factor_inverse(): lower_factor = jnp.linalg.cholesky(gram_matrix)  4.31 us
    another operation x4, other arithmetic, factor_inverse(): lax.linalg.triangular_solve(lower_factor, identity, left_side=True, lower...  3.75 us
    reshape x3, local copies, waits for them, and re-layouts, split_by_source(): received.reshape(lat_count, mode_count, received.shape[1], received.shape...  3.22 us
    unnamed x6, local copies, waits for them, and re-layouts  3 us
  transfers between devices with their start and end apart: 2, of which 2 were waited for; matrix products, arithmetic and copies ran while one was open for 16% of the time, Pallas kernels for 12%

profile of v11, /device:TPU:0, one launch (start us, length us, event | category | flops | bytes accessed | tf_op | source)
XLA Modules:
  0.0 106.6 jit_solution(4961271096576192470)
XLA Ops:
  0.6 3.0 %shard_map.50 = bf16[32,8,4608]{2,1,0:T(8,128)(2,1)} custom-call(bf16[2,4,32,4608]{3,2,1,0:T(8,128)(2,1)} %panels_ref.1), custom_call_target="tpu_custom_call" | custom-call | tf_op jit(solution)/shard_map/pallas_call | solution.py:59
  3.6 7.3 %all-to-all-start = ((bf16[32,8,4608]{2,1,0:T(8,128)(2,1)}), bf16[32,8,4608]{2,1,0:T(8,128)(2,1)S(1)}, u32[]{:S(2)}, u32[]{:S(2)}) async-start(bf16[32,8,4608]{2,1,0:T(8,128)(2,1)} %shard_map.50), calls=%async_computation | async-start | bytes 4718592 | tf_op jit(solution)/shard_map/all_to_all | solution.py:79
  10.9 2.0 %copy.27 = bf16[4,32,4608]{2,0,1:T(4,128)(2,1)} copy(bf16[4,32,4608]{2,1,0:T(8,128)(2,1)S(1)} %copy-done) | data formatting | bytes 2359296 | tf_op args[2]
  12.9 52.6 %all-to-all-done = bf16[32,8,4608]{2,1,0:T(8,128)(2,1)S(1)} async-done(((bf16[32,8,4608]{2,1,0:T(8,128)(2,1)}), bf16[32,8,4608]{2,1,0:T(8,128)(2,1)S(1)}, u32[]{:S(2)}, u32[]{:S(2)}) %all-to-all-start) | async-done | bytes 2359328 | tf_op jit(solution)/shard_map/all_to_all | solution.py:79
  65.5 4.1 %all-to-all-start.1 = ((bf16[32,4,4608]{2,1,0:T(4,128)(2,1)}), bf16[32,4,4608]{2,1,0:T(4,128)(2,1)}, u32[]{:S(2)}, u32[]{:S(2)}) async-start(bf16[32,4,4608]{2,1,0:T(4,128)(2,1)} %bitcast.70), calls=%async_computation.1 | async-start | bytes 2359296 | tf_op jit(solution)/shard_map/all_to_all | solution.py:79
  69.6 0.8 fusion.28
  70.4 0.7 copy.18
  71.0 0.3 copy.24
  71.4 0.7 copy.16
  72.0 0.3 copy.23
  72.4 6.8 %shard_map.51 = (bf16[16,36864]{1,0:T(8,128)(2,1)S(1)}, f32[16,16]{1,0:T(8,128)S(1)}) custom-call(bf16[64,36864]{1,0:T(8,128)(2,1)} %bitcast.75, bf16[16,36864]{1,0:T(8,128)(2,1)S(1)} %bitcast.74), custom_call_target="tpu_custom_call" | custom-call | flops 169869312 | bytes 7078912 | tf_op jit(solution)/shard_map/pallas_call | solution.py:33
  79.3 1.5 %cholesky.44 = f32[16,16]{1,0:T(8,128)S(1)} custom-call(f32[16,16]{1,0:T(8,128)S(1)} %fusion.26), custom_call_target="Cholesky" | custom-call | tf_op jit(solution)/shard_map/jit(cholesky)/cholesky | solution.py:71
  80.8 0.6 compare_reduce_fusion.1
  81.4 0.6 fusion.21
  82.1 1.2 %custom-call.6 = f32[1,16,16]{1,2,0:T(8,128)S(1)} custom-call(f32[1,16,16]{2,1,0:T(8,128)S(1)} %fusion.21), custom_call_target="InvertDiagBlocksLowerTriangular" | custom-call | tf_op jit(solution)/shard_map/triangular_solve/custom-call.0 | solution.py:75
  83.3 0.2 fusion.19
  83.5 1.1 %convolution_convert_fusion.1.refs_1_ = bf16[16,36864]{1,0:T(8,128)(2,1)S(1)} fusion(f32[16,16]{1,0:T(8,128)S(1)} %fusion.19, bf16[16,36864]{1,0:T(8,128)(2,1)S(1)} %get-tuple-element.13), kind=kOutput, calls=%fused_computation.1 | convolution fusion | flops 113836032 | bytes 2360320 | tf_op jit(solution)/shard_map/dot_general | solution.py:100
  84.6 6.1 %shard_map.52 = (bf16[16,36864]{1,0:T(8,128)(2,1)S(1)}, f32[16,16]{1,0:T(8,128)S(1)}) custom-call(bf16[64,36864]{1,0:T(8,128)(2,1)} %bitcast.76, bf16[16,36864]{1,0:T(8,128)(2,1)S(1)} %convolution_convert_fusion.1.refs_1_, bf16[16,36864]{1,0:T(8,128)(2,1)S(1)} %bitcast.73), custom_call_target="tpu_custom_call" | custom-call | flops 207618048 | bytes 8258560 | tf_op jit(solution)/shard_map/pallas_call | solution.py:33
  90.8 1.5 %cholesky.55 = f32[16,16]{1,0:T(8,128)S(1)} custom-call(f32[16,16]{1,0:T(8,128)S(1)} %fusion.24), custom_call_target="Cholesky" | custom-call | tf_op jit(solution)/shard_map/jit(cholesky)/cholesky | solution.py:71
  92.3 0.6 compare_reduce_fusion
  92.9 0.6 fusion.22
  93.6 1.2 %custom-call.7 = f32[1,16,16]{1,2,0:T(8,128)S(1)} custom-call(f32[1,16,16]{2,1,0:T(8,128)S(1)} %fusion.22), custom_call_target="InvertDiagBlocksLowerTriangular" | custom-call | tf_op jit(solution)/shard_map/triangular_solve/custom-call.0 | solution.py:75
  94.8 0.2 fusion.17
  95.0 1.1 %convolution_convert_fusion = bf16[16,36864]{1,0:T(8,128)(2,1)S(1)} fusion(f32[16,16]{1,0:T(8,128)S(1)} %fusion.17, bf16[16,36864]{1,0:T(8,128)(2,1)S(1)} %get-tuple-element.15), kind=kOutput, calls=%fused_computation | convolution fusion | flops 113836032 | bytes 2360320 | tf_op jit(solution)/shard_map/dot_general | solution.py:100
  96.1 1.6 %pad_maximum_fusion = bf16[2,16,1,36864]{3,1,2,0:T(8,128)(2,1)} fusion(bf16[1,16,1,36864]{3,1,2,0:T(8,128)(2,1)S(1)} %bitcast.80, bf16[1,16,1,36864]{3,1,2,0:T(8,128)(2,1)S(1)} %bitcast.71), kind=kLoop, calls=%fused_computation.2 | loop fusion | flops 1179648 | bytes 4718592 | tf_op jit(solution)/shard_map/stack | solution.py:115
  97.7 1.0 all-to-all-done.1
  98.7 1.9 %copy.21 = bf16[8,4,4,4608]{3,0,2,1:T(8,128)(2,1)S(1)} copy(bf16[8,4,4,4608]{3,2,1,0:T(4,128)(2,1)} %bitcast.16) | data formatting | bytes 2359296 | tf_op jit(solution)/shard_map/reshape | solution.py:85
  100.6 0.3 copy.25
  100.9 3.7 %fusion.4 = f32[16,1,64]{2,0,1:T(8,128)S(1)} fusion(bf16[16,36864]{1,0:T(8,128)(2,1)S(1)} %bitcast.77, bf16[64,1,36864]{2,0,1:T(8,128)(2,1)} %param.6), kind=kOutput, calls=%fused_computation.9 | convolution fusion | flops 75498496 | bytes 5902336 | tf_op jit(solution)/shard_map/nbl,pbl->pbn/dot_general | solution.py:123
  104.6 0.6 fusion.14
  105.2 0.6 fusion.8
  105.9 0.7 pad_maximum_fusion.1
  (8 shorter events, 0.2 us)
Async XLA Ops:
  3.6 7.3 %copy-start = (bf16[4,32,4608]{2,1,0:T(8,128)(2,1)S(1)}, bf16[4,32,4608]{2,1,0:T(8,128)(2,1)}, u32[]{:S(2)}) copy-start(bf16[4,32,4608]{2,1,0:T(8,128)(2,1)} %param.8) | copy-start | bytes 3538948
  3.6 61.8 %all-to-all-start = ((bf16[32,8,4608]{2,1,0:T(8,128)(2,1)}), bf16[32,8,4608]{2,1,0:T(8,128)(2,1)S(1)}, u32[]{:S(2)}, u32[]{:S(2)}) async-start(bf16[32,8,4608]{2,1,0:T(8,128)(2,1)} %shard_map.50), calls=%async_computation | async-start | bytes 4718592 | tf_op jit(solution)/shard_map/all_to_all | solution.py:79
  65.5 33.2 %all-to-all-start.1 = ((bf16[32,4,4608]{2,1,0:T(4,128)(2,1)}), bf16[32,4,4608]{2,1,0:T(4,128)(2,1)}, u32[]{:S(2)}, u32[]{:S(2)}) async-start(bf16[32,4,4608]{2,1,0:T(4,128)(2,1)} %bitcast.70), calls=%async_computation.1 | async-start | bytes 2359296 | tf_op jit(solution)/shard_map/all_to_all | solution.py:79

commit v12 on v11

--- a/solution.py
+++ b/solution.py
@@ -67,6 +67,27 @@
     )(panels)
 
 
+def by_vector_kernel(received_ref, out_ref, *, lat_count, mode_count, entry_part):
+    for lat_index in range(lat_count):
+        rows = received_ref[lat_index * mode_count:(lat_index + 1) * mode_count]
+        out_ref[:, lat_index * entry_part:(lat_index + 1) * entry_part] = rows.reshape(-1, entry_part)
+
+
+def by_vector(received):
+    lat_count = lax.axis_size("lat")
+    mode_count = lax.axis_size("mode")
+    _, vector_part, entry_part = received.shape
+    kernel = functools.partial(
+        by_vector_kernel, lat_count=lat_count, mode_count=mode_count, entry_part=entry_part
+    )
+    return pl.pallas_call(
+        kernel,
+        out_shape=jax.ShapeDtypeStruct(
+            (mode_count * vector_part, lat_count * entry_part), received.dtype
+        ),
+    )(received)
+
+
 def factor_inverse(gram_matrix):
     lower_factor = jnp.linalg.cholesky(gram_matrix)
     identity = jnp.broadcast_to(
@@ -116,7 +137,7 @@
     new_basis, finished, further_arrived = lax.optimization_barrier(
         (new_basis, finished, further_arrived)
     )
-    further_blocks = arrange(further_arrived)
+    further_blocks = by_vector(further_arrived)[:, None, :]
     products = []
     for basis_part in [earlier] + finished:
         products.append(

time: 107 us -> 108 us (level)
  Pallas kernels: 15.9 us -> 18.3 us
  local copies, waits for them, and re-layouts: 7.14 us -> 4.87 us
    pallas_call x0 -> x1, Pallas kernels: none -> 2.45 us  [by_vector(): pl.pallas_call(kernel, out_shape=jax.ShapeDtypeStruct((mode_count * vecto...]
    reshape x3 -> x2, local copies, waits for them, and re-layouts: 3.22 us -> 1.3 us  [split_by_source(): received.reshape(lat_count, mode_count, received.shape[1], received.shape...]
    unnamed x6 -> x7, local copies, waits for them, and re-layouts: 3 us -> 2.66 us
where the time goes in v12:
time: 108 us; the launch traced here: 107 us
  waiting for transfers between devices  53.5 us (50%)
  Pallas kernels  18.3 us (17%)
  starting transfers between devices  11.4 us (11%)
  other arithmetic  10.4 us (10%)
  matrix products  7.93 us (7%)
  local copies, waits for them, and re-layouts  4.87 us (5%)
    all_to_all x2, waiting for transfers between devices, send(): lax.all_to_all(block_major, ('lat', 'mode'), split_axis=0, concat_axis=0,...  53.5 us
    pallas_call x2, Pallas kernels, project_call(): pl.pallas_call(functools.partial(project_kernel, piece_count=len(pieces),...  12.9 us
    all_to_all x2, starting transfers between devices, send(): lax.all_to_all(block_major, ('lat', 'mode'), split_axis=0, concat_axis=0,...  11.4 us
    dot_general x3, matrix products, per_device(): jnp.einsum('nbl,pbl->pbn', basis_part, further_blocks, preferred_element_...  5.36 us
    another operation x6, other arithmetic, factor_inverse(): lower_factor = jnp.linalg.cholesky(gram_matrix)  4.31 us
    another operation x4, other arithmetic, factor_inverse(): lax.linalg.triangular_solve(lower_factor, identity, left_side=True, lower...  3.75 us
    pallas_call x1, Pallas kernels, block_major(): pl.pallas_call(block_major_kernel, grid=(block_count // group,), out_shap...  2.99 us
    unnamed x7, local copies, waits for them, and re-layouts  2.66 us
  transfers between devices with their start and end apart: 2, of which 2 were waited for; matrix products, arithmetic and copies ran while one was open for 16% of the time, Pallas kernels for 12%

profile of v12, /device:TPU:0, one launch (start us, length us, event | category | flops | bytes accessed | tf_op | source)
XLA Modules:
  0.0 107.2 jit_solution(12565099043393304602)
XLA Ops:
  0.6 3.0 %shard_map.50 = bf16[32,8,4608]{2,1,0:T(8,128)(2,1)} custom-call(bf16[2,4,32,4608]{3,2,1,0:T(8,128)(2,1)} %panels_ref.1), custom_call_target="tpu_custom_call" | custom-call | tf_op jit(solution)/shard_map/pallas_call | solution.py:59
  3.6 7.3 %all-to-all-start = ((bf16[32,8,4608]{2,1,0:T(8,128)(2,1)}), bf16[32,8,4608]{2,1,0:T(8,128)(2,1)S(1)}, u32[]{:S(2)}, u32[]{:S(2)}) async-start(bf16[32,8,4608]{2,1,0:T(8,128)(2,1)} %shard_map.50), calls=%async_computation | async-start | bytes 4718592 | tf_op jit(solution)/shard_map/all_to_all | solution.py:100
  10.9 2.0 %copy.14 = bf16[4,32,4608]{2,0,1:T(4,128)(2,1)} copy(bf16[4,32,4608]{2,1,0:T(8,128)(2,1)S(1)} %copy-done.1) | data formatting | bytes 2359296 | tf_op args[2]
  12.9 52.6 %all-to-all-done = bf16[32,8,4608]{2,1,0:T(8,128)(2,1)S(1)} async-done(((bf16[32,8,4608]{2,1,0:T(8,128)(2,1)}), bf16[32,8,4608]{2,1,0:T(8,128)(2,1)S(1)}, u32[]{:S(2)}, u32[]{:S(2)}) %all-to-all-start) | async-done | bytes 2359328 | tf_op jit(solution)/shard_map/all_to_all | solution.py:100
  65.5 4.1 %all-to-all-start.1 = ((bf16[32,4,4608]{2,1,0:T(4,128)(2,1)}), bf16[32,4,4608]{2,1,0:T(4,128)(2,1)}, u32[]{:S(2)}, u32[]{:S(2)}) async-start(bf16[32,4,4608]{2,1,0:T(4,128)(2,1)} %bitcast.65), calls=%async_computation.1 | async-start | bytes 2359296 | tf_op jit(solution)/shard_map/all_to_all | solution.py:100
  69.6 0.8 fusion.28
  70.4 0.7 copy.7
  71.0 0.3 copy.12
  71.4 0.7 copy.5
  72.0 0.3 copy.11
  72.4 6.8 %shard_map.51 = (bf16[16,36864]{1,0:T(8,128)(2,1)S(1)}, f32[16,16]{1,0:T(8,128)S(1)}) custom-call(bf16[64,36864]{1,0:T(8,128)(2,1)} %bitcast.70, bf16[16,36864]{1,0:T(8,128)(2,1)S(1)} %bitcast.69), custom_call_target="tpu_custom_call" | custom-call | flops 169869312 | bytes 7078912 | tf_op jit(solution)/shard_map/pallas_call | solution.py:33
  79.3 1.5 %cholesky.44 = f32[16,16]{1,0:T(8,128)S(1)} custom-call(f32[16,16]{1,0:T(8,128)S(1)} %fusion.26), custom_call_target="Cholesky" | custom-call | tf_op jit(solution)/shard_map/jit(cholesky)/cholesky | solution.py:92
  80.8 0.6 compare_reduce_fusion.1
  81.4 0.6 fusion.21
  82.1 1.2 %custom-call.6 = f32[1,16,16]{1,2,0:T(8,128)S(1)} custom-call(f32[1,16,16]{2,1,0:T(8,128)S(1)} %fusion.21), custom_call_target="InvertDiagBlocksLowerTriangular" | custom-call | tf_op jit(solution)/shard_map/triangular_solve/custom-call.0 | solution.py:96
  83.3 0.2 fusion.19
  83.5 1.1 %convolution_convert_fusion.1.refs_1_ = bf16[16,36864]{1,0:T(8,128)(2,1)S(1)} fusion(f32[16,16]{1,0:T(8,128)S(1)} %fusion.19, bf16[16,36864]{1,0:T(8,128)(2,1)S(1)} %get-tuple-element.13), kind=kOutput, calls=%fused_computation.1 | convolution fusion | flops 113836032 | bytes 2360320 | tf_op jit(solution)/shard_map/dot_general | solution.py:121
  84.6 6.1 %shard_map.52 = (bf16[16,36864]{1,0:T(8,128)(2,1)S(1)}, f32[16,16]{1,0:T(8,128)S(1)}) custom-call(bf16[64,36864]{1,0:T(8,128)(2,1)} %bitcast.71, bf16[16,36864]{1,0:T(8,128)(2,1)S(1)} %convolution_convert_fusion.1.refs_1_, bf16[16,36864]{1,0:T(8,128)(2,1)S(1)} %bitcast.68), custom_call_target="tpu_custom_call" | custom-call | flops 207618048 | bytes 8258560 | tf_op jit(solution)/shard_map/pallas_call | solution.py:33
  90.7 0.1 copy.8
  90.8 1.5 %cholesky.55 = f32[16,16]{1,0:T(8,128)S(1)} custom-call(f32[16,16]{1,0:T(8,128)S(1)} %fusion.24), custom_call_target="Cholesky" | custom-call | tf_op jit(solution)/shard_map/jit(cholesky)/cholesky | solution.py:92
  92.3 0.6 compare_reduce_fusion
  92.9 0.6 fusion.22
  93.6 1.2 %custom-call.7 = f32[1,16,16]{1,2,0:T(8,128)S(1)} custom-call(f32[1,16,16]{2,1,0:T(8,128)S(1)} %fusion.22), custom_call_target="InvertDiagBlocksLowerTriangular" | custom-call | tf_op jit(solution)/shard_map/triangular_solve/custom-call.0 | solution.py:96
  94.8 0.2 fusion.17
  95.0 1.1 %convolution_convert_fusion = bf16[16,36864]{1,0:T(8,128)(2,1)S(1)} fusion(f32[16,16]{1,0:T(8,128)S(1)} %fusion.17, bf16[16,36864]{1,0:T(8,128)(2,1)S(1)} %get-tuple-element.15), kind=kOutput, calls=%fused_computation | convolution fusion | flops 113836032 | bytes 2360320 | tf_op jit(solution)/shard_map/dot_general | solution.py:121
  96.1 1.6 %pad_maximum_fusion = bf16[2,16,1,36864]{3,1,2,0:T(8,128)(2,1)} fusion(bf16[1,16,1,36864]{3,1,2,0:T(8,128)(2,1)S(1)} %bitcast.72, bf16[1,16,1,36864]{3,1,2,0:T(8,128)(2,1)S(1)} %bitcast.66), kind=kLoop, calls=%fused_computation.2 | loop fusion | flops 1179648 | bytes 4718592 | tf_op jit(solution)/shard_map/stack | solution.py:136
  97.7 1.0 all-to-all-done.1.received_ref
  98.7 2.4 %shard_map.53 = bf16[16,36864]{1,0:T(8,128)(2,1)} custom-call(bf16[32,4,4608]{2,1,0:T(4,128)(2,1)} %all-to-all-done.1.received_ref), custom_call_target="tpu_custom_call" | custom-call | tf_op jit(solution)/shard_map/pallas_call | solution.py:83
  101.1 4.1 %fusion.4 = f32[16,1,64]{2,0,1:T(8,128)S(1)} fusion(bf16[16,36864]{1,0:T(8,128)(2,1)} %shard_map.53, bf16[64,1,36864]{2,0,1:T(8,128)(2,1)} %param.6), kind=kOutput, calls=%fused_computation.9 | convolution fusion | flops 75498496 | bytes 5902336 | tf_op jit(solution)/shard_map/nbl,pbl->pbn/dot_general | solution.py:144
  105.2 0.6 fusion.14
  105.8 0.6 fusion.8
  106.5 0.7 pad_maximum_fusion.1
  (9 shorter events, 0.2 us)
Async XLA Ops:
  3.6 7.3 %copy-start.1 = (bf16[4,32,4608]{2,1,0:T(8,128)(2,1)S(1)}, bf16[4,32,4608]{2,1,0:T(8,128)(2,1)}, u32[]{:S(2)}) copy-start(bf16[4,32,4608]{2,1,0:T(8,128)(2,1)} %param.8) | copy-start | bytes 3538948
  3.6 61.8 %all-to-all-start = ((bf16[32,8,4608]{2,1,0:T(8,128)(2,1)}), bf16[32,8,4608]{2,1,0:T(8,128)(2,1)S(1)}, u32[]{:S(2)}, u32[]{:S(2)}) async-start(bf16[32,8,4608]{2,1,0:T(8,128)(2,1)} %shard_map.50), calls=%async_computation | async-start | bytes 4718592 | tf_op jit(solution)/shard_map/all_to_all | solution.py:100
  65.5 33.2 %all-to-all-start.1 = ((bf16[32,4,4608]{2,1,0:T(4,128)(2,1)}), bf16[32,4,4608]{2,1,0:T(4,128)(2,1)}, u32[]{:S(2)}, u32[]{:S(2)}) async-start(bf16[32,4,4608]{2,1,0:T(4,128)(2,1)} %bitcast.65), calls=%async_computation.1 | async-start | bytes 2359296 | tf_op jit(solution)/shard_map/all_to_all | solution.py:100
  101.1 4.1 %copy-start = (bf16[16,36864]{1,0:T(8,128)(2,1)S(1)}, bf16[16,36864]{1,0:T(8,128)(2,1)}, u32[]{:S(2)}) copy-start(bf16[16,36864]{1,0:T(8,128)(2,1)} %shard_map.53) | copy-start | bytes 3538948

commit v13 on v11

--- a/solution.py
+++ b/solution.py
@@ -117,14 +117,14 @@
         (new_basis, finished, further_arrived)
     )
     further_blocks = arrange(further_arrived)
-    products = []
-    for basis_part in [earlier] + finished:
-        products.append(
-            jnp.einsum(
-                "nbl,pbl->pbn", basis_part, further_blocks, preferred_element_type=jnp.float32
-            )
-            / block_len
-        )
+    earlier_part = jnp.einsum(
+        "nbl,pbl->pbn", earlier, further_blocks, preferred_element_type=jnp.float32
+    )
+    new_part = jnp.einsum(
+        "knbl,pbl->pbkn", new_basis, further_blocks, preferred_element_type=jnp.float32
+    )
+    new_part = new_part.reshape(new_part.shape[0], new_part.shape[1], -1)
+    products = [earlier_part / block_len, new_part / block_len]
     coarse = jnp.concatenate(products, axis=2)
     return (new_basis, coarse)
 

time: 107 us -> 108 us (level)
  other arithmetic: 10.4 us -> 13 us
    another operation x6, other arithmetic: 4.31 us -> 5.64 us  [factor_inverse(): lower_factor = jnp.linalg.cholesky(gram_matrix)]
    reshape x3, local copies, waits for them, and re-layouts: 3.22 us -> 1.96 us  [split_by_source(): received.reshape(lat_count, mode_count, received.shape[1], received.shape...]
    div x2, other arithmetic: 0.02 us -> 1.26 us  [factor_inverse(): lower_factor = jnp.linalg.cholesky(gram_matrix)]
    dot_general x3 -> x2, matrix products: 4.92 us -> 4.54 us  [the longest x1 3.81 us: per_device(): jnp.einsum('nbl,pbl->pbn', earlier, further_blocks, preferred_element_typ...]
    unnamed x6 -> x10, local copies, waits for them, and re-layouts: 3 us -> 2.98 us
  transfers between devices with their start and end apart: 2 -> 2, of which waited for: 2 -> 1; matrix products, arithmetic and copies ran while one was open for 16% -> 19% of each run, Pallas kernels for 12% -> 12%
where the time goes in v13:
time: 108 us
  waiting for transfers between devices  52.6 us (49%)
  Pallas kernels  16 us (15%)
  other arithmetic  13 us (12%)
  starting transfers between devices  11.3 us (10%)
  matrix products  7.09 us (7%)
  local copies, waits for them, and re-layouts  6.86 us (6%)
    all_to_all x2, waiting for transfers between devices, send(): lax.all_to_all(block_major, ('lat', 'mode'), split_axis=0, concat_axis=0,...  52.6 us
    pallas_call x2, Pallas kernels, project_call(): pl.pallas_call(functools.partial(project_kernel, piece_count=len(pieces),...  13 us
    all_to_all x2, starting transfers between devices, send(): lax.all_to_all(block_major, ('lat', 'mode'), split_axis=0, concat_axis=0,...  11.3 us
    another operation x6, other arithmetic, factor_inverse(): lower_factor = jnp.linalg.cholesky(gram_matrix)  5.64 us
    dot_general x1, matrix products, per_device(): jnp.einsum('nbl,pbl->pbn', earlier, further_blocks, preferred_element_typ...  3.81 us
    another operation x4, other arithmetic, factor_inverse(): lax.linalg.triangular_solve(lower_factor, identity, left_side=True, lower...  3.75 us
    pallas_call x1, Pallas kernels, block_major(): pl.pallas_call(block_major_kernel, grid=(block_count // group,), out_shap...  2.99 us
    unnamed x10, local copies, waits for them, and re-layouts  2.98 us
  transfers between devices with their start and end apart: 2, of which 1 were waited for; matrix products, arithmetic and copies ran while one was open for 19% of the time, Pallas kernels for 12%

profile of v13, /device:TPU:0, one launch (start us, length us, event | category | flops | bytes accessed | tf_op | source)
XLA Modules:
  0.0 107.5 jit_solution(12218464353912957369)
XLA Ops:
  0.6 3.0 %shard_map.50 = bf16[32,8,4608]{2,1,0:T(8,128)(2,1)} custom-call(bf16[2,4,32,4608]{3,2,1,0:T(8,128)(2,1)} %panels_ref.1), custom_call_target="tpu_custom_call" | custom-call | tf_op jit(solution)/shard_map/pallas_call | solution.py:59
  3.6 7.3 %all-to-all-start = ((bf16[32,8,4608]{2,1,0:T(8,128)(2,1)}), bf16[32,8,4608]{2,1,0:T(8,128)(2,1)S(1)}, u32[]{:S(2)}, u32[]{:S(2)}) async-start(bf16[32,8,4608]{2,1,0:T(8,128)(2,1)} %shard_map.50), calls=%async_computation | async-start | bytes 4718592 | tf_op jit(solution)/shard_map/all_to_all | solution.py:79
  10.9 1.9 %copy.27 = bf16[4,32,4608]{2,0,1:T(4,128)(2,1)} copy(bf16[4,32,4608]{2,1,0:T(8,128)(2,1)S(1)} %copy-done.2) | data formatting | bytes 2359296 | tf_op args[2]
  12.9 52.6 %all-to-all-done = bf16[32,8,4608]{2,1,0:T(8,128)(2,1)S(1)} async-done(((bf16[32,8,4608]{2,1,0:T(8,128)(2,1)}), bf16[32,8,4608]{2,1,0:T(8,128)(2,1)S(1)}, u32[]{:S(2)}, u32[]{:S(2)}) %all-to-all-start) | async-done | bytes 2359328 | tf_op jit(solution)/shard_map/all_to_all | solution.py:79
  65.5 4.0 %all-to-all-start.1 = ((bf16[32,4,4608]{2,1,0:T(4,128)(2,1)}), bf16[32,4,4608]{2,1,0:T(4,128)(2,1)S(1)}, u32[]{:S(2)}, u32[]{:S(2)}) async-start(bf16[32,4,4608]{2,1,0:T(4,128)(2,1)} %bitcast.54), calls=%async_computation.1 | async-start | bytes 2359296 | tf_op jit(solution)/shard_map/all_to_all | solution.py:79
  69.5 1.8 %fusion.14 = (bf16[32,4,4608]{2,1,0:T(4,128)(2,1)}, bf16[32,4,4608]{2,1,0:T(4,128)(2,1)S(1)}) fusion(bf16[32,8,4608]{2,1,0:T(8,128)(2,1)S(1)} %all-to-all-done), kind=kLoop, calls=%fused_computation.31 | loop fusion | bytes 4718592 | tf_op jit(solution)/shard_map/slice | solution.py:113
  71.2 0.7 copy.16
  71.9 0.3 copy.23
  72.3 6.9 %shard_map.51 = (bf16[16,36864]{1,0:T(8,128)(2,1)S(1)}, f32[16,16]{1,0:T(8,128)S(1)}) custom-call(bf16[64,36864]{1,0:T(8,128)(2,1)} %bitcast.58, bf16[16,36864]{1,0:T(8,128)(2,1)S(1)} %bitcast.57), custom_call_target="tpu_custom_call" | custom-call | flops 169869312 | bytes 7078912 | tf_op jit(solution)/shard_map/pallas_call | solution.py:33
  79.2 0.6 fusion.12
  79.9 2.1 %cholesky.44 = f32[16,16]{1,0:T(8,128)S(1)} custom-call(f32[16,16]{1,0:T(8,128)} %fusion.12), custom_call_target="Cholesky" | custom-call | tf_op jit(solution)/shard_map/jit(cholesky)/cholesky | solution.py:71
  82.1 0.6 compare_reduce_fusion.1
  82.7 0.6 fusion.7
  83.4 1.2 %custom-call.6 = f32[1,16,16]{1,2,0:T(8,128)S(1)} custom-call(f32[1,16,16]{2,1,0:T(8,128)S(1)} %fusion.7), custom_call_target="InvertDiagBlocksLowerTriangular" | custom-call | tf_op jit(solution)/shard_map/triangular_solve/custom-call.0 | solution.py:75
  84.6 0.2 fusion.5
  84.8 0.7 copy.18
  85.5 0.3 copy.24
  85.8 1.1 convolution_convert_fusion.1.refs_1_
  86.9 6.1 %shard_map.52 = (bf16[16,36864]{1,0:T(8,128)(2,1)S(1)}, f32[16,16]{1,0:T(8,128)S(1)}) custom-call(bf16[64,36864]{1,0:T(8,128)(2,1)} %bitcast.59, bf16[16,36864]{1,0:T(8,128)(2,1)S(1)} %convolution_convert_fusion.1.refs_1_, bf16[16,36864]{1,0:T(8,128)(2,1)S(1)} %bitcast.56), custom_call_target="tpu_custom_call" | custom-call | flops 207618048 | bytes 8258560 | tf_op jit(solution)/shard_map/pallas_call | solution.py:33
  93.0 0.6 fusion.10
  93.6 2.1 %cholesky.55 = f32[16,16]{1,0:T(8,128)S(1)} custom-call(f32[16,16]{1,0:T(8,128)} %fusion.10), custom_call_target="Cholesky" | custom-call | tf_op jit(solution)/shard_map/jit(cholesky)/cholesky | solution.py:71
  95.8 0.6 compare_reduce_fusion
  96.5 0.6 fusion.8
  97.1 1.2 %custom-call.7 = f32[1,16,16]{1,2,0:T(8,128)S(1)} custom-call(f32[1,16,16]{2,1,0:T(8,128)S(1)} %fusion.8), custom_call_target="InvertDiagBlocksLowerTriangular" | custom-call | tf_op jit(solution)/shard_map/triangular_solve/custom-call.0 | solution.py:75
  98.4 0.2 fusion.3
  98.6 1.1 %fusion = bf16[1,16,1,36864]{3,1,2,0:T(8,128)(2,1)S(1)} fusion(f32[16,16]{1,0:T(8,128)S(1)} %fusion.3, bf16[16,36864]{1,0:T(8,128)(2,1)S(1)} %get-tuple-element.13), kind=kOutput, calls=%fused_computation.2 | convolution fusion | flops 113836032 | bytes 2360320 | tf_op jit(solution)/shard_map/dot_general | solution.py:100
  99.6 1.6 %pad_maximum_fusion = bf16[2,16,1,36864]{3,1,2,0:T(8,128)(2,1)} fusion(bf16[1,16,1,36864]{3,1,2,0:T(8,128)(2,1)S(1)} %fusion, bf16[1,16,1,36864]{3,1,2,0:T(8,128)(2,1)S(1)} %bitcast.55), kind=kLoop, calls=%fused_computation.3 | loop fusion | flops 1179648 | bytes 4718592 | tf_op jit(solution)/shard_map/stack | solution.py:115
  101.3 0.7 copy.21
  101.9 0.3 copy.25
  102.3 3.8 %fusion.2 = f32[16,1,64]{2,0,1:T(8,128)S(1)} fusion(bf16[16,36864]{1,0:T(8,128)(2,1)S(1)} %bitcast.60, bf16[64,1,36864]{2,0,1:T(8,128)(2,1)} %param.6), kind=kOutput, calls=%fused_computation.8 | convolution fusion | flops 75498496 | bytes 5902336 | tf_op jit(solution)/shard_map/nbl,pbl->pbn/dot_general | solution.py:120
  106.1 0.7 fusion.1
  106.8 0.7 pad_maximum_fusion.1
  (11 shorter events, 0.2 us)
Async XLA Ops:
  3.6 7.3 %copy-start.2 = (bf16[4,32,4608]{2,1,0:T(8,128)(2,1)S(1)}, bf16[4,32,4608]{2,1,0:T(8,128)(2,1)}, u32[]{:S(2)}) copy-start(bf16[4,32,4608]{2,1,0:T(8,128)(2,1)} %param.8) | copy-start | bytes 3538948
  3.6 61.8 %all-to-all-start = ((bf16[32,8,4608]{2,1,0:T(8,128)(2,1)}), bf16[32,8,4608]{2,1,0:T(8,128)(2,1)S(1)}, u32[]{:S(2)}, u32[]{:S(2)}) async-start(bf16[32,8,4608]{2,1,0:T(8,128)(2,1)} %shard_map.50), calls=%async_computation | async-start | bytes 4718592 | tf_op jit(solution)/shard_map/all_to_all | solution.py:79
  65.5 35.8 %all-to-all-start.1 = ((bf16[32,4,4608]{2,1,0:T(4,128)(2,1)}), bf16[32,4,4608]{2,1,0:T(4,128)(2,1)S(1)}, u32[]{:S(2)}, u32[]{:S(2)}) async-start(bf16[32,4,4608]{2,1,0:T(4,128)(2,1)} %bitcast.54), calls=%async_computation.1 | async-start | bytes 2359296 | tf_op jit(solution)/shard_map/all_to_all | solution.py:79
  72.3 12.5 %copy-start.1 = (bf16[32,4,4608]{2,1,0:T(4,128)(2,1)S(1)}, bf16[32,4,4608]{2,1,0:T(4,128)(2,1)}, u32[]{:S(2)}) copy-start(bf16[32,4,4608]{2,1,0:T(4,128)(2,1)} %get-tuple-element.22) | copy-start | bytes 3538948
  102.3 3.8 %copy-start = (bf16[2,16,1,36864]{3,1,2,0:T(8,128)(2,1)S(1)}, bf16[2,16,1,36864]{3,1,2,0:T(8,128)(2,1)}, u32[]{:S(2)}) copy-start(bf16[2,16,1,36864]{3,1,2,0:T(8,128)(2,1)} %pad_maximum_fusion) | copy-start | bytes 7077892

commit v14 on v13

--- a/solution.py
+++ b/solution.py
@@ -67,6 +67,35 @@
     )(panels)
 
 
+def coarse_kernel(received_ref, earlier_ref, fresh_ref, earlier_out, fresh_out, vectors, *,
+                  lat_count, mode_count, entry_part, block_len):
+    for lat_index in range(lat_count):
+        rows = received_ref[lat_index * mode_count:(lat_index + 1) * mode_count]
+        vectors[:, lat_index * entry_part:(lat_index + 1) * entry_part] = rows.reshape(-1, entry_part)
+    further_rows = vectors[...]
+    earlier_out[...] = lax.dot_general(
+        further_rows, earlier_ref[...], NT, preferred_element_type=jnp.float32) / block_len
+    fresh_out[...] = lax.dot_general(
+        further_rows, fresh_ref[...], NT, preferred_element_type=jnp.float32) / block_len
+
+
+def coarse_call(received, earlier_rows, fresh_rows, lat_count, mode_count):
+    _, vector_part, entry_part = received.shape
+    count = mode_count * vector_part
+    block_len = lat_count * entry_part
+    kernel = functools.partial(coarse_kernel, lat_count=lat_count, mode_count=mode_count,
+                               entry_part=entry_part, block_len=block_len)
+    return pl.pallas_call(
+        kernel,
+        out_shape=(
+            jax.ShapeDtypeStruct((count, earlier_rows.shape[0]), jnp.float32),
+            jax.ShapeDtypeStruct((count, fresh_rows.shape[0]), jnp.float32),
+        ),
+        scratch_shapes=[pltpu.VMEM((count, block_len), received.dtype)],
+        compiler_params=pltpu.CompilerParams(vmem_limit_bytes=48 * 1024 * 1024),
+    )(received, earlier_rows, fresh_rows)
+
+
 def factor_inverse(gram_matrix):
     lower_factor = jnp.linalg.cholesky(gram_matrix)
     identity = jnp.broadcast_to(
@@ -116,16 +145,16 @@
     new_basis, finished, further_arrived = lax.optimization_barrier(
         (new_basis, finished, further_arrived)
     )
-    further_blocks = arrange(further_arrived)
-    earlier_part = jnp.einsum(
-        "nbl,pbl->pbn", earlier, further_blocks, preferred_element_type=jnp.float32
+    lat_count = lax.axis_size("lat")
+    mode_count = lax.axis_size("mode")
+    earlier_part, fresh_part = coarse_call(
+        further_arrived,
+        earlier.reshape(earlier.shape[0], block_len),
+        new_basis.reshape(-1, block_len),
+        lat_count,
+        mode_count,
     )
-    new_part = jnp.einsum(
-        "knbl,pbl->pbkn", new_basis, further_blocks, preferred_element_type=jnp.float32
-    )
-    new_part = new_part.reshape(new_part.shape[0], new_part.shape[1], -1)
-    products = [earlier_part / block_len, new_part / block_len]
-    coarse = jnp.concatenate(products, axis=2)
+    coarse = jnp.concatenate([earlier_part, fresh_part], axis=1)[:, None, :]
     return (new_basis, coarse)
 
 

time: 108 us -> 104 us (0.963)
  matrix products: 7.09 us -> 2.55 us
  Pallas kernels: 16 us -> 20.5 us
  other arithmetic: 13 us -> 8.98 us
  waiting for transfers between devices: 52.6 us -> 54.9 us
  local copies, waits for them, and re-layouts: 6.86 us -> 4.89 us
    pallas_call x0 -> x1, Pallas kernels: none -> 4.63 us  [coarse_call(): pl.pallas_call(kernel, out_shape=(jax.ShapeDtypeStruct((count, earlier_ro...]
    dot_general x2 -> x0, matrix products: 4.54 us -> none  [the longest x1 3.81 us: per_device(): jnp.einsum('nbl,pbl->pbn', earlier, further_blocks, preferred_element_typ...]
    all_to_all x2, waiting for transfers between devices: 52.6 us -> 54.9 us  [send(): lax.all_to_all(block_major, ('lat', 'mode'), split_axis=0, concat_axis=0,...]
    another operation x1, other arithmetic: 1.61 us -> 0.22 us  [per_device(): new_basis = jnp.stack(finished, 0)]
    another operation x6, other arithmetic: 5.64 us -> 4.31 us  [factor_inverse(): lower_factor = jnp.linalg.cholesky(gram_matrix)]
    div x2, other arithmetic: 1.26 us -> 0.02 us  [factor_inverse(): lower_factor = jnp.linalg.cholesky(gram_matrix)]
    unnamed x10 -> x7, local copies, waits for them, and re-layouts: 2.98 us -> 2.66 us
  transfers between devices with their start and end apart: 2 -> 2, of which waited for: 1 -> 2; matrix products, arithmetic and copies ran while one was open for 19% -> 15% of each run, Pallas kernels for 12% -> 12%
where the time goes in v14:
time: 104 us
  waiting for transfers between devices  54.9 us (53%)
  Pallas kernels  20.5 us (20%)
  starting transfers between devices  11.4 us (11%)
  other arithmetic  8.98 us (9%)
  local copies, waits for them, and re-layouts  4.89 us (5%)
  matrix products  2.55 us (2%)
    all_to_all x2, waiting for transfers between devices, send(): lax.all_to_all(block_major, ('lat', 'mode'), split_axis=0, concat_axis=0,...  54.9 us
    pallas_call x2, Pallas kernels, project_call(): pl.pallas_call(functools.partial(project_kernel, piece_count=len(pieces),...  12.9 us
    all_to_all x2, starting transfers between devices, send(): lax.all_to_all(block_major, ('lat', 'mode'), split_axis=0, concat_axis=0,...  11.4 us
    pallas_call x1, Pallas kernels, coarse_call(): pl.pallas_call(kernel, out_shape=(jax.ShapeDtypeStruct((count, earlier_ro...  4.63 us
    another operation x6, other arithmetic, factor_inverse(): lower_factor = jnp.linalg.cholesky(gram_matrix)  4.31 us
    another operation x4, other arithmetic, factor_inverse(): lax.linalg.triangular_solve(lower_factor, identity, left_side=True, lower...  3.75 us
    pallas_call x1, Pallas kernels, block_major(): pl.pallas_call(block_major_kernel, grid=(block_count // group,), out_shap...  2.99 us
    unnamed x7, local copies, waits for them, and re-layouts  2.66 us
  transfers between devices with their start and end apart: 2, of which 2 were waited for; matrix products, arithmetic and copies ran while one was open for 15% of the time, Pallas kernels for 12%

profile of v14, /device:TPU:0, one launch (start us, length us, event | category | flops | bytes accessed | tf_op | source)
XLA Modules:
  0.0 104.0 jit_solution(8926093327420335951)
XLA Ops:
  0.6 3.0 %shard_map.50 = bf16[32,8,4608]{2,1,0:T(8,128)(2,1)} custom-call(bf16[2,4,32,4608]{3,2,1,0:T(8,128)(2,1)} %panels_ref.1), custom_call_target="tpu_custom_call" | custom-call | tf_op jit(solution)/shard_map/pallas_call | solution.py:59
  3.6 7.3 %all-to-all-start = ((bf16[32,8,4608]{2,1,0:T(8,128)(2,1)}), bf16[32,8,4608]{2,1,0:T(8,128)(2,1)S(1)}, u32[]{:S(2)}, u32[]{:S(2)}) async-start(bf16[32,8,4608]{2,1,0:T(8,128)(2,1)} %shard_map.50), calls=%async_computation | async-start | bytes 4718592 | tf_op jit(solution)/shard_map/all_to_all | solution.py:108
  10.9 0.0 copy-done.1
  10.9 2.0 %copy.14 = bf16[4,32,4608]{2,0,1:T(4,128)(2,1)} copy(bf16[4,32,4608]{2,1,0:T(8,128)(2,1)S(1)} %copy-done.1) | data formatting | bytes 2359296 | tf_op args[2]
  12.9 52.6 %all-to-all-done = bf16[32,8,4608]{2,1,0:T(8,128)(2,1)S(1)} async-done(((bf16[32,8,4608]{2,1,0:T(8,128)(2,1)}), bf16[32,8,4608]{2,1,0:T(8,128)(2,1)S(1)}, u32[]{:S(2)}, u32[]{:S(2)}) %all-to-all-start) | async-done | bytes 2359328 | tf_op jit(solution)/shard_map/all_to_all | solution.py:108
  65.5 4.1 %all-to-all-start.1 = ((bf16[32,4,4608]{2,1,0:T(4,128)(2,1)}), bf16[32,4,4608]{2,1,0:T(4,128)(2,1)}, u32[]{:S(2)}, u32[]{:S(2)}) async-start(bf16[32,4,4608]{2,1,0:T(4,128)(2,1)} %bitcast.42), calls=%async_computation.1 | async-start | bytes 2359296 | tf_op jit(solution)/shard_map/all_to_all | solution.py:108
  69.6 0.8 fusion.11
  70.4 0.7 copy.5
  71.0 0.3 copy.11
  71.4 6.8 %shard_map.51 = (bf16[16,36864]{1,0:T(8,128)(2,1)S(1)}, f32[16,16]{1,0:T(8,128)S(1)}) custom-call(bf16[64,36864]{1,0:T(8,128)(2,1)} %bitcast.47, bf16[16,36864]{1,0:T(8,128)(2,1)S(1)} %bitcast.46), custom_call_target="tpu_custom_call" | custom-call | flops 169869312 | bytes 7078912 | tf_op jit(solution)/shard_map/pallas_call | solution.py:33
  78.2 0.1 copy.6
  78.3 1.5 %cholesky.44 = f32[16,16]{1,0:T(8,128)S(1)} custom-call(f32[16,16]{1,0:T(8,128)S(1)} %fusion.10), custom_call_target="Cholesky" | custom-call | tf_op jit(solution)/shard_map/jit(cholesky)/cholesky | solution.py:100
  79.8 0.6 compare_reduce_fusion.1
  80.4 0.6 fusion.5
  81.1 1.2 %custom-call.6 = f32[1,16,16]{1,2,0:T(8,128)S(1)} custom-call(f32[1,16,16]{2,1,0:T(8,128)S(1)} %fusion.5), custom_call_target="InvertDiagBlocksLowerTriangular" | custom-call | tf_op jit(solution)/shard_map/triangular_solve/custom-call.0 | solution.py:104
  82.3 0.2 fusion.3
  82.5 0.7 copy.7
  83.2 0.3 copy.12
  83.5 1.1 %convolution_convert_fusion.1.refs_1_ = bf16[16,36864]{1,0:T(8,128)(2,1)S(1)} fusion(f32[16,16]{1,0:T(8,128)S(1)} %fusion.3, bf16[16,36864]{1,0:T(8,128)(2,1)S(1)} %get-tuple-element.13), kind=kOutput, calls=%fused_computation.1 | convolution fusion | flops 113836032 | bytes 2360320 | tf_op jit(solution)/shard_map/dot_general | solution.py:129
  84.6 6.1 %shard_map.52 = (bf16[16,36864]{1,0:T(8,128)(2,1)S(1)}, f32[16,16]{1,0:T(8,128)S(1)}) custom-call(bf16[64,36864]{1,0:T(8,128)(2,1)} %bitcast.48, bf16[16,36864]{1,0:T(8,128)(2,1)S(1)} %convolution_convert_fusion.1.refs_1_, bf16[16,36864]{1,0:T(8,128)(2,1)S(1)} %bitcast.45), custom_call_target="tpu_custom_call" | custom-call | flops 207618048 | bytes 8258560 | tf_op jit(solution)/shard_map/pallas_call | solution.py:33
  90.7 0.1 copy.8
  90.8 1.5 %cholesky.55 = f32[16,16]{1,0:T(8,128)S(1)} custom-call(f32[16,16]{1,0:T(8,128)S(1)} %fusion.8), custom_call_target="Cholesky" | custom-call | tf_op jit(solution)/shard_map/jit(cholesky)/cholesky | solution.py:100
  92.2 0.6 compare_reduce_fusion
  92.9 0.6 fusion.6
  93.6 1.2 %custom-call.7 = f32[1,16,16]{1,2,0:T(8,128)S(1)} custom-call(f32[1,16,16]{2,1,0:T(8,128)S(1)} %fusion.6), custom_call_target="InvertDiagBlocksLowerTriangular" | custom-call | tf_op jit(solution)/shard_map/triangular_solve/custom-call.0 | solution.py:104
  94.8 0.2 fusion.1
  95.0 1.1 %fusion = bf16[1,16,1,36864]{3,1,2,0:T(8,128)(2,1)S(1)} fusion(f32[16,16]{1,0:T(8,128)S(1)} %fusion.1, bf16[16,36864]{1,0:T(8,128)(2,1)S(1)} %get-tuple-element.15), kind=kOutput, calls=%fused_computation.2 | convolution fusion | flops 113836032 | bytes 2360320 | tf_op jit(solution)/shard_map/dot_general | solution.py:129
  96.1 0.2 pad_maximum_fusion
  96.3 0.0 copy-start
  96.3 2.4 %all-to-all-done.1.received_ref = bf16[32,4,4608]{2,1,0:T(4,128)(2,1)} async-done(((bf16[32,4,4608]{2,1,0:T(4,128)(2,1)}), bf16[32,4,4608]{2,1,0:T(4,128)(2,1)}, u32[]{:S(2)}, u32[]{:S(2)}) %all-to-all-start.1) | async-done | bytes 1179680 | tf_op jit(solution)/shard_map/all_to_all | solution.py:108
  98.7 4.6 %shard_map.53 = (f32[16,64]{1,0:T(8,128)S(1)}, f32[16,32]{1,0:T(8,128)S(1)}) custom-call(bf16[32,4,4608]{2,1,0:T(4,128)(2,1)} %all-to-all-done.1.received_ref, bf16[64,36864]{1,0:T(8,128)(2,1)} %bitcast.49, bf16[32,36864]{1,0:T(8,128)(2,1)S(1)} %bitcast.44), custom_call_target="tpu_custom_call" | custom-call | tf_op jit(solution)/shard_map/pallas_call | solution.py:88
  103.3 0.7 pad_maximum_fusion.1
  (6 shorter events, 0.1 us)
Async XLA Ops:
  3.6 7.3 %copy-start.1 = (bf16[4,32,4608]{2,1,0:T(8,128)(2,1)S(1)}, bf16[4,32,4608]{2,1,0:T(8,128)(2,1)}, u32[]{:S(2)}) copy-start(bf16[4,32,4608]{2,1,0:T(8,128)(2,1)} %param.8) | copy-start | bytes 3538948
  3.6 61.8 %all-to-all-start = ((bf16[32,8,4608]{2,1,0:T(8,128)(2,1)}), bf16[32,8,4608]{2,1,0:T(8,128)(2,1)S(1)}, u32[]{:S(2)}, u32[]{:S(2)}) async-start(bf16[32,8,4608]{2,1,0:T(8,128)(2,1)} %shard_map.50), calls=%async_computation | async-start | bytes 4718592 | tf_op jit(solution)/shard_map/all_to_all | solution.py:108
  65.5 33.2 %all-to-all-start.1 = ((bf16[32,4,4608]{2,1,0:T(4,128)(2,1)}), bf16[32,4,4608]{2,1,0:T(4,128)(2,1)}, u32[]{:S(2)}, u32[]{:S(2)}) async-start(bf16[32,4,4608]{2,1,0:T(4,128)(2,1)} %bitcast.42), calls=%async_computation.1 | async-start | bytes 2359296 | tf_op jit(solution)/shard_map/all_to_all | solution.py:108
  96.3 7.0 %copy-start = (bf16[2,16,1,36864]{3,1,2,0:T(8,128)(2,1)}, bf16[2,16,1,36864]{3,1,2,0:T(8,128)(2,1)S(1)}, u32[]{:S(2)}) copy-start(bf16[2,16,1,36864]{3,1,2,0:T(8,128)(2,1)S(1)} %pad_maximum_fusion) | copy-start | bytes 7077892

commit v15 on v14

--- a/solution.py
+++ b/solution.py
@@ -67,16 +67,17 @@
     )(panels)
 
 
-def coarse_kernel(received_ref, earlier_ref, fresh_ref, earlier_out, fresh_out, vectors, *,
+def coarse_kernel(received_ref, earlier_ref, fresh_ref, out_ref, vectors, *,
                   lat_count, mode_count, entry_part, block_len):
     for lat_index in range(lat_count):
         rows = received_ref[lat_index * mode_count:(lat_index + 1) * mode_count]
         vectors[:, lat_index * entry_part:(lat_index + 1) * entry_part] = rows.reshape(-1, entry_part)
     further_rows = vectors[...]
-    earlier_out[...] = lax.dot_general(
-        further_rows, earlier_ref[...], NT, preferred_element_type=jnp.float32) / block_len
-    fresh_out[...] = lax.dot_general(
-        further_rows, fresh_ref[...], NT, preferred_element_type=jnp.float32) / block_len
+    earlier_count = earlier_ref.shape[0]
+    out_ref[:, :, :earlier_count] = (lax.dot_general(
+        further_rows, earlier_ref[...], NT, preferred_element_type=jnp.float32) / block_len)[:, None, :]
+    out_ref[:, :, earlier_count:] = (lax.dot_general(
+        further_rows, fresh_ref[...], NT, preferred_element_type=jnp.float32) / block_len)[:, None, :]
 
 
 def coarse_call(received, earlier_rows, fresh_rows, lat_count, mode_count):
@@ -87,9 +88,8 @@
                                entry_part=entry_part, block_len=block_len)
     return pl.pallas_call(
         kernel,
-        out_shape=(
-            jax.ShapeDtypeStruct((count, earlier_rows.shape[0]), jnp.float32),
-            jax.ShapeDtypeStruct((count, fresh_rows.shape[0]), jnp.float32),
+        out_shape=jax.ShapeDtypeStruct(
+            (count, 1, earlier_rows.shape[0] + fresh_rows.shape[0]), jnp.float32
         ),
         scratch_shapes=[pltpu.VMEM((count, block_len), received.dtype)],
         compiler_params=pltpu.CompilerParams(vmem_limit_bytes=48 * 1024 * 1024),
@@ -147,14 +147,13 @@
     )
     lat_count = lax.axis_size("lat")
     mode_count = lax.axis_size("mode")
-    earlier_part, fresh_part = coarse_call(
+    coarse = coarse_call(
         further_arrived,
         earlier.reshape(earlier.shape[0], block_len),
         new_basis.reshape(-1, block_len),
         lat_count,
         mode_count,
     )
-    coarse = jnp.concatenate([earlier_part, fresh_part], axis=1)[:, None, :]
     return (new_basis, coarse)
 
 

time: 104 us -> 104 us (level)
  no operation moved by 1% of the time
where the time goes in v15:
time: 104 us
  waiting for transfers between devices  54.9 us (53%)
  Pallas kernels  21.2 us (20%)
  starting transfers between devices  11.4 us (11%)
  other arithmetic  8.29 us (8%)
  local copies, waits for them, and re-layouts  4.89 us (5%)
  matrix products  2.55 us (2%)
    all_to_all x2, waiting for transfers between devices, send(): lax.all_to_all(block_major, ('lat', 'mode'), split_axis=0, concat_axis=0,...  54.9 us
    pallas_call x2, Pallas kernels, project_call(): pl.pallas_call(functools.partial(project_kernel, piece_count=len(pieces),...  12.9 us
    all_to_all x2, starting transfers between devices, send(): lax.all_to_all(block_major, ('lat', 'mode'), split_axis=0, concat_axis=0,...  11.4 us
    pallas_call x1, Pallas kernels, coarse_call(): pl.pallas_call(kernel, out_shape=jax.ShapeDtypeStruct((count, 1, earlier_...  5.33 us
    another operation x6, other arithmetic, factor_inverse(): lower_factor = jnp.linalg.cholesky(gram_matrix)  4.31 us
    another operation x4, other arithmetic, factor_inverse(): lax.linalg.triangular_solve(lower_factor, identity, left_side=True, lower...  3.75 us
    pallas_call x1, Pallas kernels, block_major(): pl.pallas_call(block_major_kernel, grid=(block_count // group,), out_shap...  2.99 us
    unnamed x7, local copies, waits for them, and re-layouts  2.66 us
  transfers between devices with their start and end apart: 2, of which 2 were waited for; matrix products, arithmetic and copies ran while one was open for 15% of the time, Pallas kernels for 12%

profile of v15, /device:TPU:0, one launch (start us, length us, event | category | flops | bytes accessed | tf_op | source)
XLA Modules:
  0.0 104.0 jit_solution(15413277628339950733)
XLA Ops:
  0.6 3.0 %shard_map.50 = bf16[32,8,4608]{2,1,0:T(8,128)(2,1)} custom-call(bf16[2,4,32,4608]{3,2,1,0:T(8,128)(2,1)} %panels_ref.1), custom_call_target="tpu_custom_call" | custom-call | tf_op jit(solution)/shard_map/pallas_call | solution.py:59
  3.6 7.3 %all-to-all-start = ((bf16[32,8,4608]{2,1,0:T(8,128)(2,1)}), bf16[32,8,4608]{2,1,0:T(8,128)(2,1)S(1)}, u32[]{:S(2)}, u32[]{:S(2)}) async-start(bf16[32,8,4608]{2,1,0:T(8,128)(2,1)} %shard_map.50), calls=%async_computation | async-start | bytes 4718592 | tf_op jit(solution)/shard_map/all_to_all | solution.py:108
  10.9 0.0 copy-done.1
  10.9 2.0 %copy.13 = bf16[4,32,4608]{2,0,1:T(4,128)(2,1)} copy(bf16[4,32,4608]{2,1,0:T(8,128)(2,1)S(1)} %copy-done.1) | data formatting | bytes 2359296 | tf_op args[2]
  12.9 52.6 %all-to-all-done = bf16[32,8,4608]{2,1,0:T(8,128)(2,1)S(1)} async-done(((bf16[32,8,4608]{2,1,0:T(8,128)(2,1)}), bf16[32,8,4608]{2,1,0:T(8,128)(2,1)S(1)}, u32[]{:S(2)}, u32[]{:S(2)}) %all-to-all-start) | async-done | bytes 2359328 | tf_op jit(solution)/shard_map/all_to_all | solution.py:108
  65.5 4.1 %all-to-all-start.1 = ((bf16[32,4,4608]{2,1,0:T(4,128)(2,1)}), bf16[32,4,4608]{2,1,0:T(4,128)(2,1)}, u32[]{:S(2)}, u32[]{:S(2)}) async-start(bf16[32,4,4608]{2,1,0:T(4,128)(2,1)} %bitcast.39), calls=%async_computation.1 | async-start | bytes 2359296 | tf_op jit(solution)/shard_map/all_to_all | solution.py:108
  69.6 0.8 fusion.11
  70.4 0.7 copy.5
  71.0 0.3 copy.10
  71.4 6.8 %shard_map.51 = (bf16[16,36864]{1,0:T(8,128)(2,1)S(1)}, f32[16,16]{1,0:T(8,128)S(1)}) custom-call(bf16[64,36864]{1,0:T(8,128)(2,1)} %bitcast.44, bf16[16,36864]{1,0:T(8,128)(2,1)S(1)} %bitcast.43), custom_call_target="tpu_custom_call" | custom-call | flops 169869312 | bytes 7078912 | tf_op jit(solution)/shard_map/pallas_call | solution.py:33
  78.2 0.1 copy.6
  78.3 1.5 %cholesky.44 = f32[16,16]{1,0:T(8,128)S(1)} custom-call(f32[16,16]{1,0:T(8,128)S(1)} %fusion.10), custom_call_target="Cholesky" | custom-call | tf_op jit(solution)/shard_map/jit(cholesky)/cholesky | solution.py:100
  79.8 0.6 compare_reduce_fusion.1
  80.4 0.6 fusion.5
  81.1 1.2 %custom-call.6 = f32[1,16,16]{1,2,0:T(8,128)S(1)} custom-call(f32[1,16,16]{2,1,0:T(8,128)S(1)} %fusion.5), custom_call_target="InvertDiagBlocksLowerTriangular" | custom-call | tf_op jit(solution)/shard_map/triangular_solve/custom-call.0 | solution.py:104
  82.3 0.2 fusion.3
  82.5 0.7 copy.7
  83.2 0.3 copy.11
  83.5 1.1 %convolution_convert_fusion.1.refs_1_ = bf16[16,36864]{1,0:T(8,128)(2,1)S(1)} fusion(f32[16,16]{1,0:T(8,128)S(1)} %fusion.3, bf16[16,36864]{1,0:T(8,128)(2,1)S(1)} %get-tuple-element.11), kind=kOutput, calls=%fused_computation.1 | convolution fusion | flops 113836032 | bytes 2360320 | tf_op jit(solution)/shard_map/dot_general | solution.py:129
  84.6 6.1 %shard_map.52 = (bf16[16,36864]{1,0:T(8,128)(2,1)S(1)}, f32[16,16]{1,0:T(8,128)S(1)}) custom-call(bf16[64,36864]{1,0:T(8,128)(2,1)} %bitcast.45, bf16[16,36864]{1,0:T(8,128)(2,1)S(1)} %convolution_convert_fusion.1.refs_1_, bf16[16,36864]{1,0:T(8,128)(2,1)S(1)} %bitcast.42), custom_call_target="tpu_custom_call" | custom-call | flops 207618048 | bytes 8258560 | tf_op jit(solution)/shard_map/pallas_call | solution.py:33
  90.7 0.1 copy.8
  90.8 1.5 %cholesky.55 = f32[16,16]{1,0:T(8,128)S(1)} custom-call(f32[16,16]{1,0:T(8,128)S(1)} %fusion.8), custom_call_target="Cholesky" | custom-call | tf_op jit(solution)/shard_map/jit(cholesky)/cholesky | solution.py:100
  92.2 0.6 compare_reduce_fusion
  92.9 0.6 fusion.6
  93.6 1.2 %custom-call.7 = f32[1,16,16]{1,2,0:T(8,128)S(1)} custom-call(f32[1,16,16]{2,1,0:T(8,128)S(1)} %fusion.6), custom_call_target="InvertDiagBlocksLowerTriangular" | custom-call | tf_op jit(solution)/shard_map/triangular_solve/custom-call.0 | solution.py:104
  94.8 0.2 fusion.1
  95.0 1.1 %fusion = bf16[1,16,1,36864]{3,1,2,0:T(8,128)(2,1)S(1)} fusion(f32[16,16]{1,0:T(8,128)S(1)} %fusion.1, bf16[16,36864]{1,0:T(8,128)(2,1)S(1)} %get-tuple-element.13), kind=kOutput, calls=%fused_computation.2 | convolution fusion | flops 113836032 | bytes 2360320 | tf_op jit(solution)/shard_map/dot_general | solution.py:129
  96.1 0.2 pad_maximum_fusion
  96.3 0.0 copy-start
  96.3 2.4 %all-to-all-done.1.received_ref = bf16[32,4,4608]{2,1,0:T(4,128)(2,1)} async-done(((bf16[32,4,4608]{2,1,0:T(4,128)(2,1)}), bf16[32,4,4608]{2,1,0:T(4,128)(2,1)}, u32[]{:S(2)}, u32[]{:S(2)}) %all-to-all-start.1) | async-done | bytes 1179680 | tf_op jit(solution)/shard_map/all_to_all | solution.py:108
  98.7 5.3 %shard_map.53 = f32[16,1,96]{2,1,0:T(1,128)} custom-call(bf16[32,4,4608]{2,1,0:T(4,128)(2,1)} %all-to-all-done.1.received_ref, bf16[64,36864]{1,0:T(8,128)(2,1)} %bitcast.46, bf16[32,36864]{1,0:T(8,128)(2,1)S(1)} %bitcast.41), custom_call_target="tpu_custom_call" | custom-call | tf_op jit(solution)/shard_map/pallas_call | solution.py:89
  104.0 0.0 copy-done
  (5 shorter events, 0.1 us)
Async XLA Ops:
  3.6 7.3 %copy-start.1 = (bf16[4,32,4608]{2,1,0:T(8,128)(2,1)S(1)}, bf16[4,32,4608]{2,1,0:T(8,128)(2,1)}, u32[]{:S(2)}) copy-start(bf16[4,32,4608]{2,1,0:T(8,128)(2,1)} %param.8) | copy-start | bytes 3538948
  3.6 61.8 %all-to-all-start = ((bf16[32,8,4608]{2,1,0:T(8,128)(2,1)}), bf16[32,8,4608]{2,1,0:T(8,128)(2,1)S(1)}, u32[]{:S(2)}, u32[]{:S(2)}) async-start(bf16[32,8,4608]{2,1,0:T(8,128)(2,1)} %shard_map.50), calls=%async_computation | async-start | bytes 4718592 | tf_op jit(solution)/shard_map/all_to_all | solution.py:108
  65.5 33.2 %all-to-all-start.1 = ((bf16[32,4,4608]{2,1,0:T(4,128)(2,1)}), bf16[32,4,4608]{2,1,0:T(4,128)(2,1)}, u32[]{:S(2)}, u32[]{:S(2)}) async-start(bf16[32,4,4608]{2,1,0:T(4,128)(2,1)} %bitcast.39), calls=%async_computation.1 | async-start | bytes 2359296 | tf_op jit(solution)/shard_map/all_to_all | solution.py:108
  96.3 7.7 %copy-start = (bf16[2,16,1,36864]{3,1,2,0:T(8,128)(2,1)}, bf16[2,16,1,36864]{3,1,2,0:T(8,128)(2,1)S(1)}, u32[]{:S(2)}) copy-start(bf16[2,16,1,36864]{3,1,2,0:T(8,128)(2,1)S(1)} %pad_maximum_fusion) | copy-start | bytes 7077892

commit v16 on v14

--- a/solution.py
+++ b/solution.py
@@ -67,32 +67,41 @@
     )(panels)
 
 
-def coarse_kernel(received_ref, earlier_ref, fresh_ref, earlier_out, fresh_out, vectors, *,
-                  lat_count, mode_count, entry_part, block_len):
-    for lat_index in range(lat_count):
-        rows = received_ref[lat_index * mode_count:(lat_index + 1) * mode_count]
-        vectors[:, lat_index * entry_part:(lat_index + 1) * entry_part] = rows.reshape(-1, entry_part)
-    further_rows = vectors[...]
-    earlier_out[...] = lax.dot_general(
-        further_rows, earlier_ref[...], NT, preferred_element_type=jnp.float32) / block_len
-    fresh_out[...] = lax.dot_general(
-        further_rows, fresh_ref[...], NT, preferred_element_type=jnp.float32) / block_len
+def coarse_kernel(received_ref, earlier_ref, fresh_ref, earlier_out, fresh_out):
+    @pl.when(pl.program_id(0) == 0)
+    def _():
+        earlier_out[...] = jnp.zeros_like(earlier_out)
+        fresh_out[...] = jnp.zeros_like(fresh_out)
+
+    rows = received_ref[...]
+    further_rows = rows.reshape(-1, rows.shape[2])
+    earlier_out[...] += lax.dot_general(
+        further_rows, earlier_ref[...], NT, preferred_element_type=jnp.float32)
+    fresh_out[...] += lax.dot_general(
+        further_rows, fresh_ref[...], NT, preferred_element_type=jnp.float32)
 
 
 def coarse_call(received, earlier_rows, fresh_rows, lat_count, mode_count):
     _, vector_part, entry_part = received.shape
     count = mode_count * vector_part
-    block_len = lat_count * entry_part
-    kernel = functools.partial(coarse_kernel, lat_count=lat_count, mode_count=mode_count,
-                               entry_part=entry_part, block_len=block_len)
+    earlier_count = earlier_rows.shape[0]
+    fresh_count = fresh_rows.shape[0]
     return pl.pallas_call(
-        kernel,
+        coarse_kernel,
+        grid=(lat_count,),
         out_shape=(
-            jax.ShapeDtypeStruct((count, earlier_rows.shape[0]), jnp.float32),
-            jax.ShapeDtypeStruct((count, fresh_rows.shape[0]), jnp.float32),
+            jax.ShapeDtypeStruct((count, earlier_count), jnp.float32),
+            jax.ShapeDtypeStruct((count, fresh_count), jnp.float32),
         ),
-        scratch_shapes=[pltpu.VMEM((count, block_len), received.dtype)],
-        compiler_params=pltpu.CompilerParams(vmem_limit_bytes=48 * 1024 * 1024),
+        in_specs=[
+            pl.BlockSpec((mode_count, vector_part, entry_part), lambda l: (l, 0, 0)),
+            pl.BlockSpec((earlier_count, entry_part), lambda l: (0, l)),
+            pl.BlockSpec((fresh_count, entry_part), lambda l: (0, l)),
+        ],
+        out_specs=(
+            pl.BlockSpec((count, earlier_count), lambda l: (0, 0)),
+            pl.BlockSpec((count, fresh_count), lambda l: (0, 0)),
+        ),
     )(received, earlier_rows, fresh_rows)
 
 
@@ -154,7 +163,7 @@
         lat_count,
         mode_count,
     )
-    coarse = jnp.concatenate([earlier_part, fresh_part], axis=1)[:, None, :]
+    coarse = (jnp.concatenate([earlier_part, fresh_part], axis=1) / block_len)[:, None, :]
     return (new_basis, coarse)
 
 

time: 104 us -> 111 us (1.067)
  other arithmetic: 8.98 us -> 12.4 us
  local copies, waits for them, and re-layouts: 4.89 us -> 8.13 us
  Pallas kernels: 20.5 us -> 23.2 us
  waiting for transfers between devices: 54.9 us -> 52.6 us
    pallas_call x1, Pallas kernels: 4.63 us -> 7.31 us  [coarse_call(): pl.pallas_call(coarse_kernel, grid=(lat_count,), out_shape=(jax.ShapeDtyp...]
    all_to_all x2, waiting for transfers between devices: 54.9 us -> 52.6 us  [send(): lax.all_to_all(block_major, ('lat', 'mode'), split_axis=0, concat_axis=0,...]
    another operation x1, other arithmetic: 0.22 us -> 1.61 us  [per_device(): new_basis = jnp.stack(finished, 0)]
    div x0 -> x1, other arithmetic: none -> 1.39 us  [per_device(): jnp.concatenate([earlier_part, fresh_part], axis=1) / block_len]
    reshape x2, local copies, waits for them, and re-layouts: 1.31 us -> 2.59 us  [split_by_source(): received.reshape(lat_count, mode_count, received.shape[1], received.shape...]
  transfers between devices with their start and end apart: 2 -> 2, of which waited for: 2 -> 1; matrix products, arithmetic and copies ran while one was open for 15% -> 19% of each run, Pallas kernels for 12% -> 12%
where the time goes in v16:
time: 111 us
  waiting for transfers between devices  52.6 us (47%)
  Pallas kernels  23.2 us (21%)
  other arithmetic  12.4 us (11%)
  starting transfers between devices  11.3 us (10%)
  local copies, waits for them, and re-layouts  8.13 us (7%)
  matrix products  2.55 us (2%)
    all_to_all x2, waiting for transfers between devices, send(): lax.all_to_all(block_major, ('lat', 'mode'), split_axis=0, concat_axis=0,...  52.6 us
    pallas_call x2, Pallas kernels, project_call(): pl.pallas_call(functools.partial(project_kernel, piece_count=len(pieces),...  12.9 us
    all_to_all x2, starting transfers between devices, send(): lax.all_to_all(block_major, ('lat', 'mode'), split_axis=0, concat_axis=0,...  11.3 us
    pallas_call x1, Pallas kernels, coarse_call(): pl.pallas_call(coarse_kernel, grid=(lat_count,), out_shape=(jax.ShapeDtyp...  7.31 us
    another operation x6, other arithmetic, factor_inverse(): lower_factor = jnp.linalg.cholesky(gram_matrix)  4.99 us
    another operation x4, other arithmetic, factor_inverse(): lax.linalg.triangular_solve(lower_factor, identity, left_side=True, lower...  3.75 us
    unnamed x7, local copies, waits for them, and re-layouts  3.62 us
    pallas_call x1, Pallas kernels, block_major(): pl.pallas_call(block_major_kernel, grid=(block_count // group,), out_shap...  2.99 us
  transfers between devices with their start and end apart: 2, of which 1 were waited for; matrix products, arithmetic and copies ran while one was open for 19% of the time, Pallas kernels for 12%

profile of v16, /device:TPU:0, one launch (start us, length us, event | category | flops | bytes accessed | tf_op | source)
XLA Modules:
  0.0 110.8 jit_solution(15991123023578367259)
XLA Ops:
  0.6 3.0 %shard_map.50 = bf16[32,8,4608]{2,1,0:T(8,128)(2,1)} custom-call(bf16[2,4,32,4608]{3,2,1,0:T(8,128)(2,1)} %panels_ref.1), custom_call_target="tpu_custom_call" | custom-call | tf_op jit(solution)/shard_map/pallas_call | solution.py:59
  3.6 7.3 %all-to-all-start = ((bf16[32,8,4608]{2,1,0:T(8,128)(2,1)}), bf16[32,8,4608]{2,1,0:T(8,128)(2,1)S(1)}, u32[]{:S(2)}, u32[]{:S(2)}) async-start(bf16[32,8,4608]{2,1,0:T(8,128)(2,1)} %shard_map.50), calls=%async_computation | async-start | bytes 4718592 | tf_op jit(solution)/shard_map/all_to_all | solution.py:117
  10.9 1.9 %copy.14 = bf16[4,32,4608]{2,0,1:T(4,128)(2,1)} copy(bf16[4,32,4608]{2,1,0:T(8,128)(2,1)S(1)} %copy-done.1) | data formatting | bytes 2359296 | tf_op args[2]
  12.9 52.6 %all-to-all-done = bf16[32,8,4608]{2,1,0:T(8,128)(2,1)S(1)} async-done(((bf16[32,8,4608]{2,1,0:T(8,128)(2,1)}), bf16[32,8,4608]{2,1,0:T(8,128)(2,1)S(1)}, u32[]{:S(2)}, u32[]{:S(2)}) %all-to-all-start) | async-done | bytes 2359328 | tf_op jit(solution)/shard_map/all_to_all | solution.py:117
  65.5 4.0 %all-to-all-start.1 = ((bf16[32,4,4608]{2,1,0:T(4,128)(2,1)}), bf16[32,4,4608]{2,1,0:T(4,128)(2,1)S(1)}, u32[]{:S(2)}, u32[]{:S(2)}) async-start(bf16[32,4,4608]{2,1,0:T(4,128)(2,1)} %bitcast.42), calls=%async_computation.1 | async-start | bytes 2359296 | tf_op jit(solution)/shard_map/all_to_all | solution.py:117
  69.5 1.8 %fusion.11 = (bf16[32,4,4608]{2,1,0:T(4,128)(2,1)}, bf16[32,4,4608]{2,1,0:T(4,128)(2,1)S(1)}) fusion(bf16[32,8,4608]{2,1,0:T(8,128)(2,1)S(1)} %all-to-all-done), kind=kLoop, calls=%fused_computation.26 | loop fusion | bytes 4718592 | tf_op jit(solution)/shard_map/slice | solution.py:151
  71.2 0.7 copy.5
  71.9 0.3 copy.11
  72.3 6.8 %shard_map.51 = (bf16[16,36864]{1,0:T(8,128)(2,1)S(1)}, f32[16,16]{1,0:T(8,128)S(1)}) custom-call(bf16[64,36864]{1,0:T(8,128)(2,1)} %bitcast.46, bf16[16,36864]{1,0:T(8,128)(2,1)S(1)} %bitcast.45), custom_call_target="tpu_custom_call" | custom-call | flops 169869312 | bytes 7078912 | tf_op jit(solution)/shard_map/pallas_call | solution.py:33
  79.1 0.1 copy.6
  79.1 1.5 %cholesky.44 = f32[16,16]{1,0:T(8,128)S(1)} custom-call(f32[16,16]{1,0:T(8,128)S(1)} %fusion.10), custom_call_target="Cholesky" | custom-call | tf_op jit(solution)/shard_map/jit(cholesky)/cholesky | solution.py:109
  80.7 0.6 compare_reduce_fusion.1
  81.3 0.6 fusion.5
  82.0 1.2 %custom-call.6 = f32[1,16,16]{1,2,0:T(8,128)S(1)} custom-call(f32[1,16,16]{2,1,0:T(8,128)S(1)} %fusion.5), custom_call_target="InvertDiagBlocksLowerTriangular" | custom-call | tf_op jit(solution)/shard_map/triangular_solve/custom-call.0 | solution.py:113
  83.2 0.2 fusion.3
  83.4 1.9 %copy.7 = bf16[8,4,4,4608]{3,0,2,1:T(8,128)(2,1)S(1)} copy(bf16[8,4,4,4608]{3,2,1,0:T(4,128)(2,1)} %bitcast.52) | data formatting | bytes 2359296 | tf_op jit(solution)/shard_map/reshape | solution.py:123
  85.3 0.3 copy.12
  85.7 1.1 convolution_convert_fusion.1.refs_1_
  86.8 6.1 %shard_map.52 = (bf16[16,36864]{1,0:T(8,128)(2,1)S(1)}, f32[16,16]{1,0:T(8,128)S(1)}) custom-call(bf16[64,36864]{1,0:T(8,128)(2,1)} %bitcast.47, bf16[16,36864]{1,0:T(8,128)(2,1)S(1)} %convolution_convert_fusion.1.refs_1_, bf16[16,36864]{1,0:T(8,128)(2,1)S(1)} %bitcast.44), custom_call_target="tpu_custom_call" | custom-call | flops 207618048 | bytes 8258560 | tf_op jit(solution)/shard_map/pallas_call | solution.py:33
  92.8 0.1 copy.8
  92.9 0.6 fusion.8
  93.5 2.1 %cholesky.55 = f32[16,16]{1,0:T(8,128)S(1)} custom-call(f32[16,16]{1,0:T(8,128)} %fusion.8), custom_call_target="Cholesky" | custom-call | tf_op jit(solution)/shard_map/jit(cholesky)/cholesky | solution.py:109
  95.7 0.6 compare_reduce_fusion
  96.3 0.6 fusion.6
  97.0 1.2 %custom-call.7 = f32[1,16,16]{1,2,0:T(8,128)S(1)} custom-call(f32[1,16,16]{2,1,0:T(8,128)S(1)} %fusion.6), custom_call_target="InvertDiagBlocksLowerTriangular" | custom-call | tf_op jit(solution)/shard_map/triangular_solve/custom-call.0 | solution.py:113
  98.2 0.2 fusion.1
  98.4 1.1 fusion
  99.5 1.6 %pad_maximum_fusion = bf16[2,16,1,36864]{3,1,2,0:T(8,128)(2,1)} fusion(bf16[1,16,1,36864]{3,1,2,0:T(8,128)(2,1)S(1)} %fusion, bf16[1,16,1,36864]{3,1,2,0:T(8,128)(2,1)S(1)} %bitcast.43), kind=kLoop, calls=%fused_computation.3 | loop fusion | flops 1179648 | bytes 4718592 | tf_op jit(solution)/shard_map/stack | solution.py:153
  101.1 0.0 all-to-all-done.1.received_ref
  101.1 1.0 copy-done
  102.1 7.3 %shard_map.53 = (f32[16,64]{1,0:T(8,128)}, f32[16,32]{1,0:T(8,128)}) custom-call(bf16[32,4,4608]{2,1,0:T(4,128)(2,1)} %copy-done, bf16[64,36864]{1,0:T(8,128)(2,1)} %bitcast.48, bf16[32,36864]{1,0:T(8,128)(2,1)} %bitcast.49), custom_call_target="tpu_custom_call" | custom-call | tf_op jit(solution)/shard_map/pallas_call | solution.py:89
  109.4 1.4 %maximum_multiply_fusion = f32[16,1,96]{2,0,1:T(8,128)} fusion(f32[16,1,32]{2,0,1:T(8,128)} %bitcast.56, f32[16,1,64]{2,0,1:T(8,128)} %bitcast.55), kind=kLoop, calls=%fused_computation.13 | loop fusion | flops 3072 | bytes 12288 | tf_op jit(solution)/shard_map/div | solution.py:166
  (6 shorter events, 0.1 us)
Async XLA Ops:
  3.6 7.3 %copy-start.1 = (bf16[4,32,4608]{2,1,0:T(8,128)(2,1)S(1)}, bf16[4,32,4608]{2,1,0:T(8,128)(2,1)}, u32[]{:S(2)}) copy-start(bf16[4,32,4608]{2,1,0:T(8,128)(2,1)} %param.8) | copy-start | bytes 3538948
  3.6 61.8 %all-to-all-start = ((bf16[32,8,4608]{2,1,0:T(8,128)(2,1)}), bf16[32,8,4608]{2,1,0:T(8,128)(2,1)S(1)}, u32[]{:S(2)}, u32[]{:S(2)}) async-start(bf16[32,8,4608]{2,1,0:T(8,128)(2,1)} %shard_map.50), calls=%async_computation | async-start | bytes 4718592 | tf_op jit(solution)/shard_map/all_to_all | solution.py:117
  65.5 35.7 %all-to-all-start.1 = ((bf16[32,4,4608]{2,1,0:T(4,128)(2,1)}), bf16[32,4,4608]{2,1,0:T(4,128)(2,1)S(1)}, u32[]{:S(2)}, u32[]{:S(2)}) async-start(bf16[32,4,4608]{2,1,0:T(4,128)(2,1)} %bitcast.42), calls=%async_computation.1 | async-start | bytes 2359296 | tf_op jit(solution)/shard_map/all_to_all | solution.py:117
  101.1 1.0 copy-start

commit v17 on v16

--- a/solution.py
+++ b/solution.py
@@ -67,41 +67,50 @@
     )(panels)
 
 
-def coarse_kernel(received_ref, earlier_ref, fresh_ref, earlier_out, fresh_out):
+def coarse_kernel(received_ref, earlier_ref, fresh_ref, earlier_out, fresh_out, vectors, *,
+                  lat_count, mode_count, entry_part):
     @pl.when(pl.program_id(0) == 0)
     def _():
         earlier_out[...] = jnp.zeros_like(earlier_out)
         fresh_out[...] = jnp.zeros_like(fresh_out)
 
-    rows = received_ref[...]
-    further_rows = rows.reshape(-1, rows.shape[2])
+    for lat_index in range(lat_count):
+        rows = received_ref[lat_index * mode_count:(lat_index + 1) * mode_count]
+        vectors[:, lat_index * entry_part:(lat_index + 1) * entry_part] = rows.reshape(-1, entry_part)
+    further_rows = vectors[...]
     earlier_out[...] += lax.dot_general(
         further_rows, earlier_ref[...], NT, preferred_element_type=jnp.float32)
     fresh_out[...] += lax.dot_general(
         further_rows, fresh_ref[...], NT, preferred_element_type=jnp.float32)
 
 
-def coarse_call(received, earlier_rows, fresh_rows, lat_count, mode_count):
+def coarse_call(received, earlier_rows, fresh_rows, lat_count, mode_count, steps=2):
     _, vector_part, entry_part = received.shape
     count = mode_count * vector_part
+    steps = steps if lat_count % steps == 0 else 1
+    lat_step = lat_count // steps
+    kernel = functools.partial(coarse_kernel, lat_count=lat_step, mode_count=mode_count,
+                               entry_part=entry_part)
     earlier_count = earlier_rows.shape[0]
     fresh_count = fresh_rows.shape[0]
     return pl.pallas_call(
-        coarse_kernel,
-        grid=(lat_count,),
+        kernel,
+        grid=(steps,),
         out_shape=(
             jax.ShapeDtypeStruct((count, earlier_count), jnp.float32),
             jax.ShapeDtypeStruct((count, fresh_count), jnp.float32),
         ),
         in_specs=[
-            pl.BlockSpec((mode_count, vector_part, entry_part), lambda l: (l, 0, 0)),
-            pl.BlockSpec((earlier_count, entry_part), lambda l: (0, l)),
-            pl.BlockSpec((fresh_count, entry_part), lambda l: (0, l)),
+            pl.BlockSpec((lat_step * mode_count, vector_part, entry_part), lambda s: (s, 0, 0)),
+            pl.BlockSpec((earlier_count, lat_step * entry_part), lambda s: (0, s)),
+            pl.BlockSpec((fresh_count, lat_step * entry_part), lambda s: (0, s)),
         ],
         out_specs=(
-            pl.BlockSpec((count, earlier_count), lambda l: (0, 0)),
-            pl.BlockSpec((count, fresh_count), lambda l: (0, 0)),
+            pl.BlockSpec((count, earlier_count), lambda s: (0, 0)),
+            pl.BlockSpec((count, fresh_count), lambda s: (0, 0)),
         ),
+        scratch_shapes=[pltpu.VMEM((count, lat_step * entry_part), received.dtype)],
+        compiler_params=pltpu.CompilerParams(vmem_limit_bytes=48 * 1024 * 1024),
     )(received, earlier_rows, fresh_rows)
 
 

time: 111 us -> 104 us (0.937)
  other arithmetic: 12.4 us -> 8.97 us
  Pallas kernels: 23.2 us -> 19.8 us
  local copies, waits for them, and re-layouts: 8.13 us -> 4.89 us
  waiting for transfers between devices: 52.6 us -> 54.9 us
    pallas_call x1, Pallas kernels: 7.31 us -> 3.96 us  [coarse_call(): pl.pallas_call(kernel, grid=(steps,), out_shape=(jax.ShapeDtypeStruct((co...]
    all_to_all x2, waiting for transfers between devices: 52.6 us -> 54.9 us  [send(): lax.all_to_all(block_major, ('lat', 'mode'), split_axis=0, concat_axis=0,...]
    another operation x1, other arithmetic: 1.61 us -> 0.22 us  [per_device(): new_basis = jnp.stack(finished, 0)]
    reshape x2, local copies, waits for them, and re-layouts: 2.59 us -> 1.31 us  [split_by_source(): received.reshape(lat_count, mode_count, received.shape[1], received.shape...]
  transfers between devices with their start and end apart: 2 -> 2, of which waited for: 1 -> 2; matrix products, arithmetic and copies ran while one was open for 19% -> 15% of each run, Pallas kernels for 12% -> 12%
where the time goes in v17:
time: 104 us; the launch traced here: 103 us
  waiting for transfers between devices  54.9 us (53%)
  Pallas kernels  19.8 us (19%)
  starting transfers between devices  11.4 us (11%)
  other arithmetic  8.97 us (9%)
  local copies, waits for them, and re-layouts  4.89 us (5%)
  matrix products  2.55 us (2%)
    all_to_all x2, waiting for transfers between devices, send(): lax.all_to_all(block_major, ('lat', 'mode'), split_axis=0, concat_axis=0,...  54.9 us
    pallas_call x2, Pallas kernels, project_call(): pl.pallas_call(functools.partial(project_kernel, piece_count=len(pieces),...  12.9 us
    all_to_all x2, starting transfers between devices, send(): lax.all_to_all(block_major, ('lat', 'mode'), split_axis=0, concat_axis=0,...  11.4 us
    another operation x6, other arithmetic, factor_inverse(): lower_factor = jnp.linalg.cholesky(gram_matrix)  4.31 us
    pallas_call x1, Pallas kernels, coarse_call(): pl.pallas_call(kernel, grid=(steps,), out_shape=(jax.ShapeDtypeStruct((co...  3.96 us
    another operation x4, other arithmetic, factor_inverse(): lax.linalg.triangular_solve(lower_factor, identity, left_side=True, lower...  3.75 us
    pallas_call x1, Pallas kernels, block_major(): pl.pallas_call(block_major_kernel, grid=(block_count // group,), out_shap...  2.99 us
    unnamed x7, local copies, waits for them, and re-layouts  2.66 us
  transfers between devices with their start and end apart: 2, of which 2 were waited for; matrix products, arithmetic and copies ran while one was open for 15% of the time, Pallas kernels for 12%

profile of v17, /device:TPU:0, one launch (start us, length us, event | category | flops | bytes accessed | tf_op | source)
XLA Modules:
  0.0 103.3 jit_solution(6226564143862417781)
XLA Ops:
  0.6 3.0 %shard_map.50 = bf16[32,8,4608]{2,1,0:T(8,128)(2,1)} custom-call(bf16[2,4,32,4608]{3,2,1,0:T(8,128)(2,1)} %panels_ref.1), custom_call_target="tpu_custom_call" | custom-call | tf_op jit(solution)/shard_map/pallas_call | solution.py:59
  3.6 7.3 %all-to-all-start = ((bf16[32,8,4608]{2,1,0:T(8,128)(2,1)}), bf16[32,8,4608]{2,1,0:T(8,128)(2,1)S(1)}, u32[]{:S(2)}, u32[]{:S(2)}) async-start(bf16[32,8,4608]{2,1,0:T(8,128)(2,1)} %shard_map.50), calls=%async_computation | async-start | bytes 4718592 | tf_op jit(solution)/shard_map/all_to_all | solution.py:126
  10.9 0.0 copy-done.1
  10.9 2.0 %copy.14 = bf16[4,32,4608]{2,0,1:T(4,128)(2,1)} copy(bf16[4,32,4608]{2,1,0:T(8,128)(2,1)S(1)} %copy-done.1) | data formatting | bytes 2359296 | tf_op args[2]
  12.9 52.6 %all-to-all-done = bf16[32,8,4608]{2,1,0:T(8,128)(2,1)S(1)} async-done(((bf16[32,8,4608]{2,1,0:T(8,128)(2,1)}), bf16[32,8,4608]{2,1,0:T(8,128)(2,1)S(1)}, u32[]{:S(2)}, u32[]{:S(2)}) %all-to-all-start) | async-done | bytes 2359328 | tf_op jit(solution)/shard_map/all_to_all | solution.py:126
  65.5 4.1 %all-to-all-start.1 = ((bf16[32,4,4608]{2,1,0:T(4,128)(2,1)}), bf16[32,4,4608]{2,1,0:T(4,128)(2,1)}, u32[]{:S(2)}, u32[]{:S(2)}) async-start(bf16[32,4,4608]{2,1,0:T(4,128)(2,1)} %bitcast.42), calls=%async_computation.1 | async-start | bytes 2359296 | tf_op jit(solution)/shard_map/all_to_all | solution.py:126
  69.6 0.8 fusion.11
  70.4 0.7 copy.5
  71.0 0.3 copy.11
  71.4 6.8 %shard_map.51 = (bf16[16,36864]{1,0:T(8,128)(2,1)S(1)}, f32[16,16]{1,0:T(8,128)S(1)}) custom-call(bf16[64,36864]{1,0:T(8,128)(2,1)} %bitcast.49, bf16[16,36864]{1,0:T(8,128)(2,1)S(1)} %bitcast.46), custom_call_target="tpu_custom_call" | custom-call | flops 169869312 | bytes 7078912 | tf_op jit(solution)/shard_map/pallas_call | solution.py:33
  78.2 0.1 copy.6
  78.3 1.5 %cholesky.44 = f32[16,16]{1,0:T(8,128)S(1)} custom-call(f32[16,16]{1,0:T(8,128)S(1)} %fusion.10), custom_call_target="Cholesky" | custom-call | tf_op jit(solution)/shard_map/jit(cholesky)/cholesky | solution.py:118
  79.8 0.6 compare_reduce_fusion.1
  80.4 0.6 fusion.5
  81.1 1.2 %custom-call.6 = f32[1,16,16]{1,2,0:T(8,128)S(1)} custom-call(f32[1,16,16]{2,1,0:T(8,128)S(1)} %fusion.5), custom_call_target="InvertDiagBlocksLowerTriangular" | custom-call | tf_op jit(solution)/shard_map/triangular_solve/custom-call.0 | solution.py:122
  82.3 0.2 fusion.3
  82.5 0.7 copy.7
  83.2 0.3 copy.12
  83.5 1.1 %convolution_convert_fusion.1.refs_1_ = bf16[16,36864]{1,0:T(8,128)(2,1)S(1)} fusion(f32[16,16]{1,0:T(8,128)S(1)} %fusion.3, bf16[16,36864]{1,0:T(8,128)(2,1)S(1)} %get-tuple-element.13), kind=kOutput, calls=%fused_computation.1 | convolution fusion | flops 113836032 | bytes 2360320 | tf_op jit(solution)/shard_map/dot_general | solution.py:147
  84.6 6.1 %shard_map.52 = (bf16[16,36864]{1,0:T(8,128)(2,1)S(1)}, f32[16,16]{1,0:T(8,128)S(1)}) custom-call(bf16[64,36864]{1,0:T(8,128)(2,1)} %bitcast.50, bf16[16,36864]{1,0:T(8,128)(2,1)S(1)} %convolution_convert_fusion.1.refs_1_, bf16[16,36864]{1,0:T(8,128)(2,1)S(1)} %bitcast.45), custom_call_target="tpu_custom_call" | custom-call | flops 207618048 | bytes 8258560 | tf_op jit(solution)/shard_map/pallas_call | solution.py:33
  90.7 0.1 copy.8
  90.8 1.5 %cholesky.55 = f32[16,16]{1,0:T(8,128)S(1)} custom-call(f32[16,16]{1,0:T(8,128)S(1)} %fusion.8), custom_call_target="Cholesky" | custom-call | tf_op jit(solution)/shard_map/jit(cholesky)/cholesky | solution.py:118
  92.2 0.6 compare_reduce_fusion
  92.9 0.6 fusion.6
  93.6 1.2 %custom-call.7 = f32[1,16,16]{1,2,0:T(8,128)S(1)} custom-call(f32[1,16,16]{2,1,0:T(8,128)S(1)} %fusion.6), custom_call_target="InvertDiagBlocksLowerTriangular" | custom-call | tf_op jit(solution)/shard_map/triangular_solve/custom-call.0 | solution.py:122
  94.8 0.2 fusion.1
  95.0 1.1 %fusion = bf16[1,16,1,36864]{3,1,2,0:T(8,128)(2,1)S(1)} fusion(f32[16,16]{1,0:T(8,128)S(1)} %fusion.1, bf16[16,36864]{1,0:T(8,128)(2,1)S(1)} %get-tuple-element.15), kind=kOutput, calls=%fused_computation.2 | convolution fusion | flops 113836032 | bytes 2360320 | tf_op jit(solution)/shard_map/dot_general | solution.py:147
  96.1 0.2 pad_maximum_fusion
  96.3 0.0 copy-start
  96.3 2.4 %all-to-all-done.1.received_ref = bf16[32,4,4608]{2,1,0:T(4,128)(2,1)} async-done(((bf16[32,4,4608]{2,1,0:T(4,128)(2,1)}), bf16[32,4,4608]{2,1,0:T(4,128)(2,1)}, u32[]{:S(2)}, u32[]{:S(2)}) %all-to-all-start.1) | async-done | bytes 1179680 | tf_op jit(solution)/shard_map/all_to_all | solution.py:126
  98.7 4.0 %shard_map.53 = (f32[16,64]{1,0:T(8,128)S(1)}, f32[16,32]{1,0:T(8,128)S(1)}) custom-call(bf16[32,4,4608]{2,1,0:T(4,128)(2,1)} %all-to-all-done.1.received_ref, bf16[64,36864]{1,0:T(8,128)(2,1)} %bitcast.51, bf16[32,36864]{1,0:T(8,128)(2,1)S(1)} %bitcast.44), custom_call_target="tpu_custom_call" | custom-call | tf_op jit(solution)/shard_map/pallas_call | solution.py:96
  102.6 0.7 maximum_multiply_fusion
  (6 shorter events, 0.1 us)
Async XLA Ops:
  3.6 7.3 %copy-start.1 = (bf16[4,32,4608]{2,1,0:T(8,128)(2,1)S(1)}, bf16[4,32,4608]{2,1,0:T(8,128)(2,1)}, u32[]{:S(2)}) copy-start(bf16[4,32,4608]{2,1,0:T(8,128)(2,1)} %param.8) | copy-start | bytes 3538948
  3.6 61.8 %all-to-all-start = ((bf16[32,8,4608]{2,1,0:T(8,128)(2,1)}), bf16[32,8,4608]{2,1,0:T(8,128)(2,1)S(1)}, u32[]{:S(2)}, u32[]{:S(2)}) async-start(bf16[32,8,4608]{2,1,0:T(8,128)(2,1)} %shard_map.50), calls=%async_computation | async-start | bytes 4718592 | tf_op jit(solution)/shard_map/all_to_all | solution.py:126
  65.5 33.2 %all-to-all-start.1 = ((bf16[32,4,4608]{2,1,0:T(4,128)(2,1)}), bf16[32,4,4608]{2,1,0:T(4,128)(2,1)}, u32[]{:S(2)}, u32[]{:S(2)}) async-start(bf16[32,4,4608]{2,1,0:T(4,128)(2,1)} %bitcast.42), calls=%async_computation.1 | async-start | bytes 2359296 | tf_op jit(solution)/shard_map/all_to_all | solution.py:126
  96.3 6.3 %copy-start = (bf16[2,16,1,36864]{3,1,2,0:T(8,128)(2,1)}, bf16[2,16,1,36864]{3,1,2,0:T(8,128)(2,1)S(1)}, u32[]{:S(2)}) copy-start(bf16[2,16,1,36864]{3,1,2,0:T(8,128)(2,1)S(1)} %pad_maximum_fusion) | copy-start | bytes 7077892

commit v18 on v17

--- a/solution.py
+++ b/solution.py
@@ -84,7 +84,7 @@
         further_rows, fresh_ref[...], NT, preferred_element_type=jnp.float32)
 
 
-def coarse_call(received, earlier_rows, fresh_rows, lat_count, mode_count, steps=2):
+def coarse_call(received, earlier_rows, fresh_rows, lat_count, mode_count, steps=4):
     _, vector_part, entry_part = received.shape
     count = mode_count * vector_part
     steps = steps if lat_count % steps == 0 else 1

time: 104 us -> 104 us (level)
  no operation moved by 1% of the time
where the time goes in v18:
time: 104 us
  waiting for transfers between devices  54.9 us (53%)
  Pallas kernels  20.5 us (20%)
  starting transfers between devices  11.4 us (11%)
  other arithmetic  8.97 us (9%)
  local copies, waits for them, and re-layouts  4.89 us (5%)
  matrix products  2.55 us (2%)
    all_to_all x2, waiting for transfers between devices, send(): lax.all_to_all(block_major, ('lat', 'mode'), split_axis=0, concat_axis=0,...  54.9 us
    pallas_call x2, Pallas kernels, project_call(): pl.pallas_call(functools.partial(project_kernel, piece_count=len(pieces),...  12.9 us
    all_to_all x2, starting transfers between devices, send(): lax.all_to_all(block_major, ('lat', 'mode'), split_axis=0, concat_axis=0,...  11.4 us
    pallas_call x1, Pallas kernels, coarse_call(): pl.pallas_call(kernel, grid=(steps,), out_shape=(jax.ShapeDtypeStruct((co...  4.64 us
    another operation x6, other arithmetic, factor_inverse(): lower_factor = jnp.linalg.cholesky(gram_matrix)  4.31 us
    another operation x4, other arithmetic, factor_inverse(): lax.linalg.triangular_solve(lower_factor, identity, left_side=True, lower...  3.75 us
    pallas_call x1, Pallas kernels, block_major(): pl.pallas_call(block_major_kernel, grid=(block_count // group,), out_shap...  2.99 us
    unnamed x7, local copies, waits for them, and re-layouts  2.66 us
  transfers between devices with their start and end apart: 2, of which 2 were waited for; matrix products, arithmetic and copies ran while one was open for 15% of the time, Pallas kernels for 12%

profile of v18, /device:TPU:0, one launch (start us, length us, event | category | flops | bytes accessed | tf_op | source)
XLA Modules:
  0.0 104.0 jit_solution(2419133495846366099)
XLA Ops:
  0.6 3.0 %shard_map.50 = bf16[32,8,4608]{2,1,0:T(8,128)(2,1)} custom-call(bf16[2,4,32,4608]{3,2,1,0:T(8,128)(2,1)} %panels_ref.1), custom_call_target="tpu_custom_call" | custom-call | tf_op jit(solution)/shard_map/pallas_call | solution.py:59
  3.6 7.3 %all-to-all-start = ((bf16[32,8,4608]{2,1,0:T(8,128)(2,1)}), bf16[32,8,4608]{2,1,0:T(8,128)(2,1)S(1)}, u32[]{:S(2)}, u32[]{:S(2)}) async-start(bf16[32,8,4608]{2,1,0:T(8,128)(2,1)} %shard_map.50), calls=%async_computation | async-start | bytes 4718592 | tf_op jit(solution)/shard_map/all_to_all | solution.py:126
  10.9 0.0 copy-done.1
  10.9 2.0 %copy.14 = bf16[4,32,4608]{2,0,1:T(4,128)(2,1)} copy(bf16[4,32,4608]{2,1,0:T(8,128)(2,1)S(1)} %copy-done.1) | data formatting | bytes 2359296 | tf_op args[2]
  12.9 52.6 %all-to-all-done = bf16[32,8,4608]{2,1,0:T(8,128)(2,1)S(1)} async-done(((bf16[32,8,4608]{2,1,0:T(8,128)(2,1)}), bf16[32,8,4608]{2,1,0:T(8,128)(2,1)S(1)}, u32[]{:S(2)}, u32[]{:S(2)}) %all-to-all-start) | async-done | bytes 2359328 | tf_op jit(solution)/shard_map/all_to_all | solution.py:126
  65.5 4.1 %all-to-all-start.1 = ((bf16[32,4,4608]{2,1,0:T(4,128)(2,1)}), bf16[32,4,4608]{2,1,0:T(4,128)(2,1)}, u32[]{:S(2)}, u32[]{:S(2)}) async-start(bf16[32,4,4608]{2,1,0:T(4,128)(2,1)} %bitcast.42), calls=%async_computation.1 | async-start | bytes 2359296 | tf_op jit(solution)/shard_map/all_to_all | solution.py:126
  69.6 0.8 fusion.11
  70.4 0.7 copy.5
  71.0 0.3 copy.11
  71.4 6.8 %shard_map.51 = (bf16[16,36864]{1,0:T(8,128)(2,1)S(1)}, f32[16,16]{1,0:T(8,128)S(1)}) custom-call(bf16[64,36864]{1,0:T(8,128)(2,1)} %bitcast.49, bf16[16,36864]{1,0:T(8,128)(2,1)S(1)} %bitcast.46), custom_call_target="tpu_custom_call" | custom-call | flops 169869312 | bytes 7078912 | tf_op jit(solution)/shard_map/pallas_call | solution.py:33
  78.2 0.1 copy.6
  78.3 1.5 %cholesky.44 = f32[16,16]{1,0:T(8,128)S(1)} custom-call(f32[16,16]{1,0:T(8,128)S(1)} %fusion.10), custom_call_target="Cholesky" | custom-call | tf_op jit(solution)/shard_map/jit(cholesky)/cholesky | solution.py:118
  79.8 0.6 compare_reduce_fusion.1
  80.4 0.6 fusion.5
  81.1 1.2 %custom-call.6 = f32[1,16,16]{1,2,0:T(8,128)S(1)} custom-call(f32[1,16,16]{2,1,0:T(8,128)S(1)} %fusion.5), custom_call_target="InvertDiagBlocksLowerTriangular" | custom-call | tf_op jit(solution)/shard_map/triangular_solve/custom-call.0 | solution.py:122
  82.3 0.2 fusion.3
  82.5 0.7 copy.7
  83.2 0.3 copy.12
  83.5 1.1 %convolution_convert_fusion.1.refs_1_ = bf16[16,36864]{1,0:T(8,128)(2,1)S(1)} fusion(f32[16,16]{1,0:T(8,128)S(1)} %fusion.3, bf16[16,36864]{1,0:T(8,128)(2,1)S(1)} %get-tuple-element.13), kind=kOutput, calls=%fused_computation.1 | convolution fusion | flops 113836032 | bytes 2360320 | tf_op jit(solution)/shard_map/dot_general | solution.py:147
  84.6 6.1 %shard_map.52 = (bf16[16,36864]{1,0:T(8,128)(2,1)S(1)}, f32[16,16]{1,0:T(8,128)S(1)}) custom-call(bf16[64,36864]{1,0:T(8,128)(2,1)} %bitcast.50, bf16[16,36864]{1,0:T(8,128)(2,1)S(1)} %convolution_convert_fusion.1.refs_1_, bf16[16,36864]{1,0:T(8,128)(2,1)S(1)} %bitcast.45), custom_call_target="tpu_custom_call" | custom-call | flops 207618048 | bytes 8258560 | tf_op jit(solution)/shard_map/pallas_call | solution.py:33
  90.7 0.1 copy.8
  90.8 1.5 %cholesky.55 = f32[16,16]{1,0:T(8,128)S(1)} custom-call(f32[16,16]{1,0:T(8,128)S(1)} %fusion.8), custom_call_target="Cholesky" | custom-call | tf_op jit(solution)/shard_map/jit(cholesky)/cholesky | solution.py:118
  92.2 0.6 compare_reduce_fusion
  92.9 0.6 fusion.6
  93.6 1.2 %custom-call.7 = f32[1,16,16]{1,2,0:T(8,128)S(1)} custom-call(f32[1,16,16]{2,1,0:T(8,128)S(1)} %fusion.6), custom_call_target="InvertDiagBlocksLowerTriangular" | custom-call | tf_op jit(solution)/shard_map/triangular_solve/custom-call.0 | solution.py:122
  94.8 0.2 fusion.1
  95.0 1.1 %fusion = bf16[1,16,1,36864]{3,1,2,0:T(8,128)(2,1)S(1)} fusion(f32[16,16]{1,0:T(8,128)S(1)} %fusion.1, bf16[16,36864]{1,0:T(8,128)(2,1)S(1)} %get-tuple-element.15), kind=kOutput, calls=%fused_computation.2 | convolution fusion | flops 113836032 | bytes 2360320 | tf_op jit(solution)/shard_map/dot_general | solution.py:147
  96.1 0.2 pad_maximum_fusion
  96.3 0.0 copy-start
  96.3 2.4 %all-to-all-done.1.received_ref = bf16[32,4,4608]{2,1,0:T(4,128)(2,1)} async-done(((bf16[32,4,4608]{2,1,0:T(4,128)(2,1)}), bf16[32,4,4608]{2,1,0:T(4,128)(2,1)}, u32[]{:S(2)}, u32[]{:S(2)}) %all-to-all-start.1) | async-done | bytes 1179680 | tf_op jit(solution)/shard_map/all_to_all | solution.py:126
  98.7 4.6 %shard_map.53 = (f32[16,64]{1,0:T(8,128)S(1)}, f32[16,32]{1,0:T(8,128)S(1)}) custom-call(bf16[32,4,4608]{2,1,0:T(4,128)(2,1)} %all-to-all-done.1.received_ref, bf16[64,36864]{1,0:T(8,128)(2,1)} %bitcast.51, bf16[32,36864]{1,0:T(8,128)(2,1)S(1)} %bitcast.44), custom_call_target="tpu_custom_call" | custom-call | tf_op jit(solution)/shard_map/pallas_call | solution.py:96
  103.3 0.7 maximum_multiply_fusion
  (6 shorter events, 0.1 us)
Async XLA Ops:
  3.6 7.3 %copy-start.1 = (bf16[4,32,4608]{2,1,0:T(8,128)(2,1)S(1)}, bf16[4,32,4608]{2,1,0:T(8,128)(2,1)}, u32[]{:S(2)}) copy-start(bf16[4,32,4608]{2,1,0:T(8,128)(2,1)} %param.8) | copy-start | bytes 3538948
  3.6 61.8 %all-to-all-start = ((bf16[32,8,4608]{2,1,0:T(8,128)(2,1)}), bf16[32,8,4608]{2,1,0:T(8,128)(2,1)S(1)}, u32[]{:S(2)}, u32[]{:S(2)}) async-start(bf16[32,8,4608]{2,1,0:T(8,128)(2,1)} %shard_map.50), calls=%async_computation | async-start | bytes 4718592 | tf_op jit(solution)/shard_map/all_to_all | solution.py:126
  65.5 33.2 %all-to-all-start.1 = ((bf16[32,4,4608]{2,1,0:T(4,128)(2,1)}), bf16[32,4,4608]{2,1,0:T(4,128)(2,1)}, u32[]{:S(2)}, u32[]{:S(2)}) async-start(bf16[32,4,4608]{2,1,0:T(4,128)(2,1)} %bitcast.42), calls=%async_computation.1 | async-start | bytes 2359296 | tf_op jit(solution)/shard_map/all_to_all | solution.py:126
  96.3 7.0 %copy-start = (bf16[2,16,1,36864]{3,1,2,0:T(8,128)(2,1)}, bf16[2,16,1,36864]{3,1,2,0:T(8,128)(2,1)S(1)}, u32[]{:S(2)}) copy-start(bf16[2,16,1,36864]{3,1,2,0:T(8,128)(2,1)S(1)} %pad_maximum_fusion) | copy-start | bytes 7077892
